TPU v7x, 768 devices: a whole 4x8x12 slice. The times are simulated.
768 devices in a mesh: node: 12 (over z), section: 64 (over y, x, core).
Axes of the slice: x: 4, y: 8, z: 12, core: 2. Of those that a mesh axis runs over, the one named last changes fastest.
Arguments:
- tokens: bfloat16 [64, 3072, 512], P('section', 'node'), may hold values from -6 to 6
- cotangent: bfloat16 [64, 3072, 512], P('section', 'node'), may hold values from -6 to 6
- w_qkv: bfloat16 [512, 1536], replicated
- w_out: bfloat16 [512, 512], replicated, may hold values from -2.09375 to 2.09375
- norm_gain: float32 [512], replicated, may hold values from 0.1 to 1.9
- tile_lists: int32 [24, 5], replicated, may hold values from 0 to 23, as said below
- tile_counts: int32 [24], replicated, may hold values from 3 to 5, as said below
Outputs:
- mixed_tokens: bfloat16 [64, 3072, 512], P('section', 'node')
- grad_tokens: bfloat16 [64, 3072, 512], P('section', 'node')
- grad_w_qkv: float32 [512, 1536], P('section', 'node')
- grad_w_out: float32 [512, 512], P('section')
- grad_gain: float32 [512], P('section')
Inputs may be any that keep to these rules, and one draw needn't show every extreme that they name: `tile_lists`: tiles are numbered in order, 2 to a block, the first and last blocks counting as adjacent; entry 0 of row t is t itself, entry 1 lies in the block just before t's block, entry 2 in the block just after it, the other entries in one of these three blocks; the entries of a row are distinct. `tile_counts`: some tile has 5.
All inputs are finite; a program needn't handle non-finite values.
Results may differ from a plain program's by a relative error of at most 0.017.
Values may be sent and summed in bfloat16 or wider, within the bound.
No kernel may reach another device: no remote copies, remote signals or barrier semaphores. Data moves between devices by JAX's collectives and lax.ppermute only.
A program may use at most 64 MiB of HBM per device.

v0:
```python
import jax
import jax.numpy as jnp
from jax import lax
from jax.sharding import PartitionSpec as P

HEADS = 4
TILE = 128


EPS = 1e-06
MASKED = -1000000000.0


def extended(block, sides, width):
    for axis, dim in sides:
        count = lax.axis_size(axis)
        forward = [(i, i + 1) for i in range(count - 1)]
        forward.append((count - 1, 0))
        backward = [(target, source) for source, target in forward]
        low = lax.ppermute(
            lax.slice_in_dim(block, block.shape[dim] - width, None, axis=dim), axis, forward
        )
        high = lax.ppermute(lax.slice_in_dim(block, 0, width, axis=dim), axis, backward)
        block = jnp.concatenate([low, block, high], axis=dim)
    return block


def passed_along(block, axis, distance):
    devices = range(lax.axis_size(axis))
    route = [((i - distance) % len(devices), i) for i in devices]
    return lax.ppermute(block, axis, route)


def tile_mask(own_lists, own_counts, first_tile, tile_total):
    tile_count = own_lists.shape[0]
    span_tiles = 3 * tile_count
    places = jnp.mod(own_lists - first_tile, tile_total)
    live_entries = jnp.arange(own_lists.shape[1], dtype=jnp.int32)[None, :] < own_counts[:, None]
    window_slots = jnp.arange(span_tiles, dtype=jnp.int32)
    matches = jnp.logical_and(
        places[:, :, None] == window_slots[None, None, :], live_entries[:, :, None]
    )
    return jnp.any(matches, axis=1)


def attend(queries, window_keys, window_values, allowed):
    row_count, model_width = queries.shape
    tile_count, span_tiles = allowed.shape
    head_dim = model_width // HEADS
    score_scale = head_dim ** (-0.5)
    query_heads = queries.reshape(tile_count, TILE, HEADS, head_dim)
    key_heads = window_keys.reshape(span_tiles, TILE, HEADS, head_dim)
    value_heads = window_values.reshape(span_tiles, TILE, HEADS, head_dim)
    scores = (
        jnp.einsum("atnd,bsnd->natbs", query_heads, key_heads, preferred_element_type=jnp.float32)
        * score_scale
    )
    scores = jnp.where(allowed[None, :, None, :, None], scores, MASKED)
    row_peak = jnp.max(scores, axis=(3, 4), keepdims=True)
    expanded = jnp.exp(scores - row_peak)
    probabilities = expanded / jnp.sum(expanded, axis=(3, 4), keepdims=True)
    rounded = probabilities.astype(jnp.bfloat16)
    attended = jnp.einsum(
        "natbs,bsnd->atnd", rounded, value_heads, preferred_element_type=jnp.float32
    )
    return (attended.reshape(row_count, model_width).astype(jnp.bfloat16), probabilities, rounded)


def attend_back(grad_attended, queries, window_keys, window_values, probabilities, rounded):
    row_count, model_width = queries.shape
    tile_count = probabilities.shape[1]
    span_tiles = probabilities.shape[3]
    head_dim = model_width // HEADS
    score_scale = head_dim ** (-0.5)
    query_heads = queries.reshape(tile_count, TILE, HEADS, head_dim)
    key_heads = window_keys.reshape(span_tiles, TILE, HEADS, head_dim)
    value_heads = window_values.reshape(span_tiles, TILE, HEADS, head_dim)
    grad_heads = grad_attended.reshape(tile_count, TILE, HEADS, head_dim)
    grad_probs = jnp.einsum(
        "atnd,bsnd->natbs", grad_heads, value_heads, preferred_element_type=jnp.float32
    )
    centre = jnp.sum(grad_probs * probabilities, axis=(3, 4), keepdims=True)
    grad_scores = (probabilities * (grad_probs - centre) * score_scale).astype(jnp.bfloat16)
    grad_queries = jnp.einsum(
        "natbs,bsnd->atnd", grad_scores, key_heads, preferred_element_type=jnp.float32
    ).reshape(row_count, model_width)
    grad_keys = jnp.einsum(
        "natbs,atnd->bsnd", grad_scores, query_heads, preferred_element_type=jnp.float32
    ).reshape(span_tiles * TILE, model_width)
    grad_values = jnp.einsum(
        "natbs,atnd->bsnd", rounded, grad_heads, preferred_element_type=jnp.float32
    ).reshape(span_tiles * TILE, model_width)
    return (grad_queries, jnp.concatenate([grad_keys, grad_values], axis=1))


def on_device(tokens, cotangent, w_qkv, w_out, norm_gain, tile_lists, tile_counts):
    own_tokens = tokens[0]
    own_grads = cotangent[0]
    row_count, model_width = own_tokens.shape
    tile_count = row_count // TILE
    tile_total = tile_lists.shape[0]
    device = lax.axis_index("node")
    own_lists = lax.dynamic_slice_in_dim(tile_lists, device * tile_count, tile_count, 0)
    own_counts = lax.dynamic_slice_in_dim(tile_counts, device * tile_count, tile_count, 0)
    allowed = tile_mask(own_lists, own_counts, (device - 1) * tile_count, tile_total)
    widened = own_tokens.astype(jnp.float32)
    inverse_rms = lax.rsqrt(jnp.mean(widened * widened, axis=-1, keepdims=True) + EPS)
    unit_rows = widened * inverse_rms
    normed = (unit_rows * norm_gain).astype(jnp.bfloat16)
    projected = jnp.dot(normed, w_qkv, preferred_element_type=jnp.float32).astype(jnp.bfloat16)
    queries = projected[:, :model_width]
    window = extended(projected[:, model_width:], (("node", 0),), row_count)
    window_keys = window[:, :model_width]
    window_values = window[:, model_width:]
    attended, probabilities, rounded = attend(queries, window_keys, window_values, allowed)
    outputs = (widened + jnp.dot(attended, w_out, preferred_element_type=jnp.float32)).astype(
        jnp.bfloat16
    )
    contract_rows = (((0,), (0,)), ((), ()))
    contract_cols = (((1,), (1,)), ((), ()))
    term_out = lax.dot_general(
        attended, own_grads, contract_rows, preferred_element_type=jnp.float32
    )
    grad_attended = lax.dot_general(
        own_grads, w_out, contract_cols, preferred_element_type=jnp.float32
    ).astype(jnp.bfloat16)
    grad_queries, grad_window = attend_back(
        grad_attended, queries, window_keys, window_values, probabilities, rounded
    )
    grad_keyvals = grad_window[row_count : 2 * row_count]
    for offset, side_index in ((-1, 0), (1, 2)):
        side_part = grad_window[side_index * row_count : (side_index + 1) * row_count]
        grad_keyvals = grad_keyvals + passed_along(
            side_part.astype(jnp.bfloat16), "node", offset
        ).astype(side_part.dtype)
    grad_projected = jnp.concatenate([grad_queries, grad_keyvals], axis=1).astype(jnp.bfloat16)
    term_qkv = lax.dot_general(
        normed, grad_projected, contract_rows, preferred_element_type=jnp.float32
    )
    grad_normed = lax.dot_general(
        grad_projected, w_qkv, contract_cols, preferred_element_type=jnp.float32
    )
    term_gain = jnp.sum(grad_normed * unit_rows, axis=0)
    grad_unit = grad_normed * norm_gain
    inner_mean = jnp.mean(grad_unit * unit_rows, axis=-1, keepdims=True)
    grad_tokens = (
        own_grads.astype(jnp.float32) + inverse_rms * (grad_unit - unit_rows * inner_mean)
    ).astype(jnp.bfloat16)
    part_qkv, part_out, part_gain = (
        lax.psum_scatter(term_qkv, "section", scatter_dimension=0, tiled=True),
        lax.psum_scatter(term_out, "section", scatter_dimension=0, tiled=True),
        lax.psum_scatter(term_gain, "section", scatter_dimension=0, tiled=True),
    )
    part_qkv = lax.psum_scatter(
        part_qkv.astype(jnp.bfloat16), "node", scatter_dimension=1, tiled=True
    ).astype(jnp.float32)
    part_out, part_gain = lax.psum((part_out, part_gain), "node")
    return (outputs[None], grad_tokens[None], part_qkv, part_out, part_gain)


def solution(mesh):
    return jax.shard_map(
        on_device,
        mesh=mesh,
        in_specs=(P("section", "node", None), P("section", "node", None), P(), P(), P(), P(), P()),
        out_specs=(
            P("section", "node", None),
            P("section", "node", None),
            P("section", "node"),
            P("section", None),
            P("section"),
        ),
        check_vma=False,
    )
```

profile of v0, /device:TPU:6, one launch (start us, length us, event | category | flops | bytes accessed | tf_op | source)
XLA Modules:
  0.0 440.3 jit_solution(5743212327306458893)
XLA Ops:
  9.5 1.6 convolution_convert_fusion
  11.1 14.6 %collective-permute-start.1 = (bf16[256,1024]{1,0:T(8,128)(2,1)S(1)}, bf16[256,1024]{1,0:T(8,128)(2,1)}, u32[]{:S(2)}, u32[]{:S(2)}) collective-permute-start(bf16[256,1024]{1,0:T(8,128)(2,1)S(1)} %slice.30), channel_id=1, source_target_pairs={{64,0},{128,64},{192,128},{256,192},{320,256},{384,320},{448,384},... | collective-permute-start | bytes 1572872 | tf_op jit(solution)/shard_map/ppermute | solution.py:23
  25.7 1.9 collective-permute-start
  35.0 1.9 collective-permute-done.1
  36.9 5.4 %collective-permute-done = bf16[256,1024]{1,0:T(8,128)(2,1)} collective-permute-done((bf16[256,1024]{1,0:T(8,128)(2,1)S(1)}, bf16[256,1024]{1,0:T(8,128)(2,1)}, u32[]{:S(2)}, u32[]{:S(2)}) %collective-permute-start) | collective-permute-done | bytes 524320 | tf_op jit(solution)/shard_map/ppermute | solution.py:20
  42.3 1.3 pad_maximum_fusion
  45.5 2.0 reshape.79
  52.6 1.8 fusion.10
  54.4 1.8 fusion.7
  56.2 2.6 copy.72
  58.8 2.7 bitcast_dynamic-update-slice_fusion.1
  61.6 2.6 copy.75
  64.2 2.7 bitcast_dynamic-update-slice_fusion
  66.9 2.2 convert.14
  70.2 1.9 collective-permute-start.3
  72.1 5.3 %collective-permute-start.2 = (bf16[256,1024]{1,0:T(8,128)(2,1)}, bf16[256,1024]{1,0:T(8,128)(2,1)}, u32[]{:S(2)}, u32[]{:S(2)}) collective-permute-start(bf16[256,1024]{1,0:T(8,128)(2,1)} %get-tuple-element.13), channel_id=1, source_target_pairs={{64,0},{128,64},{192,128},{256,192},{320,256},{384,320},{448,384},... | collective-permute-start | bytes 1572872 | tf_op jit(solution)/shard_map/ppermute | solution.py:31
  80.8 2.3 fusion.39
  83.4 2.0 fusion.18
  86.1 1.3 collective-permute-done.2
  87.4 1.8 fusion.20
  89.9 2.4 fusion.36
  92.3 270.5 %all-reduce.9 = (bf16[512,1536]{1,0:T(8,128)(2,1)}, f32[512]{0:T(512)S(1)}) all-reduce(f32[512,1536]{1,0:T(8,128)} %fusion.36, f32[512]{0:T(512)S(1)} %get-tuple-element.5), channel_id=2, replica_groups=mesh['node'=12,'section'=64] {'section'}, use_global_device_ids=true, to_apply=%region_6.7.clone | all-reduce | flops 786944 | bytes 4722688
  366.2 43.2 %all-reduce.4 = (f32[8,512]{1,0:T(8,128)}, f32[8]{0:T(128)}) all-reduce(f32[8,512]{1,0:T(8,128)S(1)} %constant_dynamic-slice_fusion, f32[8]{0:T(128)S(1)} %dynamic-slice.5), channel_id=1, replica_groups=mesh['node'=12,'section'=64] {'node'}, use_global_device_ids=true, to_apply=%region_9.10 | all-reduce | flops 4104 | bytes 32832 | tf_op jit(solution)/shard_map/psum | solution.py:157
  409.4 22.1 %reduce-scatter.4.cloned.1.call-done = bf16[128,8]{1,0:T(8,128)(2,1)} async-done(((bf16[1536,8]{1,0:T(8,128)(2,1)}), bf16[128,8]{1,0:T(8,128)(2,1)}) %reduce-scatter.4.cloned.1.call-update) | async-done | bytes 2064
  (73 shorter events, 25.8 us)
Async XLA Ops:
  8.0 1.5 copy-start
  8.0 19.7 %copy-start.13 = (s32[24,5]{0,1:T(8,128)S(1)}, s32[24,5]{0,1:T(8,128)}, u32[]{:S(2)}) copy-start(s32[24,5]{0,1:T(8,128)} %param.12) | copy-start | bytes 1444
  8.0 19.9 %copy-start.14 = (s32[24]{0:T(128)S(1)}, s32[24]{0:T(128)}, u32[]{:S(2)}) copy-start(s32[24]{0:T(128)} %param.13) | copy-start | bytes 292
  8.0 21.9 %copy-start.10 = (bf16[512,512]{1,0:T(8,128)(2,1)S(1)}, bf16[512,512]{1,0:T(8,128)(2,1)}, u32[]{:S(2)}) copy-start(bf16[512,512]{1,0:T(8,128)(2,1)} %param.10) | copy-start | bytes 1572868
  8.0 21.9 %copy-start.6 = (bf16[1,256,512]{2,1,0:T(8,128)(2,1)S(1)}, bf16[1,256,512]{2,1,0:T(8,128)(2,1)}, u32[]{:S(2)}) copy-start(bf16[1,256,512]{2,1,0:T(8,128)(2,1)} %param.8) | copy-start | bytes 786436
  8.1 357.3 %all-reduce.8.cloned.1.call-start = ((), (), s32[]{:S(2)}) async-start(), calls=%async_computation.2 | async-start | bytes 2097152
  11.1 25.8 %collective-permute-start.1 = (bf16[256,1024]{1,0:T(8,128)(2,1)S(1)}, bf16[256,1024]{1,0:T(8,128)(2,1)}, u32[]{:S(2)}, u32[]{:S(2)}) collective-permute-start(bf16[256,1024]{1,0:T(8,128)(2,1)S(1)} %slice.30), channel_id=1, source_target_pairs={{64,0},{128,64},{192,128},{256,192},{320,256},{384,320},{448,384},... | collective-permute-start | bytes 1572872 | tf_op jit(solution)/shard_map/ppermute | solution.py:23
  25.7 16.6 %collective-permute-start = (bf16[256,1024]{1,0:T(8,128)(2,1)S(1)}, bf16[256,1024]{1,0:T(8,128)(2,1)}, u32[]{:S(2)}, u32[]{:S(2)}) collective-permute-start(bf16[256,1024]{1,0:T(8,128)(2,1)S(1)} %slice.30), channel_id=1, source_target_pairs={{0,64},{64,128},{128,192},{192,256},{256,320},{320,384},{384,448},... | collective-permute-start | bytes 1572872 | tf_op jit(solution)/shard_map/ppermute | solution.py:20
  29.9 17.6 %copy-start.8 = (bf16[2,128,4,128,1]{1,3,0,4,2:T(8,128)(2,1)}, bf16[2,128,4,128,1]{1,3,0,4,2:T(8,128)(2,1)S(1)}, u32[]{:S(2)}) copy-start(bf16[2,128,4,128,1]{1,3,0,4,2:T(8,128)(2,1)S(1)} %copy.86) | copy-start | bytes 786436
  45.5 3.6 copy-start.1
  47.5 1.5 copy-start.4
  47.6 1.5 copy-start.11
  50.1 1.3 copy-start.5
  51.4 3.0 copy-start.9
  66.9 10.5 %copy-start.2 = (bf16[6,128,4,128,1]{1,3,0,4,2:T(8,128)(2,1)S(1)}, bf16[6,128,4,128,1]{1,3,0,4,2:T(8,128)(2,1)}, u32[]{:S(2)}) copy-start(bf16[6,128,4,128,1]{1,3,0,4,2:T(8,128)(2,1)} %copy-done.1) | copy-start | bytes 2359300
  70.2 15.9 %collective-permute-start.3 = (bf16[256,1024]{1,0:T(8,128)(2,1)}, bf16[256,1024]{1,0:T(8,128)(2,1)}, u32[]{:S(2)}, u32[]{:S(2)}) collective-permute-start(bf16[256,1024]{1,0:T(8,128)(2,1)} %get-tuple-element.14), channel_id=1, source_target_pairs={{704,0},{0,64},{64,128},{128,192},{192,256},{256,320},{320,384},{3... | collective-permute-start | bytes 1572872 | tf_op jit(solution)/shard_map/ppermute | solution.py:31
  72.1 11.3 %copy-start.3 = (bf16[1,256,512]{2,1,0:T(8,128)(2,1)S(1)}, bf16[1,256,512]{2,1,0:T(8,128)(2,1)}, u32[]{:S(2)}) copy-start(bf16[1,256,512]{2,1,0:T(8,128)(2,1)} %param.7) | copy-start | bytes 786436
  72.1 15.3 %collective-permute-start.2 = (bf16[256,1024]{1,0:T(8,128)(2,1)}, bf16[256,1024]{1,0:T(8,128)(2,1)}, u32[]{:S(2)}, u32[]{:S(2)}) collective-permute-start(bf16[256,1024]{1,0:T(8,128)(2,1)} %get-tuple-element.13), channel_id=1, source_target_pairs={{64,0},{128,64},{192,128},{256,192},{320,256},{384,320},{448,384},... | collective-permute-start | bytes 1572872 | tf_op jit(solution)/shard_map/ppermute | solution.py:31
  80.8 8.3 %copy-start.12 = (f32[512]{0:T(512)S(1)}, f32[512]{0:T(512)}, u32[]{:S(2)}) copy-start(f32[512]{0:T(512)} %param.11) | copy-start | bytes 6148
  83.1 348.3 %reduce-scatter.4.cloned.1.call-start = ((), (), s32[]{:S(2)}) async-start(), calls=%async_computation.1 | async-start | bytes 425984
  89.9 274.5 %copy-start.7 = (bf16[1,256,512]{2,1,0:T(8,128)(2,1)S(1)}, bf16[1,256,512]{2,1,0:T(8,128)(2,1)}, u32[]{:S(2)}) copy-start(bf16[1,256,512]{2,1,0:T(8,128)(2,1)} %param.8) | copy-start | bytes 786436
Sparse Core Ops, SparseCore 0:
  83.3 203.0 all-reduce.7
Sparse Core Ops, SparseCore 1:
  365.4 66.0 reduce-scatter.3
where the time goes:
time: 441 us; the launch traced here: 440 us
  blocking collectives  314 us (71%)
  waiting for transfers between devices  31.5 us (7%)
  local copies, waits for them, and re-layouts  26.7 us (6%)
  starting transfers between devices  23.9 us (5%)
  matrix products  17.7 us (4%)
  between operations  16.5 us (4%)
  other arithmetic  10.3 us (2%)
    unnamed x1, blocking collectives  270 us
    psum x1, blocking collectives, on_device(): part_out, part_gain = lax.psum((part_out, part_gain), 'node')  43.2 us
    unnamed x4, waiting for transfers between devices  22.1 us
    ppermute x1, starting transfers between devices, extended(): lax.ppermute(lax.slice_in_dim(block, 0, width, axis=dim), axis, backward)  14.6 us
  transfers between devices with their start and end apart: 6, of which 5 were waited for; matrix products, arithmetic and copies ran while one was open for 5% of the time, Pallas kernels for 0%

commit v1 on v0

--- a/solution.py
+++ b/solution.py
@@ -1,7 +1,7 @@
 import jax
 import jax.numpy as jnp
 from jax import lax
-from jax.sharding import PartitionSpec as P
+from jax.sharding import Mesh, PartitionSpec as P
 
 HEADS = 4
 TILE = 128
@@ -146,29 +146,43 @@
     grad_tokens = (
         own_grads.astype(jnp.float32) + inverse_rms * (grad_unit - unit_rows * inner_mean)
     ).astype(jnp.bfloat16)
-    part_qkv, part_out, part_gain = (
-        lax.psum_scatter(term_qkv, "section", scatter_dimension=0, tiled=True),
-        lax.psum_scatter(term_out, "section", scatter_dimension=0, tiled=True),
-        lax.psum_scatter(term_gain, "section", scatter_dimension=0, tiled=True),
-    )
-    part_qkv = lax.psum_scatter(
-        part_qkv.astype(jnp.bfloat16), "node", scatter_dimension=1, tiled=True
-    ).astype(jnp.float32)
+    return (outputs[None], grad_tokens[None]) + reduce_terms(term_qkv, term_out, term_gain)
+
+
+def section_order(rows):
+    y_size, x_size, core_size = lax.axis_size("y"), lax.axis_size("x"), lax.axis_size("core")
+    shape = rows.shape
+    split = rows.reshape((y_size, x_size, core_size, -1) + shape[1:])
+    return jnp.moveaxis(split, (2, 1, 0), (0, 1, 2)).reshape(shape)
+
+
+def reduce_terms(term_qkv, term_out, term_gain):
+    parts = (section_order(term_qkv), section_order(term_out), section_order(term_gain))
+    for axis in ("core", "x", "y"):
+        parts = tuple(lax.psum_scatter(p, axis, scatter_dimension=0, tiled=True) for p in parts)
+    part_qkv, part_out, part_gain = parts
+    part_qkv = lax.psum_scatter(part_qkv, "node", scatter_dimension=1, tiled=True)
     part_out, part_gain = lax.psum((part_out, part_gain), "node")
-    return (outputs[None], grad_tokens[None], part_qkv, part_out, part_gain)
+    return (part_qkv, part_out, part_gain)
 
 
 def solution(mesh):
+    node_size, section_size = mesh.devices.shape
+    core_size = 2
+    x_size = 4
+    y_size = section_size // (core_size * x_size)
+    fine = Mesh(mesh.devices.reshape(node_size, y_size, x_size, core_size), ("node", "y", "x", "core"))
+    section = ("y", "x", "core")
     return jax.shard_map(
         on_device,
-        mesh=mesh,
-        in_specs=(P("section", "node", None), P("section", "node", None), P(), P(), P(), P(), P()),
+        mesh=fine,
+        in_specs=(P(section, "node", None), P(section, "node", None), P(), P(), P(), P(), P()),
         out_specs=(
-            P("section", "node", None),
-            P("section", "node", None),
-            P("section", "node"),
-            P("section", None),
-            P("section"),
+            P(section, "node", None),
+            P(section, "node", None),
+            P(section, "node"),
+            P(section, None),
+            P(section),
         ),
         check_vma=False,
     )

time: 441 us -> 368 us (0.83)
  blocking collectives: 314 us -> 70.8 us
  waiting for transfers between devices: 31.5 us -> 198 us
  local copies, waits for them, and re-layouts: 26.7 us -> 32.1 us
    unnamed x1 -> x3, blocking collectives: 270 us -> 25.8 us
    reduce_scatter x0 -> x7, waiting for transfers between devices: none -> 178 us  [the longest x6 163 us: reduce_terms(): lax.psum_scatter(p, axis, scatter_dimension=0, tiled=True)]
    unnamed x4 -> x7, waiting for transfers between devices: 22.1 us -> 0.11 us
    ppermute x2, waiting for transfers between devices: 1.98 us -> 7.7 us  [passed_along(): return lax.ppermute(block, axis, route)]
    ppermute x1, waiting for transfers between devices: 1.94 us -> 6.5 us  [extended(): lax.ppermute(lax.slice_in_dim(block, 0, width, axis=dim), axis, backward)]
    unnamed x37 -> x51, local copies, waits for them, and re-layouts: 6.77 us -> 9.95 us
  transfers between devices with their start and end apart: 6 -> 11, of which waited for: 5 -> 11; matrix products, arithmetic and copies ran while one was open for 5% -> 5% of each run, Pallas kernels for 0% -> 0%
where the time goes in v1:
time: 368 us; the launch traced here: 367 us
  waiting for transfers between devices  198 us (54%)
  blocking collectives  70.8 us (19%)
  local copies, waits for them, and re-layouts  32.1 us (9%)
  starting transfers between devices  24 us (7%)
  between operations  16.5 us (4%)
  matrix products  14.6 us (4%)
  other arithmetic  10.7 us (3%)
    reduce_scatter x6, waiting for transfers between devices, reduce_terms(): lax.psum_scatter(p, axis, scatter_dimension=0, tiled=True)  163 us
    psum x1, blocking collectives, reduce_terms(): part_out, part_gain = lax.psum((part_out, part_gain), 'node')  45 us
    unnamed x3, blocking collectives  25.8 us
    reduce_scatter x1, waiting for transfers between devices, reduce_terms(): lax.psum_scatter(part_qkv, 'node', scatter_dimension=1, tiled=True)  15 us
    ppermute x1, starting transfers between devices, extended(): lax.ppermute(lax.slice_in_dim(block, 0, width, axis=dim), axis, backward)  14.6 us
    unnamed x51, local copies, waits for them, and re-layouts  9.95 us
    ppermute x2, waiting for transfers between devices, passed_along(): return lax.ppermute(block, axis, route)  7.7 us
  transfers between devices with their start and end apart: 11, of which 11 were waited for; matrix products, arithmetic and copies ran while one was open for 5% of the time, Pallas kernels for 0%

profile of v1, /device:TPU:6, one launch (start us, length us, event | category | flops | bytes accessed | tf_op | source)
XLA Modules:
  0.0 366.9 jit_solution(1475094329940170831)
XLA Ops:
  10.3 14.6 %collective-permute-start.1 = (bf16[256,1024]{1,0:T(8,128)(2,1)S(1)}, bf16[256,1024]{1,0:T(8,128)(2,1)}, u32[]{:S(2)}, u32[]{:S(2)}) collective-permute-start(bf16[256,1024]{1,0:T(8,128)(2,1)S(1)} %slice.30), channel_id=1, source_target_pairs={{64,0},{128,64},{192,128},{256,192},{320,256},{384,320},{448,384},... | collective-permute-start | bytes 1572872 | tf_op jit(solution)/shard_map/ppermute | solution.py:23
  24.9 1.9 collective-permute-start
  29.6 6.5 %collective-permute-done.1 = bf16[256,1024]{1,0:T(8,128)(2,1)} collective-permute-done((bf16[256,1024]{1,0:T(8,128)(2,1)S(1)}, bf16[256,1024]{1,0:T(8,128)(2,1)}, u32[]{:S(2)}, u32[]{:S(2)}) %collective-permute-start.1) | collective-permute-done | bytes 524320 | tf_op jit(solution)/shard_map/ppermute | solution.py:23
  36.1 5.4 %collective-permute-done = bf16[256,1024]{1,0:T(8,128)(2,1)} collective-permute-done((bf16[256,1024]{1,0:T(8,128)(2,1)S(1)}, bf16[256,1024]{1,0:T(8,128)(2,1)}, u32[]{:S(2)}, u32[]{:S(2)}) %collective-permute-start) | collective-permute-done | bytes 524320 | tf_op jit(solution)/shard_map/ppermute | solution.py:20
  44.7 2.0 reshape.94
  53.5 2.7 copy.104
  56.2 2.7 bitcast_dynamic-update-slice_fusion.1
  60.7 2.6 copy.107
  63.3 2.7 bitcast_dynamic-update-slice_fusion
  66.0 2.3 convert.14
  71.3 5.1 %collective-permute-start.2 = (bf16[256,1024]{1,0:T(8,128)(2,1)}, bf16[256,1024]{1,0:T(8,128)(2,1)}, u32[]{:S(2)}, u32[]{:S(2)}) collective-permute-start(bf16[256,1024]{1,0:T(8,128)(2,1)} %get-tuple-element.11), channel_id=1, source_target_pairs={{64,0},{128,64},{192,128},{256,192},{320,256},{384,320},{448,384},... | collective-permute-start | bytes 1572872 | tf_op jit(solution)/shard_map/ppermute | solution.py:31
  78.8 6.5 %collective-permute-done.3 = bf16[256,1024]{1,0:T(8,128)(2,1)} collective-permute-done((bf16[256,1024]{1,0:T(8,128)(2,1)}, bf16[256,1024]{1,0:T(8,128)(2,1)}, u32[]{:S(2)}, u32[]{:S(2)}) %collective-permute-start.3) | collective-permute-done | bytes 524320 | tf_op jit(solution)/shard_map/ppermute | solution.py:31
  96.3 2.3 fusion.17
  102.4 13.7 %reduce-scatter.8.cloned.1.call-done = f32[256,1536]{1,0:T(8,128)} async-done(((f32[512,1536]{1,0:T(8,128)}), f32[256,1536]{1,0:T(8,128)}) %reduce-scatter.8.cloned.1.call-update) | async-done | bytes 1572880 | tf_op jit(solution)/shard_map/reduce_scatter | solution.py:162
  116.1 23.7 %reduce-scatter.16.cloned.1.call-done = f32[256,512]{1,0:T(8,128)} async-done(((f32[512,512]{1,0:T(8,128)}), f32[256,512]{1,0:T(8,128)}) %reduce-scatter.16.cloned.1.call-update) | async-done | bytes 524304 | tf_op jit(solution)/shard_map/reduce_scatter | solution.py:162
  139.9 37.6 %reduce-scatter.10.cloned.1.call-done = f32[64,1536]{1,0:T(8,128)} async-done(((f32[256,1536]{1,0:T(8,128)}), f32[64,1536]{1,0:T(8,128)}) %reduce-scatter.10.cloned.1.call-update) | async-done | bytes 393232 | tf_op jit(solution)/shard_map/reduce_scatter | solution.py:162
  183.4 26.7 %reduce-scatter.18.cloned.1.call-done = f32[64,512]{1,0:T(8,128)} async-done(((f32[256,512]{1,0:T(8,128)}), f32[64,512]{1,0:T(8,128)}) %reduce-scatter.18.cloned.1.call-update) | async-done | bytes 131088 | tf_op jit(solution)/shard_map/reduce_scatter | solution.py:162
  211.2 44.8 %reduce-scatter.12.cloned.1.call-done = f32[8,1536]{1,0:T(8,128)} async-done(((f32[64,1536]{1,0:T(8,128)}), f32[8,1536]{1,0:T(8,128)}) %reduce-scatter.12.cloned.1.call-update) | async-done | bytes 49168 | tf_op jit(solution)/shard_map/reduce_scatter | solution.py:162
  257.1 2.5 all-reduce
  259.7 7.5 %all-reduce.1 = f32[256]{0:T(256)S(1)} all-reduce(f32[256]{0:T(256)S(1)} %dynamic-slice.1), channel_id=10, replica_groups=mesh['node'=12,'y'=8,'x'=4,'core'=2] {'x'}, use_global_device_ids=true, to_apply=%region_16.17.clone | all-reduce | flops 256 | bytes 2048
  267.2 15.9 %all-reduce.2 = f32[64]{0:T(128)S(1)} all-reduce(f32[64]{0:T(128)S(1)} %dynamic-slice.3), channel_id=11, replica_groups=mesh['node'=12,'y'=8,'x'=4,'core'=2] {'y'}, use_global_device_ids=true, to_apply=%region_17.18.clone | all-reduce | flops 64 | bytes 512
  283.2 16.9 %reduce-scatter.20.cloned.1.call-done = f32[8,512]{1,0:T(8,128)} async-done(((f32[64,512]{1,0:T(8,128)}), f32[8,512]{1,0:T(8,128)}) %reduce-scatter.20.cloned.1.call-update) | async-done | bytes 16400 | tf_op jit(solution)/shard_map/reduce_scatter | solution.py:162
  300.1 45.0 %all-reduce.3 = (f32[8,512]{1,0:T(8,128)}, f32[8]{0:T(128)}) all-reduce(f32[8,512]{1,0:T(8,128)} %reduce-scatter.20.cloned.1.call-done, f32[8]{0:T(128)S(1)} %dynamic-slice.5), channel_id=1, replica_groups=mesh['node'=12,'y'=8,'x'=4,'core'=2] {'node'}, use_global_device_ids=true, to_apply=%region_13.14 | all-reduce | flops 4104 | bytes 32832 | tf_op jit(solution)/shard_map/psum | solution.py:165
  345.1 15.0 %reduce-scatter.14.cloned.1.call-done = f32[8,128]{1,0:T(8,128)} async-done(((f32[8,1536]{1,0:T(8,128)}), f32[8,128]{1,0:T(8,128)}) %reduce-scatter.14.cloned.1.call-update) | async-done | bytes 4112 | tf_op jit(solution)/shard_map/reduce_scatter | solution.py:164
  (110 shorter events, 43.8 us)
Async XLA Ops:
  7.2 19.7 %copy-start.19 = (s32[24,5]{0,1:T(8,128)S(1)}, s32[24,5]{0,1:T(8,128)}, u32[]{:S(2)}) copy-start(s32[24,5]{0,1:T(8,128)} %param.12) | copy-start | bytes 1444
  7.2 19.9 %copy-start.20 = (s32[24]{0:T(128)S(1)}, s32[24]{0:T(128)}, u32[]{:S(2)}) copy-start(s32[24]{0:T(128)} %param.13) | copy-start | bytes 292
  7.2 20.9 %copy-start.10 = (bf16[512,512]{1,0:T(8,128)(2,1)S(1)}, bf16[512,512]{1,0:T(8,128)(2,1)}, u32[]{:S(2)}) copy-start(bf16[512,512]{1,0:T(8,128)(2,1)} %param.10) | copy-start | bytes 1572868
  7.2 20.9 %copy-start.7 = (bf16[1,256,512]{2,1,0:T(8,128)(2,1)S(1)}, bf16[1,256,512]{2,1,0:T(8,128)(2,1)}, u32[]{:S(2)}) copy-start(bf16[1,256,512]{2,1,0:T(8,128)(2,1)} %param.8) | copy-start | bytes 786436
  7.2 108.8 %reduce-scatter.8.cloned.1.call-start = ((), (), s32[]{:S(2)}) async-start(), calls=%async_computation.7 | async-start | bytes 4718592 | tf_op jit(solution)/shard_map/reduce_scatter | solution.py:162
  10.3 25.8 %collective-permute-start.1 = (bf16[256,1024]{1,0:T(8,128)(2,1)S(1)}, bf16[256,1024]{1,0:T(8,128)(2,1)}, u32[]{:S(2)}, u32[]{:S(2)}) collective-permute-start(bf16[256,1024]{1,0:T(8,128)(2,1)S(1)} %slice.30), channel_id=1, source_target_pairs={{64,0},{128,64},{192,128},{256,192},{320,256},{384,320},{448,384},... | collective-permute-start | bytes 1572872 | tf_op jit(solution)/shard_map/ppermute | solution.py:23
  24.9 16.6 %collective-permute-start = (bf16[256,1024]{1,0:T(8,128)(2,1)S(1)}, bf16[256,1024]{1,0:T(8,128)(2,1)}, u32[]{:S(2)}, u32[]{:S(2)}) collective-permute-start(bf16[256,1024]{1,0:T(8,128)(2,1)S(1)} %slice.30), channel_id=1, source_target_pairs={{0,64},{64,128},{128,192},{192,256},{256,320},{320,384},{384,448},... | collective-permute-start | bytes 1572872 | tf_op jit(solution)/shard_map/ppermute | solution.py:20
  53.5 5.4 %copy-start.17 = (bf16[2,128,4,128,1]{1,3,0,4,2:T(8,128)(2,1)S(1)}, bf16[2,128,4,128,1]{1,3,0,4,2:T(8,128)(2,1)}, u32[]{:S(2)}) copy-start(bf16[2,128,4,128,1]{1,3,0,4,2:T(8,128)(2,1)} %copy.126) | copy-start | bytes 786436
  66.0 10.4 %copy-start.2 = (bf16[4,2,128,6,128]{2,4,3,1,0:T(8,128)(2,1)S(1)}, bf16[4,2,128,6,128]{2,4,3,1,0:T(8,128)(2,1)}, u32[]{:S(2)}) copy-start(bf16[4,2,128,6,128]{2,4,3,1,0:T(8,128)(2,1)} %copy-done.1) | copy-start | bytes 4718596
  66.0 10.4 %copy-start.4 = (bf16[6,128,4,128,1]{1,3,0,4,2:T(8,128)(2,1)S(1)}, bf16[6,128,4,128,1]{1,3,0,4,2:T(8,128)(2,1)}, u32[]{:S(2)}) copy-start(bf16[6,128,4,128,1]{1,3,0,4,2:T(8,128)(2,1)} %copy-done.3) | copy-start | bytes 2359300
  69.4 15.9 %collective-permute-start.3 = (bf16[256,1024]{1,0:T(8,128)(2,1)}, bf16[256,1024]{1,0:T(8,128)(2,1)}, u32[]{:S(2)}, u32[]{:S(2)}) collective-permute-start(bf16[256,1024]{1,0:T(8,128)(2,1)} %get-tuple-element.12), channel_id=1, source_target_pairs={{704,0},{0,64},{64,128},{128,192},{192,256},{256,320},{320,384},{3... | collective-permute-start | bytes 1572872 | tf_op jit(solution)/shard_map/ppermute | solution.py:31
  71.3 15.2 %collective-permute-start.2 = (bf16[256,1024]{1,0:T(8,128)(2,1)}, bf16[256,1024]{1,0:T(8,128)(2,1)}, u32[]{:S(2)}, u32[]{:S(2)}) collective-permute-start(bf16[256,1024]{1,0:T(8,128)(2,1)} %get-tuple-element.11), channel_id=1, source_target_pairs={{64,0},{128,64},{192,128},{256,192},{320,256},{384,320},{448,384},... | collective-permute-start | bytes 1572872 | tf_op jit(solution)/shard_map/ppermute | solution.py:31
  78.8 11.8 %copy-start.15 = (bf16[32,8,4,128]{3,1,2,0:T(8,128)(2,1)}, bf16[32,8,4,128]{3,1,2,0:T(8,128)(2,1)S(1)}, u32[]{:S(2)}) copy-start(bf16[32,8,4,128]{3,1,2,0:T(8,128)(2,1)S(1)} %copy.175) | copy-start | bytes 786436
  78.8 10.9 %copy-start.5 = (bf16[1,256,512]{2,1,0:T(8,128)(2,1)S(1)}, bf16[1,256,512]{2,1,0:T(8,128)(2,1)}, u32[]{:S(2)}) copy-start(bf16[1,256,512]{2,1,0:T(8,128)(2,1)} %param.7) | copy-start | bytes 786436
  78.8 10.9 %copy-start.18 = (f32[512]{0:T(512)S(1)}, f32[512]{0:T(512)}, u32[]{:S(2)}) copy-start(f32[512]{0:T(512)} %param.11) | copy-start | bytes 6148
  96.1 43.8 %reduce-scatter.16.cloned.1.call-start = ((), (), s32[]{:S(2)}) async-start(), calls=%async_computation.11 | async-start | bytes 1572864 | tf_op jit(solution)/shard_map/reduce_scatter | solution.py:162
  101.2 109.0 %copy-start.11 = (bf16[512,512]{1,0:T(8,128)(2,1)S(1)}, bf16[512,512]{1,0:T(8,128)(2,1)}, u32[]{:S(2)}) copy-start(bf16[512,512]{1,0:T(8,128)(2,1)} %param.10) | copy-start | bytes 1572868
  101.2 154.8 %copy-start.8 = (bf16[1,256,512]{2,1,0:T(8,128)(2,1)S(1)}, bf16[1,256,512]{2,1,0:T(8,128)(2,1)}, u32[]{:S(2)}) copy-start(bf16[1,256,512]{2,1,0:T(8,128)(2,1)} %param.8) | copy-start | bytes 786436
  101.2 154.8 %copy-start.13 = (f32[256,512]{1,0:T(8,128)S(1)}, f32[256,512]{1,0:T(8,128)}, u32[]{:S(2)}) copy-start(f32[256,512]{1,0:T(8,128)} %copy-done.12) | copy-start | bytes 1572868
  102.3 75.2 %reduce-scatter.10.cloned.1.call-start = ((), (), s32[]{:S(2)}) async-start(), calls=%async_computation.8 | async-start | bytes 1966080 | tf_op jit(solution)/shard_map/reduce_scatter | solution.py:162
  116.1 94.0 %reduce-scatter.18.cloned.1.call-start = ((), (), s32[]{:S(2)}) async-start(), calls=%async_computation.12 | async-start | bytes 655360 | tf_op jit(solution)/shard_map/reduce_scatter | solution.py:162
  139.9 116.1 %reduce-scatter.12.cloned.1.call-start = ((), (), s32[]{:S(2)}) async-start(), calls=%async_computation.9 | async-start | bytes 442368 | tf_op jit(solution)/shard_map/reduce_scatter | solution.py:162
  177.6 122.5 %reduce-scatter.20.cloned.1.call-start = ((), (), s32[]{:S(2)}) async-start(), calls=%async_computation.13 | async-start | bytes 147456 | tf_op jit(solution)/shard_map/reduce_scatter | solution.py:162
  210.1 149.9 %reduce-scatter.14.cloned.1.call-start = ((), (), s32[]{:S(2)}) async-start(), calls=%async_computation.10 | async-start | bytes 53248 | tf_op jit(solution)/shard_map/reduce_scatter | solution.py:164
  (8 other events, 15.4 us)
Sparse Core Ops, SparseCore 0:
  96.2 19.8 reduce-scatter.7
  119.1 20.6 reduce-scatter.15
  143.0 34.5 reduce-scatter.9
  180.5 29.5 reduce-scatter.17
  213.0 42.9 reduce-scatter.11
  258.9 41.1 reduce-scatter.19
  303.7 56.2 reduce-scatter.13

commit v2 on v1

--- a/solution.py
+++ b/solution.py
@@ -156,13 +156,29 @@
     return jnp.moveaxis(split, (2, 1, 0), (0, 1, 2)).reshape(shape)
 
 
+def exchange_sum(block, axis):
+    count = lax.axis_size(axis)
+    pieces = block.reshape((count, block.shape[0] // count) + block.shape[1:])
+    return jnp.sum(lax.all_to_all(pieces, axis, 0, 0, tiled=False), axis=0)
+
+
 def reduce_terms(term_qkv, term_out, term_gain):
-    parts = (section_order(term_qkv), section_order(term_out), section_order(term_gain))
+    rows, model_width = term_out.shape
+    gain_block = jnp.zeros((rows, 128), jnp.float32).at[:, 0].set(term_gain)
+    joined = section_order(jnp.concatenate([term_qkv, term_out, gain_block], axis=1))
     for axis in ("core", "x", "y"):
-        parts = tuple(lax.psum_scatter(p, axis, scatter_dimension=0, tiled=True) for p in parts)
-    part_qkv, part_out, part_gain = parts
-    part_qkv = lax.psum_scatter(part_qkv, "node", scatter_dimension=1, tiled=True)
-    part_out, part_gain = lax.psum((part_out, part_gain), "node")
+        joined = exchange_sum(joined, axis)
+    node_count = lax.axis_size("node")
+    qkv_width = term_qkv.shape[1]
+    own_rows = joined.shape[0]
+    qkv_blocks = jnp.moveaxis(joined[:, :qkv_width].reshape(own_rows, node_count, -1), 1, 0)
+    shared = jnp.broadcast_to(joined[None, :, qkv_width:], (node_count, own_rows, joined.shape[1] - qkv_width))
+    mixed = jnp.concatenate([qkv_blocks, shared], axis=2)
+    summed = jnp.sum(lax.all_to_all(mixed, "node", 0, 0, tiled=False), axis=0)
+    block_width = qkv_width // node_count
+    part_qkv = summed[:, :block_width]
+    part_out = summed[:, block_width : block_width + model_width]
+    part_gain = summed[:, block_width + model_width]
     return (part_qkv, part_out, part_gain)
 
 

time: 368 us -> 188 us (0.51)
  waiting for transfers between devices: 198 us -> 25.7 us
  between operations: 16.5 us -> 1.05 us
  other arithmetic: 10.7 us -> 22 us
  local copies, waits for them, and re-layouts: 32.1 us -> 24.5 us
  blocking collectives: 70.8 us -> 64.2 us
  starting transfers between devices: 24 us -> 29.9 us
  matrix products: 14.6 us -> 18.4 us
    reduce_scatter x7 -> x0, waiting for transfers between devices: 178 us -> none  [the longest x6 163 us: reduce_terms(): lax.psum_scatter(p, axis, scatter_dimension=0, tiled=True)]
    all_to_all x0 -> x3, blocking collectives: none -> 64.2 us  [exchange_sum(): return jnp.sum(lax.all_to_all(pieces, axis, 0, 0, tiled=False), axis=0)]
    psum x1 -> x0, blocking collectives: 45 us -> none  [reduce_terms(): part_out, part_gain = lax.psum((part_out, part_gain), 'node')]
    unnamed x3 -> x0, blocking collectives: 25.8 us -> none
    all_to_all x0 -> x1, waiting for transfers between devices: none -> 10.8 us  [reduce_terms(): summed = jnp.sum(lax.all_to_all(mixed, 'node', 0, 0, tiled=False), axis=0)]
    unnamed x51 -> x30, local copies, waits for them, and re-layouts: 9.95 us -> 3 us
    reduce_sum x1 -> x4, other arithmetic: 0.92 us -> 7.11 us  [the longest x3 7.09 us: exchange_sum(): return jnp.sum(lax.all_to_all(pieces, axis, 0, 0, tiled=False), axis=0)]
    all_to_all x0 -> x1, starting transfers between devices: none -> 6.17 us  [reduce_terms(): summed = jnp.sum(lax.all_to_all(mixed, 'node', 0, 0, tiled=False), axis=0)]
  transfers between devices with their start and end apart: 11 -> 5, of which waited for: 11 -> 5; matrix products, arithmetic and copies ran while one was open for 5% -> 7% of each run, Pallas kernels for 0% -> 0%
where the time goes in v2:
time: 188 us; the launch traced here: 186 us
  blocking collectives  64.2 us (34%)
  starting transfers between devices  29.9 us (16%)
  waiting for transfers between devices  25.7 us (14%)
  local copies, waits for them, and re-layouts  24.5 us (13%)
  other arithmetic  22 us (12%)
  matrix products  18.4 us (10%)
    all_to_all x3, blocking collectives, exchange_sum(): return jnp.sum(lax.all_to_all(pieces, axis, 0, 0, tiled=False), axis=0)  64.2 us
    ppermute x1, starting transfers between devices, extended(): lax.ppermute(lax.slice_in_dim(block, 0, width, axis=dim), axis, backward)  14.6 us
    all_to_all x1, waiting for transfers between devices, reduce_terms(): summed = jnp.sum(lax.all_to_all(mixed, 'node', 0, 0, tiled=False), axis=0)  10.8 us
    ppermute x2, starting transfers between devices, passed_along(): return lax.ppermute(block, axis, route)  7.22 us
    reduce_sum x3, other arithmetic, exchange_sum(): return jnp.sum(lax.all_to_all(pieces, axis, 0, 0, tiled=False), axis=0)  7.09 us
    ppermute x2, waiting for transfers between devices, passed_along(): return lax.ppermute(block, axis, route)  6.21 us
    all_to_all x1, starting transfers between devices, reduce_terms(): summed = jnp.sum(lax.all_to_all(mixed, 'node', 0, 0, tiled=False), axis=0)  6.17 us
    ppermute x1, waiting for transfers between devices, extended(): lax.ppermute(lax.slice_in_dim(block, block.shape[dim] - width, None, axis...  5.43 us
  transfers between devices with their start and end apart: 5, of which 5 were waited for; matrix products, arithmetic and copies ran while one was open for 7% of the time, Pallas kernels for 0%

profile of v2, /device:TPU:6, one launch (start us, length us, event | category | flops | bytes accessed | tf_op | source)
XLA Modules:
  0.0 185.8 jit_solution(1967086110242260077)
XLA Ops:
  3.8 14.6 %collective-permute-start.1 = (bf16[256,1024]{1,0:T(8,128)(2,1)S(1)}, bf16[256,1024]{1,0:T(8,128)(2,1)}, u32[]{:S(2)}, u32[]{:S(2)}) collective-permute-start(bf16[256,1024]{1,0:T(8,128)(2,1)S(1)} %slice.64), channel_id=1, source_target_pairs={{64,0},{128,64},{192,128},{256,192},{320,256},{384,320},{448,384},... | collective-permute-start | bytes 1572872 | tf_op jit(solution)/shard_map/ppermute | solution.py:23
  18.4 1.9 %collective-permute-start = (bf16[256,1024]{1,0:T(8,128)(2,1)S(1)}, bf16[256,1024]{1,0:T(8,128)(2,1)}, u32[]{:S(2)}, u32[]{:S(2)}) collective-permute-start(bf16[256,1024]{1,0:T(8,128)(2,1)S(1)} %slice.64), channel_id=1, source_target_pairs={{0,64},{64,128},{128,192},{192,256},{256,320},{320,384},{384,448},... | collective-permute-start | bytes 1572872 | tf_op jit(solution)/shard_map/ppermute | solution.py:20
  26.3 3.2 %collective-permute-done.1 = bf16[256,1024]{1,0:T(8,128)(2,1)} collective-permute-done((bf16[256,1024]{1,0:T(8,128)(2,1)S(1)}, bf16[256,1024]{1,0:T(8,128)(2,1)}, u32[]{:S(2)}, u32[]{:S(2)}) %collective-permute-start.1) | collective-permute-done | bytes 524320 | tf_op jit(solution)/shard_map/ppermute | solution.py:23
  29.5 5.4 %collective-permute-done = bf16[256,1024]{1,0:T(8,128)(2,1)} collective-permute-done((bf16[256,1024]{1,0:T(8,128)(2,1)S(1)}, bf16[256,1024]{1,0:T(8,128)(2,1)}, u32[]{:S(2)}, u32[]{:S(2)}) %collective-permute-start) | collective-permute-done | bytes 524320 | tf_op jit(solution)/shard_map/ppermute | solution.py:20
  38.1 2.0 %reshape.128 = bf16[6,128,4,128]{3,2,1,0:T(4,128)(2,1)S(1)} reshape(bf16[768,512]{1,0:T(8,128)(2,1)} %get-tuple-element.23) | data formatting | bytes 1572864 | tf_op jit(solution)/shard_map/reshape | solution.py:53
  48.2 2.7 %fusion.7 = f32[6,128,4,128]{1,3,0,2:T(8,128)} fusion(bf16[2,128,4,128,1]{1,3,0,4,2:T(8,128)(2,1)} %copy-done.8, bf16[4,2,128,6,128]{2,4,3,1,0:T(8,128)(2,1)S(1)} %get-tuple-element.19), kind=kOutput, calls=%fused_computation.17 | convolution fusion | flops 201326592 | bytes 3407872 | tf_op jit(solution)/shard_map/natbs,atnd->bsnd/dot_general | solution.py:87
  50.9 2.6 %copy.79 = f32[6,128,4,128]{3,2,1,0:T(4,128)} copy(f32[6,128,4,128]{1,3,0,2:T(8,128)} %fusion.7) | data formatting | bytes 3145728 | tf_op jit(solution)/shard_map/natbs,atnd->bsnd/transpose | solution.py:87
  53.5 2.7 %bitcast_dynamic-update-slice_fusion.1 = f32[768,1024]{1,0:T(8,128)} fusion(f32[96,8,4,128]{3,2,1,0:T(4,128)} %bitcast.111), kind=kLoop, calls=%fused_computation.11 | loop fusion | bytes 3145728
  56.2 2.6 %copy.82 = f32[6,128,4,128]{3,2,1,0:T(4,128)} copy(f32[6,128,4,128]{1,3,0,2:T(8,128)} %fusion.10) | data formatting | bytes 3145728 | tf_op jit(solution)/shard_map/natbs,atnd->bsnd/transpose | solution.py:90
  58.9 2.7 %bitcast_dynamic-update-slice_fusion = f32[768,1024]{1,0:T(8,128)} fusion(f32[768,1024]{1,0:T(8,128)} %bitcast_dynamic-update-slice_fusion.1, f32[96,8,4,128]{3,2,1,0:T(4,128)} %bitcast.110), kind=kLoop, calls=%fused_computation.10 | loop fusion | bytes 3145728 | tf_op jit(solution)/shard_map/concatenate | solution.py:93
  61.6 2.2 %convert.14 = bf16[768,1024]{1,0:T(8,128)(2,1)S(1)} convert(f32[768,1024]{1,0:T(8,128)} %bitcast_dynamic-update-slice_fusion) | non-fusion elementwise | flops 786432 | bytes 4718592 | tf_op jit(solution)/shard_map/convert.6
  64.8 1.9 %collective-permute-start.3 = (bf16[256,1024]{1,0:T(8,128)(2,1)}, bf16[256,1024]{1,0:T(8,128)(2,1)}, u32[]{:S(2)}, u32[]{:S(2)}) collective-permute-start(bf16[256,1024]{1,0:T(8,128)(2,1)} %get-tuple-element.22), channel_id=1, source_target_pairs={{704,0},{0,64},{64,128},{128,192},{192,256},{256,320},{320,384},{3... | collective-permute-start | bytes 1572872 | tf_op jit(solution)/shard_map/ppermute | solution.py:31
  66.7 5.3 %collective-permute-start.2 = (bf16[256,1024]{1,0:T(8,128)(2,1)}, bf16[256,1024]{1,0:T(8,128)(2,1)}, u32[]{:S(2)}, u32[]{:S(2)}) collective-permute-start(bf16[256,1024]{1,0:T(8,128)(2,1)} %get-tuple-element.21), channel_id=1, source_target_pairs={{64,0},{128,64},{192,128},{256,192},{320,256},{384,320},{448,384},... | collective-permute-start | bytes 1572872 | tf_op jit(solution)/shard_map/ppermute | solution.py:31
  75.7 5.0 %collective-permute-done.3 = bf16[256,1024]{1,0:T(8,128)(2,1)} collective-permute-done((bf16[256,1024]{1,0:T(8,128)(2,1)}, bf16[256,1024]{1,0:T(8,128)(2,1)}, u32[]{:S(2)}, u32[]{:S(2)}) %collective-permute-start.3) | collective-permute-done | bytes 524320 | tf_op jit(solution)/shard_map/ppermute | solution.py:31
  85.2 2.4 %fusion.36 = f32[512,1536]{1,0:T(8,128)} fusion(bf16[256,1024]{1,0:T(8,128)(2,1)S(1)} %fusion.20, bf16[256,512]{1,0:T(8,128)(2,1)S(1)} %bitcast.119, bf16[1,256,512]{2,1,0:T(8,128)(2,1)S(1)} %copy-done.3, f32[512]{0:T(512)S(1)} %copy-done.11, f32[256]{0:T(256)S(1)} %add_rsqrt_fusion), kind=kOutput, calls=%fused_computation.50 | convolution fusion | flops 404750336 | bytes 4197376 | tf_op jit(solution)/shard_map/dot_general | solution.py:137
  88.3 2.2 %select_maximum_fusion = f32[512,2176]{1,0:T(8,128)S(1)} fusion(f32[512,1]{1,0:T(8,128)S(1)} %copy.83, f32[512,512]{1,0:T(8,128)S(1)} %fusion.39, f32[512,1536]{1,0:T(8,128)} %fusion.36), kind=kLoop, calls=%fused_computation | loop fusion | flops 4456448 | bytes 8652800 | tf_op jit(solution)/shard_map/concatenate | solution.py:168
  90.8 8.4 %all_to_all.20 = f32[2,256,2176]{2,1,0:T(8,128)} all-to-all(f32[2,256,2176]{2,1,0:T(8,128)S(1)} %bitcast.108), channel_id=1, replica_groups=mesh['node'=12,'y'=8,'x'=4,'core'=2] {'core'}, dimensions={0} | all-to-all | bytes 8912896 | tf_op jit(solution)/shard_map/all_to_all | solution.py:162
  99.2 4.2 %reduce_sum.86 = f32[256,2176]{1,0:T(8,128)} reduce(f32[2,256,2176]{2,1,0:T(8,128)} %all_to_all.20, f32[]{:T(128)} %constant.53.clone.1), dimensions={0}, to_apply=%region_8.9 | reduce | flops 557056 | bytes 6684676 | tf_op jit(solution)/shard_map/reduce_sum | solution.py:162
  103.4 31.2 %all_to_all.21 = f32[4,64,2176]{2,1,0:T(8,128)} all-to-all(f32[4,64,2176]{2,1,0:T(8,128)} %bitcast.109), channel_id=1, replica_groups=mesh['node'=12,'y'=8,'x'=4,'core'=2] {'x'}, dimensions={0} | all-to-all | bytes 4456448 | tf_op jit(solution)/shard_map/all_to_all | solution.py:162
  136.4 24.6 %all_to_all.22 = f32[8,8,2176]{2,1,0:T(8,128)} all-to-all(f32[8,8,2176]{2,1,0:T(8,128)S(1)} %bitcast.117), channel_id=1, replica_groups=mesh['node'=12,'y'=8,'x'=4,'core'=2] {'y'}, dimensions={0} | all-to-all | bytes 1114112 | tf_op jit(solution)/shard_map/all_to_all | solution.py:162
  162.9 6.2 %all-to-all-start.3 = ((f32[12,8,768]{2,1,0:T(8,128)}), f32[12,8,768]{2,1,0:T(8,128)S(1)}, u32[]{:S(2)}, u32[]{:S(2)}) async-start(f32[12,8,768]{2,1,0:T(8,128)} %pad_maximum_fusion.4), calls=%async_computation.3 | async-start | bytes 589824 | tf_op jit(solution)/shard_map/all_to_all | solution.py:177
  169.1 2.0 %fusion.18 = bf16[1,256,512]{2,1,0:T(8,128)(2,1)} fusion(bf16[512,512]{1,0:T(8,128)(2,1)} %param.12, bf16[1,256,512]{2,1,0:T(8,128)(2,1)S(1)} %copy-done.3, bf16[32,8,4,128]{3,2,1,0:T(4,128)(2,1)S(1)} %bitcast.116), kind=kOutput, calls=%fused_computation.28 | convolution fusion | flops 134610944 | bytes 1310720 | tf_op jit(solution)/shard_map/dot_general | solution.py:116
  171.2 2.0 %fusion.38 = bf16[1,256,512]{2,1,0:T(8,128)(2,1)} fusion(f32[256,512]{1,0:T(8,128)} %get-tuple-element.29, bf16[1,256,512]{2,1,0:T(8,128)(2,1)S(1)} %copy-done.7, bf16[1,256,512]{2,1,0:T(8,128)(2,1)S(1)} %copy-done.3, f32[256]{0:T(256)S(1)} %broadcast_multiply_fusion, f32[512]{0:T(512)S(1)} %copy-done.11, f32[256]{0:T(256)S(1)} %add_rsqrt_fusion), kind=kLoop, calls=%fused_computation.53 | loop fusion | flops 1179648 | bytes 1314816 | tf_op jit(solution)/shard_map/broadcast_in_dim | solution.py:149
  173.1 10.8 %all-to-all-done.3 = f32[12,8,768]{2,1,0:T(8,128)S(1)} async-done(((f32[12,8,768]{2,1,0:T(8,128)}), f32[12,8,768]{2,1,0:T(8,128)S(1)}, u32[]{:S(2)}, u32[]{:S(2)}) %all-to-all-start.3) | async-done | bytes 294944 | tf_op jit(solution)/shard_map/all_to_all | solution.py:177
  (77 shorter events, 35.7 us)
Async XLA Ops:
  0.6 1.5 copy-start
  0.6 19.7 %copy-start.12 = (s32[24,5]{0,1:T(8,128)S(1)}, s32[24,5]{0,1:T(8,128)}, u32[]{:S(2)}) copy-start(s32[24,5]{0,1:T(8,128)} %param.14) | copy-start | bytes 1444
  0.7 19.9 %copy-start.13 = (s32[24]{0:T(128)S(1)}, s32[24]{0:T(128)}, u32[]{:S(2)}) copy-start(s32[24]{0:T(128)} %param.15) | copy-start | bytes 292
  0.7 21.9 %copy-start.9 = (bf16[512,512]{1,0:T(8,128)(2,1)S(1)}, bf16[512,512]{1,0:T(8,128)(2,1)}, u32[]{:S(2)}) copy-start(bf16[512,512]{1,0:T(8,128)(2,1)} %param.12) | copy-start | bytes 1572868
  0.7 21.8 %copy-start.6 = (bf16[1,256,512]{2,1,0:T(8,128)(2,1)S(1)}, bf16[1,256,512]{2,1,0:T(8,128)(2,1)}, u32[]{:S(2)}) copy-start(bf16[1,256,512]{2,1,0:T(8,128)(2,1)} %param.10) | copy-start | bytes 786436
  3.8 25.8 %collective-permute-start.1 = (bf16[256,1024]{1,0:T(8,128)(2,1)S(1)}, bf16[256,1024]{1,0:T(8,128)(2,1)}, u32[]{:S(2)}, u32[]{:S(2)}) collective-permute-start(bf16[256,1024]{1,0:T(8,128)(2,1)S(1)} %slice.64), channel_id=1, source_target_pairs={{64,0},{128,64},{192,128},{256,192},{320,256},{384,320},{448,384},... | collective-permute-start | bytes 1572872 | tf_op jit(solution)/shard_map/ppermute | solution.py:23
  18.4 16.6 %collective-permute-start = (bf16[256,1024]{1,0:T(8,128)(2,1)S(1)}, bf16[256,1024]{1,0:T(8,128)(2,1)}, u32[]{:S(2)}, u32[]{:S(2)}) collective-permute-start(bf16[256,1024]{1,0:T(8,128)(2,1)S(1)} %slice.64), channel_id=1, source_target_pairs={{0,64},{64,128},{128,192},{192,256},{256,320},{320,384},{384,448},... | collective-permute-start | bytes 1572872 | tf_op jit(solution)/shard_map/ppermute | solution.py:20
  22.5 17.6 %copy-start.8 = (bf16[2,128,4,128,1]{1,3,0,4,2:T(8,128)(2,1)}, bf16[2,128,4,128,1]{1,3,0,4,2:T(8,128)(2,1)S(1)}, u32[]{:S(2)}) copy-start(bf16[2,128,4,128,1]{1,3,0,4,2:T(8,128)(2,1)S(1)} %copy.96) | copy-start | bytes 786436
  38.1 3.6 %copy-start.1 = (bf16[6,128,4,128,1]{1,3,0,4,2:T(8,128)(2,1)}, bf16[6,128,4,128,1]{1,3,0,4,2:T(8,128)(2,1)S(1)}, u32[]{:S(2)}) copy-start(bf16[6,128,4,128,1]{1,3,0,4,2:T(8,128)(2,1)S(1)} %copy.93) | copy-start | bytes 2359300
  40.2 1.5 copy-start.4
  40.2 1.5 copy-start.10
  42.8 1.3 copy-start.5
  61.6 10.5 %copy-start.2 = (bf16[6,128,4,128,1]{1,3,0,4,2:T(8,128)(2,1)S(1)}, bf16[6,128,4,128,1]{1,3,0,4,2:T(8,128)(2,1)}, u32[]{:S(2)}) copy-start(bf16[6,128,4,128,1]{1,3,0,4,2:T(8,128)(2,1)} %copy-done.1) | copy-start | bytes 2359300
  64.8 15.9 %collective-permute-start.3 = (bf16[256,1024]{1,0:T(8,128)(2,1)}, bf16[256,1024]{1,0:T(8,128)(2,1)}, u32[]{:S(2)}, u32[]{:S(2)}) collective-permute-start(bf16[256,1024]{1,0:T(8,128)(2,1)} %get-tuple-element.22), channel_id=1, source_target_pairs={{704,0},{0,64},{64,128},{128,192},{192,256},{256,320},{320,384},{3... | collective-permute-start | bytes 1572872 | tf_op jit(solution)/shard_map/ppermute | solution.py:31
  66.7 15.2 %collective-permute-start.2 = (bf16[256,1024]{1,0:T(8,128)(2,1)}, bf16[256,1024]{1,0:T(8,128)(2,1)}, u32[]{:S(2)}, u32[]{:S(2)}) collective-permute-start(bf16[256,1024]{1,0:T(8,128)(2,1)} %get-tuple-element.21), channel_id=1, source_target_pairs={{64,0},{128,64},{192,128},{256,192},{320,256},{384,320},{448,384},... | collective-permute-start | bytes 1572872 | tf_op jit(solution)/shard_map/ppermute | solution.py:31
  73.2 10.5 %copy-start.3 = (bf16[1,256,512]{2,1,0:T(8,128)(2,1)S(1)}, bf16[1,256,512]{2,1,0:T(8,128)(2,1)}, u32[]{:S(2)}) copy-start(bf16[1,256,512]{2,1,0:T(8,128)(2,1)} %param.9) | copy-start | bytes 786436
  73.2 10.5 %copy-start.11 = (f32[512]{0:T(512)S(1)}, f32[512]{0:T(512)}, u32[]{:S(2)}) copy-start(f32[512]{0:T(512)} %param.13) | copy-start | bytes 6148
  134.6 36.6 %copy-start.7 = (bf16[1,256,512]{2,1,0:T(8,128)(2,1)S(1)}, bf16[1,256,512]{2,1,0:T(8,128)(2,1)}, u32[]{:S(2)}) copy-start(bf16[1,256,512]{2,1,0:T(8,128)(2,1)} %param.10) | copy-start | bytes 786436
  162.9 21.0 %all-to-all-start.3 = ((f32[12,8,768]{2,1,0:T(8,128)}), f32[12,8,768]{2,1,0:T(8,128)S(1)}, u32[]{:S(2)}, u32[]{:S(2)}) async-start(f32[12,8,768]{2,1,0:T(8,128)} %pad_maximum_fusion.4), calls=%async_computation.3 | async-start | bytes 589824 | tf_op jit(solution)/shard_map/all_to_all | solution.py:177

commit v3 on v2

--- a/solution.py
+++ b/solution.py
@@ -159,7 +159,11 @@
 def exchange_sum(block, axis):
     count = lax.axis_size(axis)
     pieces = block.reshape((count, block.shape[0] // count) + block.shape[1:])
-    return jnp.sum(lax.all_to_all(pieces, axis, 0, 0, tiled=False), axis=0)
+    return wide_sum(lax.all_to_all(pieces.astype(jnp.bfloat16), axis, 0, 0, tiled=False))
+
+
+def wide_sum(pieces):
+    return jnp.sum(pieces.astype(jnp.float32), axis=0)
 
 
 def reduce_terms(term_qkv, term_out, term_gain):
@@ -174,7 +178,7 @@
     qkv_blocks = jnp.moveaxis(joined[:, :qkv_width].reshape(own_rows, node_count, -1), 1, 0)
     shared = jnp.broadcast_to(joined[None, :, qkv_width:], (node_count, own_rows, joined.shape[1] - qkv_width))
     mixed = jnp.concatenate([qkv_blocks, shared], axis=2)
-    summed = jnp.sum(lax.all_to_all(mixed, "node", 0, 0, tiled=False), axis=0)
+    summed = wide_sum(lax.all_to_all(mixed.astype(jnp.bfloat16), "node", 0, 0, tiled=False))
     block_width = qkv_width // node_count
     part_qkv = summed[:, :block_width]
     part_out = summed[:, block_width : block_width + model_width]

time: 188 us -> 158 us (0.84)
  blocking collectives: 64.2 us -> 25.2 us
  waiting for transfers between devices: 25.7 us -> 34.9 us
  starting transfers between devices: 29.9 us -> 37.1 us
  other arithmetic: 22 us -> 16 us
    all_to_all x3 -> x2, blocking collectives: 64.2 us -> 25.2 us  [exchange_sum(): lax.all_to_all(pieces.astype(jnp.bfloat16), axis, 0, 0, tiled=False)]
    all_to_all x1 -> x2, waiting for transfers between devices: 10.8 us -> 20 us  [the longest x1 10.7 us: reduce_terms(): lax.all_to_all(mixed.astype(jnp.bfloat16), 'node', 0, 0, tiled=False)]
    all_to_all x1 -> x2, starting transfers between devices: 6.17 us -> 13.4 us  [the longest x1 7.25 us: exchange_sum(): lax.all_to_all(pieces.astype(jnp.bfloat16), axis, 0, 0, tiled=False)]
    reduce_sum x4, other arithmetic: 7.11 us -> 4.3 us  [wide_sum(): return jnp.sum(pieces.astype(jnp.float32), axis=0)]
    concatenate x1, other arithmetic: 2.19 us -> 0.16 us  [reduce_terms(): jnp.concatenate([term_qkv, term_out, gain_block], axis=1)]
  transfers between devices with their start and end apart: 5 -> 6, of which waited for: 5 -> 6; matrix products, arithmetic and copies ran while one was open for 7% -> 8% of each run, Pallas kernels for 0% -> 0%
where the time goes in v3:
time: 158 us; the launch traced here: 156 us
  starting transfers between devices  37.1 us (23%)
  waiting for transfers between devices  34.9 us (22%)
  blocking collectives  25.2 us (16%)
  local copies, waits for them, and re-layouts  24.7 us (16%)
  matrix products  16.8 us (11%)
  other arithmetic  16 us (10%)
    all_to_all x2, blocking collectives, exchange_sum(): lax.all_to_all(pieces.astype(jnp.bfloat16), axis, 0, 0, tiled=False)  25.2 us
    ppermute x1, starting transfers between devices, extended(): lax.ppermute(lax.slice_in_dim(block, 0, width, axis=dim), axis, backward)  14.6 us
    all_to_all x1, waiting for transfers between devices, reduce_terms(): lax.all_to_all(mixed.astype(jnp.bfloat16), 'node', 0, 0, tiled=False)  10.7 us
    all_to_all x1, waiting for transfers between devices, exchange_sum(): lax.all_to_all(pieces.astype(jnp.bfloat16), axis, 0, 0, tiled=False)  9.34 us
    all_to_all x1, starting transfers between devices, exchange_sum(): lax.all_to_all(pieces.astype(jnp.bfloat16), axis, 0, 0, tiled=False)  7.25 us
    ppermute x2, starting transfers between devices, passed_along(): return lax.ppermute(block, axis, route)  7.22 us
    ppermute x2, waiting for transfers between devices, passed_along(): return lax.ppermute(block, axis, route)  6.22 us
    all_to_all x1, starting transfers between devices, reduce_terms(): lax.all_to_all(mixed.astype(jnp.bfloat16), 'node', 0, 0, tiled=False)  6.14 us
  transfers between devices with their start and end apart: 6, of which 6 were waited for; matrix products, arithmetic and copies ran while one was open for 8% of the time, Pallas kernels for 0%

profile of v3, /device:TPU:6, one launch (start us, length us, event | category | flops | bytes accessed | tf_op | source)
XLA Modules:
  0.0 155.8 jit_solution(10176709787016092815)
XLA Ops:
  3.8 14.6 %collective-permute-start.1 = (bf16[256,1024]{1,0:T(8,128)(2,1)S(1)}, bf16[256,1024]{1,0:T(8,128)(2,1)}, u32[]{:S(2)}, u32[]{:S(2)}) collective-permute-start(bf16[256,1024]{1,0:T(8,128)(2,1)S(1)} %slice.65), channel_id=1, source_target_pairs={{64,0},{128,64},{192,128},{256,192},{320,256},{384,320},{448,384},... | collective-permute-start | bytes 1572872 | tf_op jit(solution)/shard_map/ppermute | solution.py:23
  18.4 1.9 %collective-permute-start = (bf16[256,1024]{1,0:T(8,128)(2,1)S(1)}, bf16[256,1024]{1,0:T(8,128)(2,1)}, u32[]{:S(2)}, u32[]{:S(2)}) collective-permute-start(bf16[256,1024]{1,0:T(8,128)(2,1)S(1)} %slice.65), channel_id=1, source_target_pairs={{0,64},{64,128},{128,192},{192,256},{256,320},{320,384},{384,448},... | collective-permute-start | bytes 1572872 | tf_op jit(solution)/shard_map/ppermute | solution.py:20
  26.4 3.2 %collective-permute-done.1 = bf16[256,1024]{1,0:T(8,128)(2,1)} collective-permute-done((bf16[256,1024]{1,0:T(8,128)(2,1)S(1)}, bf16[256,1024]{1,0:T(8,128)(2,1)}, u32[]{:S(2)}, u32[]{:S(2)}) %collective-permute-start.1) | collective-permute-done | bytes 524320 | tf_op jit(solution)/shard_map/ppermute | solution.py:23
  29.6 5.4 %collective-permute-done = bf16[256,1024]{1,0:T(8,128)(2,1)} collective-permute-done((bf16[256,1024]{1,0:T(8,128)(2,1)S(1)}, bf16[256,1024]{1,0:T(8,128)(2,1)}, u32[]{:S(2)}, u32[]{:S(2)}) %collective-permute-start) | collective-permute-done | bytes 524320 | tf_op jit(solution)/shard_map/ppermute | solution.py:20
  38.2 2.0 %reshape.128 = bf16[6,128,4,128]{3,2,1,0:T(4,128)(2,1)S(1)} reshape(bf16[768,512]{1,0:T(8,128)(2,1)} %get-tuple-element.23) | data formatting | bytes 1572864 | tf_op jit(solution)/shard_map/reshape | solution.py:53
  45.5 1.8 %fusion.12 = f32[6,128,4,128]{1,3,0,2:T(8,128)} fusion(bf16[2,128,4,128,1]{1,3,0,4,2:T(8,128)(2,1)S(1)} %copy-done.10, bf16[4,2,128,6,128]{2,4,3,1,0:T(8,128)(2,1)S(1)} %get-tuple-element.20), kind=kOutput, calls=%fused_computation.20 | convolution fusion | flops 201326592 | bytes 3407872 | tf_op jit(solution)/shard_map/natbs,atnd->bsnd/dot_general | solution.py:90
  48.5 2.8 %fusion.9 = f32[6,128,4,128]{1,3,0,2:T(8,128)} fusion(bf16[2,128,4,128,1]{1,3,0,4,2:T(8,128)(2,1)} %copy-done.8, bf16[4,2,128,6,128]{2,4,3,1,0:T(8,128)(2,1)S(1)} %get-tuple-element.19), kind=kOutput, calls=%fused_computation.19 | convolution fusion | flops 201326592 | bytes 3407872 | tf_op jit(solution)/shard_map/natbs,atnd->bsnd/dot_general | solution.py:87
  51.2 2.6 %copy.79 = f32[6,128,4,128]{3,2,1,0:T(4,128)} copy(f32[6,128,4,128]{1,3,0,2:T(8,128)} %fusion.9) | data formatting | bytes 3145728 | tf_op jit(solution)/shard_map/natbs,atnd->bsnd/transpose | solution.py:87
  53.8 2.7 %bitcast_dynamic-update-slice_fusion.1 = f32[768,1024]{1,0:T(8,128)} fusion(f32[96,8,4,128]{3,2,1,0:T(4,128)} %bitcast.109), kind=kLoop, calls=%fused_computation.13 | loop fusion | bytes 3145728
  56.5 2.6 %copy.82 = f32[6,128,4,128]{3,2,1,0:T(4,128)} copy(f32[6,128,4,128]{1,3,0,2:T(8,128)} %fusion.12) | data formatting | bytes 3145728 | tf_op jit(solution)/shard_map/natbs,atnd->bsnd/transpose | solution.py:90
  59.2 2.7 %bitcast_dynamic-update-slice_fusion = f32[768,1024]{1,0:T(8,128)} fusion(f32[768,1024]{1,0:T(8,128)} %bitcast_dynamic-update-slice_fusion.1, f32[96,8,4,128]{3,2,1,0:T(4,128)} %bitcast.108), kind=kLoop, calls=%fused_computation.12 | loop fusion | bytes 3145728 | tf_op jit(solution)/shard_map/concatenate | solution.py:93
  61.9 2.1 %convert.38 = bf16[768,1024]{1,0:T(8,128)(2,1)S(1)} convert(f32[768,1024]{1,0:T(8,128)} %bitcast_dynamic-update-slice_fusion) | non-fusion elementwise | flops 786432 | bytes 4718592 | tf_op jit(solution)/shard_map/convert.19
  65.1 1.9 %collective-permute-start.3 = (bf16[256,1024]{1,0:T(8,128)(2,1)}, bf16[256,1024]{1,0:T(8,128)(2,1)}, u32[]{:S(2)}, u32[]{:S(2)}) collective-permute-start(bf16[256,1024]{1,0:T(8,128)(2,1)} %get-tuple-element.22), channel_id=1, source_target_pairs={{704,0},{0,64},{64,128},{128,192},{192,256},{256,320},{320,384},{3... | collective-permute-start | bytes 1572872 | tf_op jit(solution)/shard_map/ppermute | solution.py:31
  67.0 5.3 %collective-permute-start.2 = (bf16[256,1024]{1,0:T(8,128)(2,1)}, bf16[256,1024]{1,0:T(8,128)(2,1)}, u32[]{:S(2)}, u32[]{:S(2)}) collective-permute-start(bf16[256,1024]{1,0:T(8,128)(2,1)} %get-tuple-element.21), channel_id=1, source_target_pairs={{64,0},{128,64},{192,128},{256,192},{320,256},{384,320},{448,384},... | collective-permute-start | bytes 1572872 | tf_op jit(solution)/shard_map/ppermute | solution.py:31
  76.0 5.0 %collective-permute-done.3 = bf16[256,1024]{1,0:T(8,128)(2,1)} collective-permute-done((bf16[256,1024]{1,0:T(8,128)(2,1)}, bf16[256,1024]{1,0:T(8,128)(2,1)}, u32[]{:S(2)}, u32[]{:S(2)}) %collective-permute-start.3) | collective-permute-done | bytes 524320 | tf_op jit(solution)/shard_map/ppermute | solution.py:31
  82.2 1.8 %fusion.22 = bf16[256,1024]{1,0:T(8,128)(2,1)S(1)} fusion(f32[768,1024]{1,0:T(8,128)} %bitcast_dynamic-update-slice_fusion, bf16[256,1024]{1,0:T(8,128)(2,1)} %collective-permute-done.3, bf16[256,1024]{1,0:T(8,128)(2,1)} %collective-permute-done.2), kind=kLoop, calls=%fused_computation.34 | loop fusion | flops 1310720 | bytes 2621440 | tf_op jit(solution)/shard_map/convert.15
  87.4 6.4 %all_to_all.20 = bf16[2,256,2176]{2,1,0:T(8,128)(2,1)} all-to-all(bf16[2,256,2176]{2,1,0:T(8,128)(2,1)S(1)} %bitcast.107), channel_id=1, replica_groups=mesh['node'=12,'y'=8,'x'=4,'core'=2] {'core'}, dimensions={0} | all-to-all | bytes 4456448 | tf_op jit(solution)/shard_map/all_to_all | solution.py:162
  93.8 3.3 %reduce_sum.92 = bf16[256,2176]{1,0:T(8,128)(2,1)} reduce(bf16[2,256,2176]{2,1,0:T(8,128)(2,1)} %all_to_all.20, bf16[]{:T(256)} %constant.71.clone.1), dimensions={0}, to_apply=%region_8.9 | reduce | flops 557056 | bytes 3342338 | tf_op jit(solution)/shard_map/reduce_sum | solution.py:166
  97.1 18.8 %all_to_all.21 = bf16[4,64,2176]{2,1,0:T(8,128)(2,1)S(1)} all-to-all(bf16[4,64,2176]{2,1,0:T(8,128)(2,1)} %bitcast.110), channel_id=1, replica_groups=mesh['node'=12,'y'=8,'x'=4,'core'=2] {'x'}, dimensions={0} | all-to-all | bytes 2228224 | tf_op jit(solution)/shard_map/all_to_all | solution.py:162
  116.8 7.2 %all-to-all-start.2 = ((bf16[8,8,2176]{2,1,0:T(8,128)(2,1)}), bf16[8,8,2176]{2,1,0:T(8,128)(2,1)S(1)}, u32[]{:S(2)}, u32[]{:S(2)}) async-start(bf16[8,8,2176]{2,1,0:T(8,128)(2,1)} %bitcast.116), calls=%async_computation.2 | async-start | bytes 557056 | tf_op jit(solution)/shard_map/all_to_all | solution.py:162
  124.1 2.0 %fusion.20 = bf16[1,256,512]{2,1,0:T(8,128)(2,1)} fusion(bf16[512,512]{1,0:T(8,128)(2,1)} %param.12, bf16[1,256,512]{2,1,0:T(8,128)(2,1)S(1)} %copy-done.3, bf16[32,8,4,128]{3,2,1,0:T(4,128)(2,1)S(1)} %bitcast.115), kind=kOutput, calls=%fused_computation.31 | convolution fusion | flops 134610944 | bytes 1310720 | tf_op jit(solution)/shard_map/dot_general | solution.py:116
  126.1 9.3 %all-to-all-done.2 = bf16[8,8,2176]{2,1,0:T(8,128)(2,1)S(1)} async-done(((bf16[8,8,2176]{2,1,0:T(8,128)(2,1)}), bf16[8,8,2176]{2,1,0:T(8,128)(2,1)S(1)}, u32[]{:S(2)}, u32[]{:S(2)}) %all-to-all-start.2) | async-done | bytes 278560 | tf_op jit(solution)/shard_map/all_to_all | solution.py:162
  136.2 6.1 %all-to-all-start.3 = ((bf16[12,8,768]{2,1,0:T(8,128)(2,1)}), bf16[12,8,768]{2,1,0:T(8,128)(2,1)S(1)}, u32[]{:S(2)}, u32[]{:S(2)}) async-start(bf16[12,8,768]{2,1,0:T(8,128)(2,1)} %pad_maximum_fusion.4), calls=%async_computation.3 | async-start | bytes 294912 | tf_op jit(solution)/shard_map/all_to_all | solution.py:181
  143.3 10.7 %all-to-all-done.3 = bf16[12,8,768]{2,1,0:T(8,128)(2,1)S(1)} async-done(((bf16[12,8,768]{2,1,0:T(8,128)(2,1)}), bf16[12,8,768]{2,1,0:T(8,128)(2,1)S(1)}, u32[]{:S(2)}, u32[]{:S(2)}) %all-to-all-start.3) | async-done | bytes 147488 | tf_op jit(solution)/shard_map/all_to_all | solution.py:181
  (80 shorter events, 32.2 us)
Async XLA Ops:
  0.6 1.5 copy-start
  0.6 19.8 %copy-start.13 = (s32[24,5]{0,1:T(8,128)S(1)}, s32[24,5]{0,1:T(8,128)}, u32[]{:S(2)}) copy-start(s32[24,5]{0,1:T(8,128)} %param.14) | copy-start | bytes 1444
  0.7 19.9 %copy-start.14 = (s32[24]{0:T(128)S(1)}, s32[24]{0:T(128)}, u32[]{:S(2)}) copy-start(s32[24]{0:T(128)} %param.15) | copy-start | bytes 292
  2.1 20.5 %copy-start.6 = (bf16[1,256,512]{2,1,0:T(8,128)(2,1)S(1)}, bf16[1,256,512]{2,1,0:T(8,128)(2,1)}, u32[]{:S(2)}) copy-start(bf16[1,256,512]{2,1,0:T(8,128)(2,1)} %param.10) | copy-start | bytes 786436
  2.1 20.5 %copy-start.9 = (bf16[512,512]{1,0:T(8,128)(2,1)S(1)}, bf16[512,512]{1,0:T(8,128)(2,1)}, u32[]{:S(2)}) copy-start(bf16[512,512]{1,0:T(8,128)(2,1)} %param.12) | copy-start | bytes 1572868
  3.8 25.8 %collective-permute-start.1 = (bf16[256,1024]{1,0:T(8,128)(2,1)S(1)}, bf16[256,1024]{1,0:T(8,128)(2,1)}, u32[]{:S(2)}, u32[]{:S(2)}) collective-permute-start(bf16[256,1024]{1,0:T(8,128)(2,1)S(1)} %slice.65), channel_id=1, source_target_pairs={{64,0},{128,64},{192,128},{256,192},{320,256},{384,320},{448,384},... | collective-permute-start | bytes 1572872 | tf_op jit(solution)/shard_map/ppermute | solution.py:23
  18.4 16.6 %collective-permute-start = (bf16[256,1024]{1,0:T(8,128)(2,1)S(1)}, bf16[256,1024]{1,0:T(8,128)(2,1)}, u32[]{:S(2)}, u32[]{:S(2)}) collective-permute-start(bf16[256,1024]{1,0:T(8,128)(2,1)S(1)} %slice.65), channel_id=1, source_target_pairs={{0,64},{64,128},{128,192},{192,256},{256,320},{320,384},{384,448},... | collective-permute-start | bytes 1572872 | tf_op jit(solution)/shard_map/ppermute | solution.py:20
  22.6 17.6 %copy-start.8 = (bf16[2,128,4,128,1]{1,3,0,4,2:T(8,128)(2,1)}, bf16[2,128,4,128,1]{1,3,0,4,2:T(8,128)(2,1)S(1)}, u32[]{:S(2)}) copy-start(bf16[2,128,4,128,1]{1,3,0,4,2:T(8,128)(2,1)S(1)} %copy.96) | copy-start | bytes 786436
  38.2 2.9 %copy-start.1 = (bf16[6,128,4,128,1]{1,3,0,4,2:T(8,128)(2,1)}, bf16[6,128,4,128,1]{1,3,0,4,2:T(8,128)(2,1)S(1)}, u32[]{:S(2)}) copy-start(bf16[6,128,4,128,1]{1,3,0,4,2:T(8,128)(2,1)S(1)} %copy.93) | copy-start | bytes 2359300
  40.3 1.5 copy-start.4
  41.1 1.0 copy-start.10
  43.1 1.3 copy-start.5
  64.0 8.3 %copy-start.2 = (bf16[6,128,4,128,1]{1,3,0,4,2:T(8,128)(2,1)S(1)}, bf16[6,128,4,128,1]{1,3,0,4,2:T(8,128)(2,1)}, u32[]{:S(2)}) copy-start(bf16[6,128,4,128,1]{1,3,0,4,2:T(8,128)(2,1)} %copy-done.1) | copy-start | bytes 2359300
  65.1 15.9 %collective-permute-start.3 = (bf16[256,1024]{1,0:T(8,128)(2,1)}, bf16[256,1024]{1,0:T(8,128)(2,1)}, u32[]{:S(2)}, u32[]{:S(2)}) collective-permute-start(bf16[256,1024]{1,0:T(8,128)(2,1)} %get-tuple-element.22), channel_id=1, source_target_pairs={{704,0},{0,64},{64,128},{128,192},{192,256},{256,320},{320,384},{3... | collective-permute-start | bytes 1572872 | tf_op jit(solution)/shard_map/ppermute | solution.py:31
  67.0 15.2 %collective-permute-start.2 = (bf16[256,1024]{1,0:T(8,128)(2,1)}, bf16[256,1024]{1,0:T(8,128)(2,1)}, u32[]{:S(2)}, u32[]{:S(2)}) collective-permute-start(bf16[256,1024]{1,0:T(8,128)(2,1)} %get-tuple-element.21), channel_id=1, source_target_pairs={{64,0},{128,64},{192,128},{256,192},{320,256},{384,320},{448,384},... | collective-permute-start | bytes 1572872 | tf_op jit(solution)/shard_map/ppermute | solution.py:31
  74.6 9.4 %copy-start.3 = (bf16[1,256,512]{2,1,0:T(8,128)(2,1)S(1)}, bf16[1,256,512]{2,1,0:T(8,128)(2,1)}, u32[]{:S(2)}) copy-start(bf16[1,256,512]{2,1,0:T(8,128)(2,1)} %param.9) | copy-start | bytes 786436
  74.6 9.4 %copy-start.12 = (f32[512]{0:T(512)S(1)}, f32[512]{0:T(512)}, u32[]{:S(2)}) copy-start(f32[512]{0:T(512)} %param.13) | copy-start | bytes 6148
  116.8 25.6 %copy-start.7 = (bf16[1,256,512]{2,1,0:T(8,128)(2,1)S(1)}, bf16[1,256,512]{2,1,0:T(8,128)(2,1)}, u32[]{:S(2)}) copy-start(bf16[1,256,512]{2,1,0:T(8,128)(2,1)} %param.10) | copy-start | bytes 786436
  116.8 25.6 %copy-start.11 = (f32[256,512]{1,0:T(8,128)S(1)}, f32[256,512]{1,0:T(8,128)}, u32[]{:S(2)}) copy-start(f32[256,512]{1,0:T(8,128)} %get-tuple-element.29) | copy-start | bytes 1572868
  116.8 18.6 %all-to-all-start.2 = ((bf16[8,8,2176]{2,1,0:T(8,128)(2,1)}), bf16[8,8,2176]{2,1,0:T(8,128)(2,1)S(1)}, u32[]{:S(2)}, u32[]{:S(2)}) async-start(bf16[8,8,2176]{2,1,0:T(8,128)(2,1)} %bitcast.116), calls=%async_computation.2 | async-start | bytes 557056 | tf_op jit(solution)/shard_map/all_to_all | solution.py:162
  136.2 17.8 %all-to-all-start.3 = ((bf16[12,8,768]{2,1,0:T(8,128)(2,1)}), bf16[12,8,768]{2,1,0:T(8,128)(2,1)S(1)}, u32[]{:S(2)}, u32[]{:S(2)}) async-start(bf16[12,8,768]{2,1,0:T(8,128)(2,1)} %pad_maximum_fusion.4), calls=%async_computation.3 | async-start | bytes 294912 | tf_op jit(solution)/shard_map/all_to_all | solution.py:181

commit v4 on v3

--- a/solution.py
+++ b/solution.py
@@ -1,6 +1,7 @@
 import jax
 import jax.numpy as jnp
 from jax import lax
+from jax.experimental import pallas as pl
 from jax.sharding import Mesh, PartitionSpec as P
 
 HEADS = 4
@@ -43,54 +44,60 @@
     return jnp.any(matches, axis=1)
 
 
-def attend(queries, window_keys, window_values, allowed):
-    row_count, model_width = queries.shape
-    tile_count, span_tiles = allowed.shape
-    head_dim = model_width // HEADS
+def attention_kernel(mask_ref, q_ref, k_ref, v_ref, ga_ref, att_ref, gq_ref, gk_ref, gv_ref):
+    head_dim = q_ref.shape[1]
     score_scale = head_dim ** (-0.5)
-    query_heads = queries.reshape(tile_count, TILE, HEADS, head_dim)
-    key_heads = window_keys.reshape(span_tiles, TILE, HEADS, head_dim)
-    value_heads = window_values.reshape(span_tiles, TILE, HEADS, head_dim)
-    scores = (
-        jnp.einsum("atnd,bsnd->natbs", query_heads, key_heads, preferred_element_type=jnp.float32)
-        * score_scale
-    )
-    scores = jnp.where(allowed[None, :, None, :, None], scores, MASKED)
-    row_peak = jnp.max(scores, axis=(3, 4), keepdims=True)
-    expanded = jnp.exp(scores - row_peak)
-    probabilities = expanded / jnp.sum(expanded, axis=(3, 4), keepdims=True)
-    rounded = probabilities.astype(jnp.bfloat16)
-    attended = jnp.einsum(
-        "natbs,bsnd->atnd", rounded, value_heads, preferred_element_type=jnp.float32
-    )
-    return (attended.reshape(row_count, model_width).astype(jnp.bfloat16), probabilities, rounded)
-
-
-def attend_back(grad_attended, queries, window_keys, window_values, probabilities, rounded):
-    row_count, model_width = queries.shape
-    tile_count = probabilities.shape[1]
-    span_tiles = probabilities.shape[3]
-    head_dim = model_width // HEADS
-    score_scale = head_dim ** (-0.5)
-    query_heads = queries.reshape(tile_count, TILE, HEADS, head_dim)
-    key_heads = window_keys.reshape(span_tiles, TILE, HEADS, head_dim)
-    value_heads = window_values.reshape(span_tiles, TILE, HEADS, head_dim)
-    grad_heads = grad_attended.reshape(tile_count, TILE, HEADS, head_dim)
-    grad_probs = jnp.einsum(
-        "atnd,bsnd->natbs", grad_heads, value_heads, preferred_element_type=jnp.float32
-    )
-    centre = jnp.sum(grad_probs * probabilities, axis=(3, 4), keepdims=True)
-    grad_scores = (probabilities * (grad_probs - centre) * score_scale).astype(jnp.bfloat16)
-    grad_queries = jnp.einsum(
-        "natbs,bsnd->atnd", grad_scores, key_heads, preferred_element_type=jnp.float32
-    ).reshape(row_count, model_width)
-    grad_keys = jnp.einsum(
-        "natbs,atnd->bsnd", grad_scores, query_heads, preferred_element_type=jnp.float32
-    ).reshape(span_tiles * TILE, model_width)
-    grad_values = jnp.einsum(
-        "natbs,atnd->bsnd", rounded, grad_heads, preferred_element_type=jnp.float32
-    ).reshape(span_tiles * TILE, model_width)
-    return (grad_queries, jnp.concatenate([grad_keys, grad_values], axis=1))
+    keys = k_ref[...]
+    values = v_ref[...]
+    nt = (((1,), (1,)), ((), ()))
+    tn = (((0,), (0,)), ((), ()))
+    grad_keys = jnp.zeros(gk_ref.shape, jnp.float32)
+    grad_values = jnp.zeros(gv_ref.shape, jnp.float32)
+    for tile in range(q_ref.shape[0] // TILE):
+        rows = slice(tile * TILE, (tile + 1) * TILE)
+        queries = q_ref[rows, :]
+        grads = ga_ref[rows, :]
+        keep = mask_ref[tile : tile + 1, :] > 0.5
+        scores = lax.dot_general(queries, keys, nt, preferred_element_type=jnp.float32) * score_scale
+        scores = jnp.where(keep, scores, MASKED)
+        peak = jnp.max(scores, axis=1, keepdims=True)
+        expanded = jnp.exp(scores - peak)
+        probabilities = expanded / jnp.sum(expanded, axis=1, keepdims=True)
+        rounded = probabilities.astype(jnp.bfloat16)
+        att_ref[rows, :] = jnp.dot(rounded, values, preferred_element_type=jnp.float32).astype(att_ref.dtype)
+        grad_probs = lax.dot_general(grads, values, nt, preferred_element_type=jnp.float32)
+        centre = jnp.sum(grad_probs * probabilities, axis=1, keepdims=True)
+        grad_scores = (probabilities * (grad_probs - centre) * score_scale).astype(jnp.bfloat16)
+        gq_ref[rows, :] = jnp.dot(grad_scores, keys, preferred_element_type=jnp.float32)
+        grad_keys = grad_keys + lax.dot_general(grad_scores, queries, tn, preferred_element_type=jnp.float32)
+        grad_values = grad_values + lax.dot_general(rounded, grads, tn, preferred_element_type=jnp.float32)
+    gk_ref[...] = grad_keys
+    gv_ref[...] = grad_values
+
+
+def fused_attention(keep_rows, queries, window_keys, window_values, grad_attended, heads):
+    rows, width = queries.shape
+    span = window_keys.shape[0]
+    head_dim = width // heads
+    q_spec = pl.BlockSpec((rows, head_dim), lambda h: (0, h))
+    w_spec = pl.BlockSpec((span, head_dim), lambda h: (0, h))
+    m_spec = pl.BlockSpec(keep_rows.shape, lambda h: (0, 0))
+    flops = 12 * rows * span * width
+    cost = pl.CostEstimate(flops=flops, transcendentals=rows * span * heads,
+                           bytes_accessed=2 * (2 * rows * width + 2 * span * width) + 4 * (rows * width + 2 * span * width) + 2 * rows * width)
+    return pl.pallas_call(
+        attention_kernel,
+        grid=(heads,),
+        in_specs=[m_spec, q_spec, w_spec, w_spec, q_spec],
+        out_specs=[q_spec, q_spec, w_spec, w_spec],
+        out_shape=[
+            jax.ShapeDtypeStruct((rows, width), jnp.bfloat16),
+            jax.ShapeDtypeStruct((rows, width), jnp.float32),
+            jax.ShapeDtypeStruct((span, width), jnp.float32),
+            jax.ShapeDtypeStruct((span, width), jnp.float32),
+        ],
+        cost_estimate=cost,
+    )(keep_rows, queries, window_keys, window_values, grad_attended)
 
 
 def on_device(tokens, cotangent, w_qkv, w_out, norm_gain, tile_lists, tile_counts):
@@ -112,20 +119,22 @@
     window = extended(projected[:, model_width:], (("node", 0),), row_count)
     window_keys = window[:, :model_width]
     window_values = window[:, model_width:]
-    attended, probabilities, rounded = attend(queries, window_keys, window_values, allowed)
-    outputs = (widened + jnp.dot(attended, w_out, preferred_element_type=jnp.float32)).astype(
-        jnp.bfloat16
-    )
     contract_rows = (((0,), (0,)), ((), ()))
     contract_cols = (((1,), (1,)), ((), ()))
-    term_out = lax.dot_general(
-        attended, own_grads, contract_rows, preferred_element_type=jnp.float32
-    )
     grad_attended = lax.dot_general(
         own_grads, w_out, contract_cols, preferred_element_type=jnp.float32
     ).astype(jnp.bfloat16)
-    grad_queries, grad_window = attend_back(
-        grad_attended, queries, window_keys, window_values, probabilities, rounded
+    keep_rows = jnp.zeros((8, window_keys.shape[0]), jnp.float32)
+    keep_rows = keep_rows.at[:tile_count].set(jnp.repeat(allowed, TILE, axis=1).astype(jnp.float32))
+    attended, grad_queries, grad_keys, grad_values = fused_attention(
+        keep_rows, queries, window_keys, window_values, grad_attended, HEADS
+    )
+    grad_window = jnp.concatenate([grad_keys, grad_values], axis=1)
+    outputs = (widened + jnp.dot(attended, w_out, preferred_element_type=jnp.float32)).astype(
+        jnp.bfloat16
+    )
+    term_out = lax.dot_general(
+        attended, own_grads, contract_rows, preferred_element_type=jnp.float32
     )
     grad_keyvals = grad_window[row_count : 2 * row_count]
     for offset, side_index in ((-1, 0), (1, 2)):

time: 158 us -> 140 us (0.89)
  local copies, waits for them, and re-layouts: 24.7 us -> 8.32 us
  matrix products: 16.8 us -> 7.19 us
  Pallas kernels: 0 us -> 9.4 us
  waiting for transfers between devices: 34.9 us -> 41.3 us
  other arithmetic: 16 us -> 10.8 us
  starting transfers between devices: 37.1 us -> 35.3 us
    pallas_call x0 -> x1, Pallas kernels: none -> 9.4 us  [fused_attention(): pl.pallas_call(attention_kernel, grid=(heads,), in_specs=[m_spec, q_spec,...]
    dot_general x6 -> x0, matrix products: 8.64 us -> none  [the longest x1 2.75 us: attend_back(): jnp.einsum('natbs,atnd->bsnd', grad_scores, query_heads, preferred_elemen...]
    reshape x7 -> x0, local copies, waits for them, and re-layouts: 6.66 us -> none  [the longest x1 2.03 us: attend(): value_heads = window_values.reshape(span_tiles, TILE, HEADS, head_dim)]
    ppermute x2, waiting for transfers between devices: 6.22 us -> 12.7 us  [passed_along(): return lax.ppermute(block, axis, route)]
    transpose x3 -> x0, local copies, waits for them, and re-layouts: 6.39 us -> none  [the longest x1 2.63 us: attend_back(): jnp.einsum('natbs,atnd->bsnd', rounded, grad_heads, preferred_element_typ...]
    another operation x4 -> x5, other arithmetic: 5.17 us -> 1.84 us
    concatenate x1, local copies, waits for them, and re-layouts: 2.72 us -> 0.12 us  [on_device(): grad_window = jnp.concatenate([grad_keys, grad_values], axis=1)]
    ppermute x1, starting transfers between devices: 14.6 us -> 12.2 us  [extended(): lax.ppermute(lax.slice_in_dim(block, 0, width, axis=dim), axis, backward)]
  transfers between devices with their start and end apart: 6 -> 6, of which waited for: 6 -> 6; matrix products, arithmetic and copies ran while one was open for 8% -> 5% of each run, Pallas kernels for 0% -> 0%
where the time goes in v4:
time: 140 us; the launch traced here: 138 us
  waiting for transfers between devices  41.3 us (30%)
  starting transfers between devices  35.3 us (25%)
  blocking collectives  25.2 us (18%)
  other arithmetic  10.8 us (8%)
  Pallas kernels  9.4 us (7%)
  local copies, waits for them, and re-layouts  8.32 us (6%)
  matrix products  7.19 us (5%)
    all_to_all x2, blocking collectives, exchange_sum(): lax.all_to_all(pieces.astype(jnp.bfloat16), axis, 0, 0, tiled=False)  25.2 us
    ppermute x2, waiting for transfers between devices, passed_along(): return lax.ppermute(block, axis, route)  12.7 us
    ppermute x1, starting transfers between devices, extended(): lax.ppermute(lax.slice_in_dim(block, 0, width, axis=dim), axis, backward)  12.2 us
    all_to_all x1, waiting for transfers between devices, reduce_terms(): lax.all_to_all(mixed.astype(jnp.bfloat16), 'node', 0, 0, tiled=False)  10.7 us
    pallas_call x1, Pallas kernels, fused_attention(): pl.pallas_call(attention_kernel, grid=(heads,), in_specs=[m_spec, q_spec,...  9.4 us
    all_to_all x1, waiting for transfers between devices, exchange_sum(): lax.all_to_all(pieces.astype(jnp.bfloat16), axis, 0, 0, tiled=False)  9.34 us
    ppermute x2, starting transfers between devices, passed_along(): return lax.ppermute(block, axis, route)  7.64 us
    ppermute x1, waiting for transfers between devices, extended(): lax.ppermute(lax.slice_in_dim(block, block.shape[dim] - width, None, axis...  7.4 us
  transfers between devices with their start and end apart: 6, of which 6 were waited for; matrix products, arithmetic and copies ran while one was open for 5% of the time, Pallas kernels for 0%

profile of v4, /device:TPU:6, one launch (start us, length us, event | category | flops | bytes accessed | tf_op | source)
XLA Modules:
  0.0 138.5 jit_solution(1372951348754343507)
XLA Ops:
  0.6 1.2 fusion.17
  2.1 1.6 %convolution_convert_fusion.1 = bf16[256,1536]{1,0:T(8,128)(2,1)S(1)} fusion(bf16[512,1536]{1,0:T(8,128)(2,1)S(1)} %copy-done, bf16[1,256,512]{2,1,0:T(8,128)(2,1)} %param.11, f32[512]{0:T(512)} %param.15, f32[256]{0:T(256)S(1)} %add_rsqrt_fusion), kind=kOutput, calls=%fused_computation.3 | convolution fusion | flops 403570688 | bytes 2624512 | tf_op jit(solution)/shard_map/dot_general | solution.py:117
  4.6 4.3 %collective-permute-start = (bf16[256,1024]{1,0:T(8,128)(2,1)}, bf16[256,1024]{1,0:T(8,128)(2,1)}, u32[]{:S(2)}, u32[]{:S(2)}) collective-permute-start(bf16[256,1024]{1,0:T(8,128)(2,1)} %slice.82), channel_id=1, source_target_pairs={{0,64},{64,128},{128,192},{192,256},{256,320},{320,384},{384,448},... | collective-permute-start | bytes 1572872 | tf_op jit(solution)/shard_map/ppermute | solution.py:21
  8.9 12.2 %collective-permute-start.1 = (bf16[256,1024]{1,0:T(8,128)(2,1)}, bf16[256,1024]{1,0:T(8,128)(2,1)}, u32[]{:S(2)}, u32[]{:S(2)}) collective-permute-start(bf16[256,1024]{1,0:T(8,128)(2,1)} %slice.82), channel_id=1, source_target_pairs={{64,0},{128,64},{192,128},{256,192},{320,256},{384,320},{448,384},... | collective-permute-start | bytes 1572872 | tf_op jit(solution)/shard_map/ppermute | solution.py:24
  23.0 1.0 convolution_convert_fusion.3.ga_ref
  24.1 7.4 %collective-permute-done = bf16[256,1024]{1,0:T(8,128)(2,1)} collective-permute-done((bf16[256,1024]{1,0:T(8,128)(2,1)}, bf16[256,1024]{1,0:T(8,128)(2,1)}, u32[]{:S(2)}, u32[]{:S(2)}) %collective-permute-start) | collective-permute-done | bytes 524320 | tf_op jit(solution)/shard_map/ppermute | solution.py:21
  31.5 1.2 collective-permute-done.1
  32.6 1.5 %pad_maximum_fusion = bf16[768,1024]{1,0:T(8,128)(2,1)S(1)} fusion(bf16[256,1024]{1,0:T(8,128)(2,1)} %collective-permute-done.1, bf16[256,1024]{1,0:T(8,128)(2,1)} %slice.82, bf16[256,1024]{1,0:T(8,128)(2,1)} %collective-permute-done), kind=kLoop, calls=%fused_computation.5 | loop fusion | flops 4718592 | bytes 3145728 | tf_op jit(solution)/shard_map/concatenate | solution.py:25
  34.1 1.3 fusion.30
  35.4 9.4 %shard_map.110 = (bf16[256,512]{1,0:T(8,128)(2,1)}, f32[256,512]{1,0:T(8,128)}, f32[768,512]{1,0:T(8,128)}, f32[768,512]{1,0:T(8,128)}) custom-call(f32[8,768]{1,0:T(8,128)} %scatter.6.mask_ref, bf16[256,512]{1,0:T(8,128)(2,1)} %slice.81.q_ref, bf16[768,512]{1,0:T(8,128)(2,1)} %get-tuple-element.42.k_ref, bf16[768,512]{1,0:T(8,128)(2,1)} %get-tuple-element.41.v_ref, ...), custom_call_target="tpu_custom_call" | custom-call | flops 1207959552 | bytes 6029312 | tf_op jit(solution)/shard_map/pallas_call | solution.py:88
  44.8 1.6 %constant_dynamic-update-slice_fusion.1 = f32[768,1024]{1,0:T(8,128)S(1)} fusion(f32[768,512]{1,0:T(8,128)} %get-tuple-element.35), kind=kLoop, calls=%fused_computation.44 | loop fusion | bytes 3145728
  47.1 5.7 %collective-permute-start.2 = (bf16[256,1024]{1,0:T(8,128)(2,1)S(1)}, bf16[256,1024]{1,0:T(8,128)(2,1)S(1)}, u32[]{:S(2)}, u32[]{:S(2)}) collective-permute-start(bf16[256,1024]{1,0:T(8,128)(2,1)S(1)} %get-tuple-element.39), channel_id=1, source_target_pairs={{64,0},{128,64},{192,128},{256,192},{320,256},{384,320},{448,384},... | collective-permute-start | bytes 1572872 | tf_op jit(solution)/shard_map/ppermute | solution.py:32
  52.9 1.9 %collective-permute-start.3 = (bf16[256,1024]{1,0:T(8,128)(2,1)S(1)}, bf16[256,1024]{1,0:T(8,128)(2,1)S(1)}, u32[]{:S(2)}, u32[]{:S(2)}) collective-permute-start(bf16[256,1024]{1,0:T(8,128)(2,1)S(1)} %get-tuple-element.40), channel_id=1, source_target_pairs={{704,0},{0,64},{64,128},{128,192},{192,256},{256,320},{320,384},{3... | collective-permute-start | bytes 1572872 | tf_op jit(solution)/shard_map/ppermute | solution.py:32
  55.8 7.4 %collective-permute-done.2 = bf16[256,1024]{1,0:T(8,128)(2,1)S(1)} collective-permute-done((bf16[256,1024]{1,0:T(8,128)(2,1)S(1)}, bf16[256,1024]{1,0:T(8,128)(2,1)S(1)}, u32[]{:S(2)}, u32[]{:S(2)}) %collective-permute-start.2) | collective-permute-done | bytes 524320 | tf_op jit(solution)/shard_map/ppermute | solution.py:32
  63.2 5.3 %collective-permute-done.3 = bf16[256,1024]{1,0:T(8,128)(2,1)S(1)} collective-permute-done((bf16[256,1024]{1,0:T(8,128)(2,1)S(1)}, bf16[256,1024]{1,0:T(8,128)(2,1)S(1)}, u32[]{:S(2)}, u32[]{:S(2)}) %collective-permute-start.3) | collective-permute-done | bytes 524320 | tf_op jit(solution)/shard_map/ppermute | solution.py:32
  69.5 1.4 %fusion.16 = (bf16[512]{0:T(512)(128)(2,1)S(1)}, f32[256]{0:T(256)S(1)}, f32[256,512]{1,0:T(8,128)}) fusion(bf16[1,256,512]{2,1,0:T(8,128)(2,1)S(1)} %copy-done.1, f32[256]{0:T(256)S(1)} %add_rsqrt_fusion, f32[512]{0:T(512)S(1)} %copy-done.8, bf16[512,1536]{1,0:T(8,128)(2,1)S(1)} %copy-done, bf16[256,1024]{1,0:T(8,128)(2,1)S(1)} %fusion.5, ...), kind=kOutput, calls=%fused_computation.28 | convolution fusion | flops 405142784 | bytes 3150848 | tf_op jit(solution)/shard_map/dot_general | solution.py:149
  72.2 6.4 %all_to_all.20 = bf16[2,256,2176]{2,1,0:T(8,128)(2,1)} all-to-all(bf16[2,256,2176]{2,1,0:T(8,128)(2,1)S(1)} %bitcast.42), channel_id=1, replica_groups=mesh['node'=12,'y'=8,'x'=4,'core'=2] {'core'}, dimensions={0} | all-to-all | bytes 4456448 | tf_op jit(solution)/shard_map/all_to_all | solution.py:171
  78.6 3.3 %reduce_sum.72 = bf16[256,2176]{1,0:T(8,128)(2,1)} reduce(bf16[2,256,2176]{2,1,0:T(8,128)(2,1)} %all_to_all.20, bf16[]{:T(256)} %constant.91.clone.1), dimensions={0}, to_apply=%region_5.6 | reduce | flops 557056 | bytes 3342338 | tf_op jit(solution)/shard_map/reduce_sum | solution.py:175
  81.9 18.8 %all_to_all.21 = bf16[4,64,2176]{2,1,0:T(8,128)(2,1)S(1)} all-to-all(bf16[4,64,2176]{2,1,0:T(8,128)(2,1)} %bitcast.43), channel_id=1, replica_groups=mesh['node'=12,'y'=8,'x'=4,'core'=2] {'x'}, dimensions={0} | all-to-all | bytes 2228224 | tf_op jit(solution)/shard_map/all_to_all | solution.py:171
  101.6 7.2 %all-to-all-start.2 = ((bf16[8,8,2176]{2,1,0:T(8,128)(2,1)}), bf16[8,8,2176]{2,1,0:T(8,128)(2,1)S(1)}, u32[]{:S(2)}, u32[]{:S(2)}) async-start(bf16[8,8,2176]{2,1,0:T(8,128)(2,1)} %bitcast.9), calls=%async_computation.2 | async-start | bytes 557056 | tf_op jit(solution)/shard_map/all_to_all | solution.py:171
  108.9 2.0 %fusion.3 = bf16[1,256,512]{2,1,0:T(8,128)(2,1)} fusion(bf16[256,512]{1,0:T(8,128)(2,1)S(1)} %copy-done.5, bf16[512,512]{1,0:T(8,128)(2,1)} %param.14, bf16[1,256,512]{2,1,0:T(8,128)(2,1)S(1)} %copy-done.1), kind=kOutput, calls=%fused_computation.10 | convolution fusion | flops 134610944 | bytes 1310720 | tf_op jit(solution)/shard_map/dot_general | solution.py:133
  110.9 9.3 %all-to-all-done.2 = bf16[8,8,2176]{2,1,0:T(8,128)(2,1)S(1)} async-done(((bf16[8,8,2176]{2,1,0:T(8,128)(2,1)}), bf16[8,8,2176]{2,1,0:T(8,128)(2,1)S(1)}, u32[]{:S(2)}, u32[]{:S(2)}) %all-to-all-start.2) | async-done | bytes 278560 | tf_op jit(solution)/shard_map/all_to_all | solution.py:171
  121.0 3.9 %all-to-all-start.3 = ((bf16[12,8,768]{2,1,0:T(8,128)(2,1)}), bf16[12,8,768]{2,1,0:T(8,128)(2,1)S(1)}, u32[]{:S(2)}, u32[]{:S(2)}) async-start(bf16[12,8,768]{2,1,0:T(8,128)(2,1)} %pad_maximum_fusion.4), calls=%async_computation.3 | async-start | bytes 294912 | tf_op jit(solution)/shard_map/all_to_all | solution.py:190
  125.9 10.7 %all-to-all-done.3 = bf16[12,8,768]{2,1,0:T(8,128)(2,1)S(1)} async-done(((bf16[12,8,768]{2,1,0:T(8,128)(2,1)}), bf16[12,8,768]{2,1,0:T(8,128)(2,1)S(1)}, u32[]{:S(2)}, u32[]{:S(2)}) %all-to-all-start.3) | async-done | bytes 147488 | tf_op jit(solution)/shard_map/all_to_all | solution.py:190
  (58 shorter events, 11.3 us)
Async XLA Ops:
  0.6 1.5 %copy-start = (bf16[512,1536]{1,0:T(8,128)(2,1)S(1)}, bf16[512,1536]{1,0:T(8,128)(2,1)}, u32[]{:S(2)}) copy-start(bf16[512,1536]{1,0:T(8,128)(2,1)} %param.13) | copy-start | bytes 4718596
  2.1 19.0 %copy-start.9 = (s32[24,5]{0,1:T(8,128)S(1)}, s32[24,5]{0,1:T(8,128)}, u32[]{:S(2)}) copy-start(s32[24,5]{0,1:T(8,128)} %param.16) | copy-start | bytes 1444
  2.1 19.2 %copy-start.10 = (s32[24]{0:T(128)S(1)}, s32[24]{0:T(128)}, u32[]{:S(2)}) copy-start(s32[24]{0:T(128)} %param.17) | copy-start | bytes 292
  2.1 20.9 %copy-start.2 = (bf16[1,256,512]{2,1,0:T(8,128)(2,1)S(1)}, bf16[1,256,512]{2,1,0:T(8,128)(2,1)}, u32[]{:S(2)}) copy-start(bf16[1,256,512]{2,1,0:T(8,128)(2,1)} %param.12) | copy-start | bytes 786436
  2.1 20.9 %copy-start.3 = (bf16[512,512]{1,0:T(8,128)(2,1)S(1)}, bf16[512,512]{1,0:T(8,128)(2,1)}, u32[]{:S(2)}) copy-start(bf16[512,512]{1,0:T(8,128)(2,1)} %param.14) | copy-start | bytes 1572868
  4.6 26.8 %collective-permute-start = (bf16[256,1024]{1,0:T(8,128)(2,1)}, bf16[256,1024]{1,0:T(8,128)(2,1)}, u32[]{:S(2)}, u32[]{:S(2)}) collective-permute-start(bf16[256,1024]{1,0:T(8,128)(2,1)} %slice.82), channel_id=1, source_target_pairs={{0,64},{64,128},{128,192},{192,256},{256,320},{320,384},{384,448},... | collective-permute-start | bytes 1572872 | tf_op jit(solution)/shard_map/ppermute | solution.py:21
  8.9 23.7 %collective-permute-start.1 = (bf16[256,1024]{1,0:T(8,128)(2,1)}, bf16[256,1024]{1,0:T(8,128)(2,1)}, u32[]{:S(2)}, u32[]{:S(2)}) collective-permute-start(bf16[256,1024]{1,0:T(8,128)(2,1)} %slice.82), channel_id=1, source_target_pairs={{64,0},{128,64},{192,128},{256,192},{320,256},{384,320},{448,384},... | collective-permute-start | bytes 1572872 | tf_op jit(solution)/shard_map/ppermute | solution.py:24
  44.8 1.9 %copy-start.4 = (f32[768,512]{1,0:T(8,128)S(1)}, f32[768,512]{1,0:T(8,128)}, u32[]{:S(2)}) copy-start(f32[768,512]{1,0:T(8,128)} %get-tuple-element.36) | copy-start | bytes 4718596
  47.0 8.4 %copy-start.6 = (f32[256,512]{1,0:T(8,128)S(1)}, f32[256,512]{1,0:T(8,128)}, u32[]{:S(2)}) copy-start(f32[256,512]{1,0:T(8,128)} %get-tuple-element.34) | copy-start | bytes 1572868
  47.0 8.4 %copy-start.5 = (bf16[256,512]{1,0:T(8,128)(2,1)S(1)}, bf16[256,512]{1,0:T(8,128)(2,1)}, u32[]{:S(2)}) copy-start(bf16[256,512]{1,0:T(8,128)(2,1)} %get-tuple-element.33) | copy-start | bytes 786436
  47.1 16.0 %collective-permute-start.2 = (bf16[256,1024]{1,0:T(8,128)(2,1)S(1)}, bf16[256,1024]{1,0:T(8,128)(2,1)S(1)}, u32[]{:S(2)}, u32[]{:S(2)}) collective-permute-start(bf16[256,1024]{1,0:T(8,128)(2,1)S(1)} %get-tuple-element.39), channel_id=1, source_target_pairs={{64,0},{128,64},{192,128},{256,192},{320,256},{384,320},{448,384},... | collective-permute-start | bytes 1572872 | tf_op jit(solution)/shard_map/ppermute | solution.py:32
  52.9 15.7 %collective-permute-start.3 = (bf16[256,1024]{1,0:T(8,128)(2,1)S(1)}, bf16[256,1024]{1,0:T(8,128)(2,1)S(1)}, u32[]{:S(2)}, u32[]{:S(2)}) collective-permute-start(bf16[256,1024]{1,0:T(8,128)(2,1)S(1)} %get-tuple-element.40), channel_id=1, source_target_pairs={{704,0},{0,64},{64,128},{128,192},{192,256},{256,320},{320,384},{3... | collective-permute-start | bytes 1572872 | tf_op jit(solution)/shard_map/ppermute | solution.py:32
  55.8 13.0 %copy-start.1 = (bf16[1,256,512]{2,1,0:T(8,128)(2,1)S(1)}, bf16[1,256,512]{2,1,0:T(8,128)(2,1)}, u32[]{:S(2)}) copy-start(bf16[1,256,512]{2,1,0:T(8,128)(2,1)} %param.11) | copy-start | bytes 786436
  55.8 13.0 %copy-start.8 = (f32[512]{0:T(512)S(1)}, f32[512]{0:T(512)}, u32[]{:S(2)}) copy-start(f32[512]{0:T(512)} %param.15) | copy-start | bytes 6148
  101.6 23.4 %copy-start.7 = (f32[256,512]{1,0:T(8,128)S(1)}, f32[256,512]{1,0:T(8,128)}, u32[]{:S(2)}) copy-start(f32[256,512]{1,0:T(8,128)} %get-tuple-element.43) | copy-start | bytes 1572868
  101.6 18.6 %all-to-all-start.2 = ((bf16[8,8,2176]{2,1,0:T(8,128)(2,1)}), bf16[8,8,2176]{2,1,0:T(8,128)(2,1)S(1)}, u32[]{:S(2)}, u32[]{:S(2)}) async-start(bf16[8,8,2176]{2,1,0:T(8,128)(2,1)} %bitcast.9), calls=%async_computation.2 | async-start | bytes 557056 | tf_op jit(solution)/shard_map/all_to_all | solution.py:171
  121.0 15.6 %all-to-all-start.3 = ((bf16[12,8,768]{2,1,0:T(8,128)(2,1)}), bf16[12,8,768]{2,1,0:T(8,128)(2,1)S(1)}, u32[]{:S(2)}, u32[]{:S(2)}) async-start(bf16[12,8,768]{2,1,0:T(8,128)(2,1)} %pad_maximum_fusion.4), calls=%async_computation.3 | async-start | bytes 294912 | tf_op jit(solution)/shard_map/all_to_all | solution.py:190

commit v5 on v4

--- a/solution.py
+++ b/solution.py
@@ -136,18 +136,21 @@
     term_out = lax.dot_general(
         attended, own_grads, contract_rows, preferred_element_type=jnp.float32
     )
+    grad_q = grad_queries.astype(jnp.bfloat16)
+    term_q = lax.dot_general(normed, grad_q, contract_rows, preferred_element_type=jnp.float32)
+    early = section_sum(jnp.concatenate([term_q, term_out], axis=1))
     grad_keyvals = grad_window[row_count : 2 * row_count]
     for offset, side_index in ((-1, 0), (1, 2)):
         side_part = grad_window[side_index * row_count : (side_index + 1) * row_count]
         grad_keyvals = grad_keyvals + passed_along(
             side_part.astype(jnp.bfloat16), "node", offset
         ).astype(side_part.dtype)
-    grad_projected = jnp.concatenate([grad_queries, grad_keyvals], axis=1).astype(jnp.bfloat16)
-    term_qkv = lax.dot_general(
-        normed, grad_projected, contract_rows, preferred_element_type=jnp.float32
-    )
+    grad_kv = grad_keyvals.astype(jnp.bfloat16)
+    term_kv = lax.dot_general(normed, grad_kv, contract_rows, preferred_element_type=jnp.float32)
     grad_normed = lax.dot_general(
-        grad_projected, w_qkv, contract_cols, preferred_element_type=jnp.float32
+        grad_q, w_qkv[:, :model_width], contract_cols, preferred_element_type=jnp.float32
+    ) + lax.dot_general(
+        grad_kv, w_qkv[:, model_width:], contract_cols, preferred_element_type=jnp.float32
     )
     term_gain = jnp.sum(grad_normed * unit_rows, axis=0)
     grad_unit = grad_normed * norm_gain
@@ -155,7 +158,9 @@
     grad_tokens = (
         own_grads.astype(jnp.float32) + inverse_rms * (grad_unit - unit_rows * inner_mean)
     ).astype(jnp.bfloat16)
-    return (outputs[None], grad_tokens[None]) + reduce_terms(term_qkv, term_out, term_gain)
+    gain_block = jnp.zeros((model_width, 128), jnp.float32).at[:, 0].set(term_gain)
+    late = section_sum(jnp.concatenate([term_kv, gain_block], axis=1))
+    return (outputs[None], grad_tokens[None]) + node_sum(early, late, model_width)
 
 
 def section_order(rows):
@@ -175,20 +180,23 @@
     return jnp.sum(pieces.astype(jnp.float32), axis=0)
 
 
-def reduce_terms(term_qkv, term_out, term_gain):
-    rows, model_width = term_out.shape
-    gain_block = jnp.zeros((rows, 128), jnp.float32).at[:, 0].set(term_gain)
-    joined = section_order(jnp.concatenate([term_qkv, term_out, gain_block], axis=1))
+def section_sum(term):
+    joined = section_order(term)
     for axis in ("core", "x", "y"):
         joined = exchange_sum(joined, axis)
+    return joined
+
+
+def node_sum(early, late, model_width):
     node_count = lax.axis_size("node")
-    qkv_width = term_qkv.shape[1]
-    own_rows = joined.shape[0]
-    qkv_blocks = jnp.moveaxis(joined[:, :qkv_width].reshape(own_rows, node_count, -1), 1, 0)
-    shared = jnp.broadcast_to(joined[None, :, qkv_width:], (node_count, own_rows, joined.shape[1] - qkv_width))
+    own_rows = early.shape[0]
+    qkv = jnp.concatenate([early[:, :model_width], late[:, : 2 * model_width]], axis=1)
+    rest = jnp.concatenate([early[:, model_width:], late[:, 2 * model_width :]], axis=1)
+    qkv_blocks = jnp.moveaxis(qkv.reshape(own_rows, node_count, -1), 1, 0)
+    shared = jnp.broadcast_to(rest[None], (node_count,) + rest.shape)
     mixed = jnp.concatenate([qkv_blocks, shared], axis=2)
     summed = wide_sum(lax.all_to_all(mixed.astype(jnp.bfloat16), "node", 0, 0, tiled=False))
-    block_width = qkv_width // node_count
+    block_width = qkv.shape[1] // node_count
     part_qkv = summed[:, :block_width]
     part_out = summed[:, block_width : block_width + model_width]
     part_gain = summed[:, block_width + model_width]

time: 140 us -> 152 us (1.086)
  blocking collectives: 25.2 us -> 9.39 us
  starting transfers between devices: 35.3 us -> 48.7 us
  waiting for transfers between devices: 41.3 us -> 53.6 us
  local copies, waits for them, and re-layouts: 8.32 us -> 10.2 us
    all_to_all x1 -> x4, waiting for transfers between devices: 9.34 us -> 29.8 us  [exchange_sum(): lax.all_to_all(pieces.astype(jnp.bfloat16), axis, 0, 0, tiled=False)]
    all_to_all x2, blocking collectives: 25.2 us -> 9.39 us  [exchange_sum(): lax.all_to_all(pieces.astype(jnp.bfloat16), axis, 0, 0, tiled=False)]
    all_to_all x1 -> x4, starting transfers between devices: 7.24 us -> 20.8 us  [exchange_sum(): lax.all_to_all(pieces.astype(jnp.bfloat16), axis, 0, 0, tiled=False)]
    ppermute x2, waiting for transfers between devices: 12.7 us -> 5.26 us  [passed_along(): return lax.ppermute(block, axis, route)]
    convert_element_type x0 -> x1, other arithmetic: none -> 1.75 us  [on_device(): grad_kv = grad_keyvals.astype(jnp.bfloat16)]
    unnamed x25 -> x29, local copies, waits for them, and re-layouts: 2.27 us -> 3.42 us
    reduce_sum x4 -> x7, other arithmetic: 4.3 us -> 3.85 us  [wide_sum(): return jnp.sum(pieces.astype(jnp.float32), axis=0)]
  transfers between devices with their start and end apart: 6 -> 9, of which waited for: 6 -> 8; matrix products, arithmetic and copies ran while one was open for 5% -> 8% of each run, Pallas kernels for 0% -> 0%
where the time goes in v5:
time: 152 us; the launch traced here: 150 us
  waiting for transfers between devices  53.6 us (35%)
  starting transfers between devices  48.7 us (32%)
  other arithmetic  10.4 us (7%)
  local copies, waits for them, and re-layouts  10.2 us (7%)
  Pallas kernels  9.4 us (6%)
  blocking collectives  9.39 us (6%)
  matrix products  7.48 us (5%)
    all_to_all x4, waiting for transfers between devices, exchange_sum(): lax.all_to_all(pieces.astype(jnp.bfloat16), axis, 0, 0, tiled=False)  29.8 us
    all_to_all x4, starting transfers between devices, exchange_sum(): lax.all_to_all(pieces.astype(jnp.bfloat16), axis, 0, 0, tiled=False)  20.8 us
    ppermute x1, starting transfers between devices, extended(): lax.ppermute(lax.slice_in_dim(block, 0, width, axis=dim), axis, backward)  12.2 us
    all_to_all x1, waiting for transfers between devices, node_sum(): lax.all_to_all(mixed.astype(jnp.bfloat16), 'node', 0, 0, tiled=False)  10.9 us
    pallas_call x1, Pallas kernels, fused_attention(): pl.pallas_call(attention_kernel, grid=(heads,), in_specs=[m_spec, q_spec,...  9.4 us
    all_to_all x2, blocking collectives, exchange_sum(): lax.all_to_all(pieces.astype(jnp.bfloat16), axis, 0, 0, tiled=False)  9.39 us
    ppermute x2, starting transfers between devices, passed_along(): return lax.ppermute(block, axis, route)  7.52 us
    ppermute x1, waiting for transfers between devices, extended(): lax.ppermute(lax.slice_in_dim(block, block.shape[dim] - width, None, axis...  6.43 us
  transfers between devices with their start and end apart: 9, of which 8 were waited for; matrix products, arithmetic and copies ran while one was open for 8% of the time, Pallas kernels for 0%

profile of v5, /device:TPU:6, one launch (start us, length us, event | category | flops | bytes accessed | tf_op | source)
XLA Modules:
  0.0 150.3 jit_solution(13276563140848884345)
XLA Ops:
  1.8 2.2 %convolution_convert_fusion = bf16[256,1536]{1,0:T(8,128)(2,1)S(1)} fusion(bf16[512,1536]{1,0:T(8,128)(2,1)} %param.13, bf16[1,256,512]{2,1,0:T(8,128)(2,1)} %param.11, f32[512]{0:T(512)} %param.15, f32[256]{0:T(256)S(1)} %add_rsqrt_fusion), kind=kOutput, calls=%fused_computation | convolution fusion | flops 403570688 | bytes 2624512 | tf_op jit(solution)/shard_map/dot_general | solution.py:117
  4.1 4.3 %collective-permute-start = (bf16[256,1024]{1,0:T(8,128)(2,1)S(1)}, bf16[256,1024]{1,0:T(8,128)(2,1)S(1)}, u32[]{:S(2)}, u32[]{:S(2)}) collective-permute-start(bf16[256,1024]{1,0:T(8,128)(2,1)S(1)} %slice.99), channel_id=1, source_target_pairs={{0,64},{64,128},{128,192},{192,256},{256,320},{320,384},{384,448},... | collective-permute-start | bytes 1572872 | tf_op jit(solution)/shard_map/ppermute | solution.py:21
  8.4 12.2 %collective-permute-start.1 = (bf16[256,1024]{1,0:T(8,128)(2,1)S(1)}, bf16[256,1024]{1,0:T(8,128)(2,1)S(1)}, u32[]{:S(2)}, u32[]{:S(2)}) collective-permute-start(bf16[256,1024]{1,0:T(8,128)(2,1)S(1)} %slice.99), channel_id=1, source_target_pairs={{64,0},{128,64},{192,128},{256,192},{320,256},{384,320},{448,384},... | collective-permute-start | bytes 1572872 | tf_op jit(solution)/shard_map/ppermute | solution.py:24
  24.1 6.4 %collective-permute-done = bf16[256,1024]{1,0:T(8,128)(2,1)S(1)} collective-permute-done((bf16[256,1024]{1,0:T(8,128)(2,1)S(1)}, bf16[256,1024]{1,0:T(8,128)(2,1)S(1)}, u32[]{:S(2)}, u32[]{:S(2)}) %collective-permute-start) | collective-permute-done | bytes 524320 | tf_op jit(solution)/shard_map/ppermute | solution.py:21
  33.1 9.4 %shard_map.110 = (bf16[256,512]{1,0:T(8,128)(2,1)}, f32[256,512]{1,0:T(8,128)}, f32[768,512]{1,0:T(8,128)}, f32[768,512]{1,0:T(8,128)}) custom-call(f32[8,768]{1,0:T(8,128)} %scatter.6.mask_ref, bf16[256,512]{1,0:T(8,128)(2,1)} %slice.98.q_ref, bf16[768,512]{1,0:T(8,128)(2,1)} %get-tuple-element.42.k_ref, bf16[768,512]{1,0:T(8,128)(2,1)} %get-tuple-element.41.v_ref, ...), custom_call_target="tpu_custom_call" | custom-call | flops 1207959552 | bytes 6029312 | tf_op jit(solution)/shard_map/pallas_call | solution.py:88
  42.5 1.6 %constant_dynamic-update-slice_fusion.1 = f32[768,1024]{1,0:T(8,128)S(1)} fusion(f32[768,512]{1,0:T(8,128)} %get-tuple-element.35), kind=kLoop, calls=%fused_computation.52 | loop fusion | bytes 3145728
  44.8 1.4 copy-done.1
  47.3 5.6 %collective-permute-start.2 = (bf16[256,1024]{1,0:T(8,128)(2,1)}, bf16[256,1024]{1,0:T(8,128)(2,1)}, u32[]{:S(2)}, u32[]{:S(2)}) collective-permute-start(bf16[256,1024]{1,0:T(8,128)(2,1)} %get-tuple-element.39), channel_id=1, source_target_pairs={{64,0},{128,64},{192,128},{256,192},{320,256},{384,320},{448,384},... | collective-permute-start | bytes 1572872 | tf_op jit(solution)/shard_map/ppermute | solution.py:32
  52.9 1.9 %collective-permute-start.3 = (bf16[256,1024]{1,0:T(8,128)(2,1)}, bf16[256,1024]{1,0:T(8,128)(2,1)}, u32[]{:S(2)}, u32[]{:S(2)}) collective-permute-start(bf16[256,1024]{1,0:T(8,128)(2,1)} %get-tuple-element.40), channel_id=1, source_target_pairs={{704,0},{0,64},{64,128},{128,192},{192,256},{256,320},{320,384},{3... | collective-permute-start | bytes 1572872 | tf_op jit(solution)/shard_map/ppermute | solution.py:32
  56.4 4.7 %all_to_all.35 = bf16[2,256,1024]{2,1,0:T(8,128)(2,1)S(1)} all-to-all(bf16[2,256,1024]{2,1,0:T(8,128)(2,1)S(1)} %bitcast.52), channel_id=1, replica_groups=mesh['node'=12,'y'=8,'x'=4,'core'=2] {'core'}, dimensions={0} | all-to-all | bytes 2097152 | tf_op jit(solution)/shard_map/all_to_all | solution.py:176
  62.2 1.4 fusion.19
  63.6 5.3 %collective-permute-done.3 = bf16[256,1024]{1,0:T(8,128)(2,1)} collective-permute-done((bf16[256,1024]{1,0:T(8,128)(2,1)}, bf16[256,1024]{1,0:T(8,128)(2,1)}, u32[]{:S(2)}, u32[]{:S(2)}) %collective-permute-start.3) | collective-permute-done | bytes 524320 | tf_op jit(solution)/shard_map/ppermute | solution.py:32
  68.9 1.8 %fusion.5 = bf16[256,1024]{1,0:T(8,128)(2,1)S(1)} fusion(f32[768,1024]{1,0:T(8,128)} %copy-done.1, bf16[256,1024]{1,0:T(8,128)(2,1)} %collective-permute-done.3, bf16[256,1024]{1,0:T(8,128)(2,1)} %collective-permute-done.2), kind=kLoop, calls=%fused_computation.15 | loop fusion | flops 1310720 | bytes 2621440 | tf_op jit(solution)/shard_map/convert_element_type | solution.py:148
  72.8 4.7 %all_to_all.36 = bf16[2,256,1152]{2,1,0:T(8,128)(2,1)S(1)} all-to-all(bf16[2,256,1152]{2,1,0:T(8,128)(2,1)S(1)} %bitcast.50), channel_id=1, replica_groups=mesh['node'=12,'y'=8,'x'=4,'core'=2] {'core'}, dimensions={0} | all-to-all | bytes 2359296 | tf_op jit(solution)/shard_map/all_to_all | solution.py:176
  77.5 4.8 %all-to-all-start.1 = ((bf16[4,64,1024]{2,1,0:T(8,128)(2,1)}), bf16[4,64,1024]{2,1,0:T(8,128)(2,1)S(1)}, u32[]{:S(2)}, u32[]{:S(2)}) async-start(bf16[4,64,1024]{2,1,0:T(8,128)(2,1)} %bitcast.8), calls=%async_computation.1 | async-start | bytes 1048576 | tf_op jit(solution)/shard_map/all_to_all | solution.py:176
  83.4 6.6 %all-to-all-done.1 = bf16[4,64,1024]{2,1,0:T(8,128)(2,1)S(1)} async-done(((bf16[4,64,1024]{2,1,0:T(8,128)(2,1)}), bf16[4,64,1024]{2,1,0:T(8,128)(2,1)S(1)}, u32[]{:S(2)}, u32[]{:S(2)}) %all-to-all-start.1) | async-done | bytes 524320 | tf_op jit(solution)/shard_map/all_to_all | solution.py:176
  90.0 5.5 %all-to-all-start.4 = ((bf16[4,64,1152]{2,1,0:T(8,128)(2,1)}), bf16[4,64,1152]{2,1,0:T(8,128)(2,1)S(1)}, u32[]{:S(2)}, u32[]{:S(2)}) async-start(bf16[4,64,1152]{2,1,0:T(8,128)(2,1)} %bitcast.13), calls=%async_computation.4 | async-start | bytes 1179648 | tf_op jit(solution)/shard_map/all_to_all | solution.py:176
  96.2 6.8 %all-to-all-done.4 = bf16[4,64,1152]{2,1,0:T(8,128)(2,1)S(1)} async-done(((bf16[4,64,1152]{2,1,0:T(8,128)(2,1)}), bf16[4,64,1152]{2,1,0:T(8,128)(2,1)S(1)}, u32[]{:S(2)}, u32[]{:S(2)}) %all-to-all-start.4) | async-done | bytes 589856 | tf_op jit(solution)/shard_map/all_to_all | solution.py:176
  103.1 7.1 %all-to-all-start.2 = ((bf16[8,8,1024]{2,1,0:T(8,128)(2,1)}), bf16[8,8,1024]{2,1,0:T(8,128)(2,1)S(1)}, u32[]{:S(2)}, u32[]{:S(2)}) async-start(bf16[8,8,1024]{2,1,0:T(8,128)(2,1)} %bitcast.9), calls=%async_computation.2 | async-start | bytes 262144 | tf_op jit(solution)/shard_map/all_to_all | solution.py:176
  112.0 7.3 %all-to-all-done.2 = bf16[8,8,1024]{2,1,0:T(8,128)(2,1)S(1)} async-done(((bf16[8,8,1024]{2,1,0:T(8,128)(2,1)}), bf16[8,8,1024]{2,1,0:T(8,128)(2,1)S(1)}, u32[]{:S(2)}, u32[]{:S(2)}) %all-to-all-start.2) | async-done | bytes 131104 | tf_op jit(solution)/shard_map/all_to_all | solution.py:176
  119.3 3.4 %all-to-all-start.5 = ((bf16[8,8,1152]{2,1,0:T(8,128)(2,1)}), bf16[8,8,1152]{2,1,0:T(8,128)(2,1)S(1)}, u32[]{:S(2)}, u32[]{:S(2)}) async-start(bf16[8,8,1152]{2,1,0:T(8,128)(2,1)} %bitcast.14), calls=%async_computation.5 | async-start | bytes 294912 | tf_op jit(solution)/shard_map/all_to_all | solution.py:176
  122.7 9.1 %all-to-all-done.5 = bf16[8,8,1152]{2,1,0:T(8,128)(2,1)S(1)} async-done(((bf16[8,8,1152]{2,1,0:T(8,128)(2,1)}), bf16[8,8,1152]{2,1,0:T(8,128)(2,1)S(1)}, u32[]{:S(2)}, u32[]{:S(2)}) %all-to-all-start.5) | async-done | bytes 147488 | tf_op jit(solution)/shard_map/all_to_all | solution.py:176
  132.6 3.9 %all-to-all-start.6 = ((bf16[12,8,768]{2,1,0:T(8,128)(2,1)}), bf16[12,8,768]{2,1,0:T(8,128)(2,1)S(1)}, u32[]{:S(2)}, u32[]{:S(2)}) async-start(bf16[12,8,768]{2,1,0:T(8,128)(2,1)} %pad_maximum_fusion.2), calls=%async_computation.6 | async-start | bytes 294912 | tf_op jit(solution)/shard_map/all_to_all | solution.py:198
  137.4 10.9 %all-to-all-done.6 = bf16[12,8,768]{2,1,0:T(8,128)(2,1)S(1)} async-done(((bf16[12,8,768]{2,1,0:T(8,128)(2,1)}), bf16[12,8,768]{2,1,0:T(8,128)(2,1)S(1)}, u32[]{:S(2)}, u32[]{:S(2)}) %all-to-all-start.6) | async-done | bytes 147488 | tf_op jit(solution)/shard_map/all_to_all | solution.py:198
  (78 shorter events, 20.9 us)
Async XLA Ops:
  0.6 22.5 %copy-start = (bf16[512,512]{1,0:T(8,128)(2,1)S(1)}, bf16[512,512]{1,0:T(8,128)(2,1)}, u32[]{:S(2)}) copy-start(bf16[512,512]{1,0:T(8,128)(2,1)} %param.14) | copy-start | bytes 1572868
  1.8 18.8 %copy-start.11 = (s32[24,5]{0,1:T(8,128)S(1)}, s32[24,5]{0,1:T(8,128)}, u32[]{:S(2)}) copy-start(s32[24,5]{0,1:T(8,128)} %param.16) | copy-start | bytes 1444
  1.8 19.0 %copy-start.12 = (s32[24]{0:T(128)S(1)}, s32[24]{0:T(128)}, u32[]{:S(2)}) copy-start(s32[24]{0:T(128)} %param.17) | copy-start | bytes 292
  1.8 21.3 %copy-start.4 = (bf16[1,256,512]{2,1,0:T(8,128)(2,1)S(1)}, bf16[1,256,512]{2,1,0:T(8,128)(2,1)}, u32[]{:S(2)}) copy-start(bf16[1,256,512]{2,1,0:T(8,128)(2,1)} %param.12) | copy-start | bytes 786436
  4.1 26.5 %collective-permute-start = (bf16[256,1024]{1,0:T(8,128)(2,1)S(1)}, bf16[256,1024]{1,0:T(8,128)(2,1)S(1)}, u32[]{:S(2)}, u32[]{:S(2)}) collective-permute-start(bf16[256,1024]{1,0:T(8,128)(2,1)S(1)} %slice.99), channel_id=1, source_target_pairs={{0,64},{64,128},{128,192},{192,256},{256,320},{320,384},{384,448},... | collective-permute-start | bytes 1572872 | tf_op jit(solution)/shard_map/ppermute | solution.py:21
  8.4 23.4 %collective-permute-start.1 = (bf16[256,1024]{1,0:T(8,128)(2,1)S(1)}, bf16[256,1024]{1,0:T(8,128)(2,1)S(1)}, u32[]{:S(2)}, u32[]{:S(2)}) collective-permute-start(bf16[256,1024]{1,0:T(8,128)(2,1)S(1)} %slice.99), channel_id=1, source_target_pairs={{64,0},{128,64},{192,128},{256,192},{320,256},{384,320},{448,384},... | collective-permute-start | bytes 1572872 | tf_op jit(solution)/shard_map/ppermute | solution.py:24
  42.5 1.9 %copy-start.7 = (f32[768,512]{1,0:T(8,128)S(1)}, f32[768,512]{1,0:T(8,128)}, u32[]{:S(2)}) copy-start(f32[768,512]{1,0:T(8,128)} %get-tuple-element.36) | copy-start | bytes 4718596
  44.5 1.7 %copy-start.1 = (f32[768,1024]{1,0:T(8,128)}, f32[768,1024]{1,0:T(8,128)S(1)}, u32[]{:S(2)}) copy-start(f32[768,1024]{1,0:T(8,128)S(1)} %constant_dynamic-update-slice_fusion) | copy-start | bytes 9437188
  46.2 8.6 %copy-start.2 = (bf16[1,256,512]{2,1,0:T(8,128)(2,1)S(1)}, bf16[1,256,512]{2,1,0:T(8,128)(2,1)}, u32[]{:S(2)}) copy-start(bf16[1,256,512]{2,1,0:T(8,128)(2,1)} %param.11) | copy-start | bytes 786436
  46.2 8.6 %copy-start.6 = (f32[256,512]{1,0:T(8,128)S(1)}, f32[256,512]{1,0:T(8,128)}, u32[]{:S(2)}) copy-start(f32[256,512]{1,0:T(8,128)} %get-tuple-element.34) | copy-start | bytes 1572868
  46.2 8.6 %copy-start.10 = (f32[512]{0:T(512)S(1)}, f32[512]{0:T(512)}, u32[]{:S(2)}) copy-start(f32[512]{0:T(512)} %param.15) | copy-start | bytes 6148
  46.2 9.1 %copy-start.8 = (bf16[256,512]{1,0:T(8,128)(2,1)S(1)}, bf16[256,512]{1,0:T(8,128)(2,1)}, u32[]{:S(2)}) copy-start(bf16[256,512]{1,0:T(8,128)(2,1)} %get-tuple-element.33) | copy-start | bytes 786436
  47.3 16.3 %collective-permute-start.2 = (bf16[256,1024]{1,0:T(8,128)(2,1)}, bf16[256,1024]{1,0:T(8,128)(2,1)}, u32[]{:S(2)}, u32[]{:S(2)}) collective-permute-start(bf16[256,1024]{1,0:T(8,128)(2,1)} %get-tuple-element.39), channel_id=1, source_target_pairs={{64,0},{128,64},{192,128},{256,192},{320,256},{384,320},{448,384},... | collective-permute-start | bytes 1572872 | tf_op jit(solution)/shard_map/ppermute | solution.py:32
  52.9 15.9 %collective-permute-start.3 = (bf16[256,1024]{1,0:T(8,128)(2,1)}, bf16[256,1024]{1,0:T(8,128)(2,1)}, u32[]{:S(2)}, u32[]{:S(2)}) collective-permute-start(bf16[256,1024]{1,0:T(8,128)(2,1)} %get-tuple-element.40), channel_id=1, source_target_pairs={{704,0},{0,64},{64,128},{128,192},{192,256},{256,320},{320,384},{3... | collective-permute-start | bytes 1572872 | tf_op jit(solution)/shard_map/ppermute | solution.py:32
  56.4 5.9 %copy-start.3 = (bf16[512,1536]{1,0:T(8,128)(2,1)S(1)}, bf16[512,1536]{1,0:T(8,128)(2,1)}, u32[]{:S(2)}) copy-start(bf16[512,1536]{1,0:T(8,128)(2,1)} %param.13) | copy-start | bytes 4718596
  77.5 12.5 %all-to-all-start.1 = ((bf16[4,64,1024]{2,1,0:T(8,128)(2,1)}), bf16[4,64,1024]{2,1,0:T(8,128)(2,1)S(1)}, u32[]{:S(2)}, u32[]{:S(2)}) async-start(bf16[4,64,1024]{2,1,0:T(8,128)(2,1)} %bitcast.8), calls=%async_computation.1 | async-start | bytes 1048576 | tf_op jit(solution)/shard_map/all_to_all | solution.py:176
  82.3 27.9 %copy-start.9 = (bf16[256,512]{1,0:T(8,128)(2,1)S(1)}, bf16[256,512]{1,0:T(8,128)(2,1)}, u32[]{:S(2)}) copy-start(bf16[256,512]{1,0:T(8,128)(2,1)} %get-tuple-element.33) | copy-start | bytes 786436
  90.0 13.1 %all-to-all-start.4 = ((bf16[4,64,1152]{2,1,0:T(8,128)(2,1)}), bf16[4,64,1152]{2,1,0:T(8,128)(2,1)S(1)}, u32[]{:S(2)}, u32[]{:S(2)}) async-start(bf16[4,64,1152]{2,1,0:T(8,128)(2,1)} %bitcast.13), calls=%async_computation.4 | async-start | bytes 1179648 | tf_op jit(solution)/shard_map/all_to_all | solution.py:176
  103.1 16.2 %all-to-all-start.2 = ((bf16[8,8,1024]{2,1,0:T(8,128)(2,1)}), bf16[8,8,1024]{2,1,0:T(8,128)(2,1)S(1)}, u32[]{:S(2)}, u32[]{:S(2)}) async-start(bf16[8,8,1024]{2,1,0:T(8,128)(2,1)} %bitcast.9), calls=%async_computation.2 | async-start | bytes 262144 | tf_op jit(solution)/shard_map/all_to_all | solution.py:176
  110.2 26.3 %copy-start.5 = (bf16[1,256,512]{2,1,0:T(8,128)(2,1)S(1)}, bf16[1,256,512]{2,1,0:T(8,128)(2,1)}, u32[]{:S(2)}) copy-start(bf16[1,256,512]{2,1,0:T(8,128)(2,1)} %param.12) | copy-start | bytes 786436
  119.3 12.6 %all-to-all-start.5 = ((bf16[8,8,1152]{2,1,0:T(8,128)(2,1)}), bf16[8,8,1152]{2,1,0:T(8,128)(2,1)S(1)}, u32[]{:S(2)}, u32[]{:S(2)}) async-start(bf16[8,8,1152]{2,1,0:T(8,128)(2,1)} %bitcast.14), calls=%async_computation.5 | async-start | bytes 294912 | tf_op jit(solution)/shard_map/all_to_all | solution.py:176
  132.6 15.8 %all-to-all-start.6 = ((bf16[12,8,768]{2,1,0:T(8,128)(2,1)}), bf16[12,8,768]{2,1,0:T(8,128)(2,1)S(1)}, u32[]{:S(2)}, u32[]{:S(2)}) async-start(bf16[12,8,768]{2,1,0:T(8,128)(2,1)} %pad_maximum_fusion.2), calls=%async_computation.6 | async-start | bytes 294912 | tf_op jit(solution)/shard_map/all_to_all | solution.py:198

commit v6 on v4

--- a/solution.py
+++ b/solution.py
@@ -161,8 +161,8 @@
 def section_order(rows):
     y_size, x_size, core_size = lax.axis_size("y"), lax.axis_size("x"), lax.axis_size("core")
     shape = rows.shape
-    split = rows.reshape((y_size, x_size, core_size, -1) + shape[1:])
-    return jnp.moveaxis(split, (2, 1, 0), (0, 1, 2)).reshape(shape)
+    split = rows.reshape((y_size, x_size * core_size, -1) + shape[1:])
+    return jnp.swapaxes(split, 0, 1).reshape(shape)
 
 
 def exchange_sum(block, axis):
@@ -179,7 +179,7 @@
     rows, model_width = term_out.shape
     gain_block = jnp.zeros((rows, 128), jnp.float32).at[:, 0].set(term_gain)
     joined = section_order(jnp.concatenate([term_qkv, term_out, gain_block], axis=1))
-    for axis in ("core", "x", "y"):
+    for axis in (("x", "core"), "y"):
         joined = exchange_sum(joined, axis)
     node_count = lax.axis_size("node")
     qkv_width = term_qkv.shape[1]

time: 140 us -> 145 us (1.036)
  blocking collectives: 25.2 us -> 31.2 us
    all_to_all x2 -> x1, blocking collectives: 25.2 us -> 31.2 us  [exchange_sum(): lax.all_to_all(pieces.astype(jnp.bfloat16), axis, 0, 0, tiled=False)]
    all_to_all x1, waiting for transfers between devices: 9.34 us -> 11 us  [exchange_sum(): lax.all_to_all(pieces.astype(jnp.bfloat16), axis, 0, 0, tiled=False)]
    reduce_sum x4 -> x3, other arithmetic: 4.3 us -> 2.78 us  [wide_sum(): return jnp.sum(pieces.astype(jnp.float32), axis=0)]
where the time goes in v6:
time: 145 us; the launch traced here: 143 us
  waiting for transfers between devices  41.9 us (29%)
  starting transfers between devices  35.2 us (24%)
  blocking collectives  31.2 us (22%)
  other arithmetic  10.3 us (7%)
  Pallas kernels  9.4 us (6%)
  local copies, waits for them, and re-layouts  8.32 us (6%)
  matrix products  6.13 us (4%)
    all_to_all x1, blocking collectives, exchange_sum(): lax.all_to_all(pieces.astype(jnp.bfloat16), axis, 0, 0, tiled=False)  31.2 us
    ppermute x2, waiting for transfers between devices, passed_along(): return lax.ppermute(block, axis, route)  12.7 us
    ppermute x1, starting transfers between devices, extended(): lax.ppermute(lax.slice_in_dim(block, 0, width, axis=dim), axis, backward)  12.2 us
    all_to_all x1, waiting for transfers between devices, exchange_sum(): lax.all_to_all(pieces.astype(jnp.bfloat16), axis, 0, 0, tiled=False)  11 us
    all_to_all x1, waiting for transfers between devices, reduce_terms(): lax.all_to_all(mixed.astype(jnp.bfloat16), 'node', 0, 0, tiled=False)  9.64 us
    pallas_call x1, Pallas kernels, fused_attention(): pl.pallas_call(attention_kernel, grid=(heads,), in_specs=[m_spec, q_spec,...  9.4 us
    ppermute x2, starting transfers between devices, passed_along(): return lax.ppermute(block, axis, route)  7.64 us
    ppermute x1, waiting for transfers between devices, extended(): lax.ppermute(lax.slice_in_dim(block, block.shape[dim] - width, None, axis...  7.4 us
  transfers between devices with their start and end apart: 6, of which 6 were waited for; matrix products, arithmetic and copies ran while one was open for 5% of the time, Pallas kernels for 0%

profile of v6, /device:TPU:6, one launch (start us, length us, event | category | flops | bytes accessed | tf_op | source)
XLA Modules:
  0.0 143.4 jit_solution(3814349496437972019)
XLA Ops:
  0.6 1.2 fusion.17
  2.1 1.6 %convolution_convert_fusion.1 = bf16[256,1536]{1,0:T(8,128)(2,1)S(1)} fusion(bf16[512,1536]{1,0:T(8,128)(2,1)S(1)} %copy-done, bf16[1,256,512]{2,1,0:T(8,128)(2,1)} %param.11, f32[512]{0:T(512)} %param.15, f32[256]{0:T(256)S(1)} %add_rsqrt_fusion), kind=kOutput, calls=%fused_computation.3 | convolution fusion | flops 403570688 | bytes 2624512 | tf_op jit(solution)/shard_map/dot_general | solution.py:117
  4.6 4.3 %collective-permute-start = (bf16[256,1024]{1,0:T(8,128)(2,1)}, bf16[256,1024]{1,0:T(8,128)(2,1)}, u32[]{:S(2)}, u32[]{:S(2)}) collective-permute-start(bf16[256,1024]{1,0:T(8,128)(2,1)} %slice.82), channel_id=1, source_target_pairs={{0,64},{64,128},{128,192},{192,256},{256,320},{320,384},{384,448},... | collective-permute-start | bytes 1572872 | tf_op jit(solution)/shard_map/ppermute | solution.py:21
  8.9 12.2 %collective-permute-start.1 = (bf16[256,1024]{1,0:T(8,128)(2,1)}, bf16[256,1024]{1,0:T(8,128)(2,1)}, u32[]{:S(2)}, u32[]{:S(2)}) collective-permute-start(bf16[256,1024]{1,0:T(8,128)(2,1)} %slice.82), channel_id=1, source_target_pairs={{64,0},{128,64},{192,128},{256,192},{320,256},{384,320},{448,384},... | collective-permute-start | bytes 1572872 | tf_op jit(solution)/shard_map/ppermute | solution.py:24
  23.0 1.0 convolution_convert_fusion.3.ga_ref
  24.1 7.4 %collective-permute-done = bf16[256,1024]{1,0:T(8,128)(2,1)} collective-permute-done((bf16[256,1024]{1,0:T(8,128)(2,1)}, bf16[256,1024]{1,0:T(8,128)(2,1)}, u32[]{:S(2)}, u32[]{:S(2)}) %collective-permute-start) | collective-permute-done | bytes 524320 | tf_op jit(solution)/shard_map/ppermute | solution.py:21
  31.5 1.2 collective-permute-done.1
  32.6 1.5 %pad_maximum_fusion = bf16[768,1024]{1,0:T(8,128)(2,1)S(1)} fusion(bf16[256,1024]{1,0:T(8,128)(2,1)} %collective-permute-done.1, bf16[256,1024]{1,0:T(8,128)(2,1)} %slice.82, bf16[256,1024]{1,0:T(8,128)(2,1)} %collective-permute-done), kind=kLoop, calls=%fused_computation.6 | loop fusion | flops 4718592 | bytes 3145728 | tf_op jit(solution)/shard_map/concatenate | solution.py:25
  34.1 1.3 fusion.30
  35.4 9.4 %shard_map.110 = (bf16[256,512]{1,0:T(8,128)(2,1)}, f32[256,512]{1,0:T(8,128)}, f32[768,512]{1,0:T(8,128)}, f32[768,512]{1,0:T(8,128)}) custom-call(f32[8,768]{1,0:T(8,128)} %scatter.6.mask_ref, bf16[256,512]{1,0:T(8,128)(2,1)} %slice.81.q_ref, bf16[768,512]{1,0:T(8,128)(2,1)} %get-tuple-element.42.k_ref, bf16[768,512]{1,0:T(8,128)(2,1)} %get-tuple-element.41.v_ref, ...), custom_call_target="tpu_custom_call" | custom-call | flops 1207959552 | bytes 6029312 | tf_op jit(solution)/shard_map/pallas_call | solution.py:88
  44.8 1.6 %constant_dynamic-update-slice_fusion.1 = f32[768,1024]{1,0:T(8,128)S(1)} fusion(f32[768,512]{1,0:T(8,128)} %get-tuple-element.35), kind=kLoop, calls=%fused_computation.45 | loop fusion | bytes 3145728
  47.1 5.7 %collective-permute-start.2 = (bf16[256,1024]{1,0:T(8,128)(2,1)S(1)}, bf16[256,1024]{1,0:T(8,128)(2,1)S(1)}, u32[]{:S(2)}, u32[]{:S(2)}) collective-permute-start(bf16[256,1024]{1,0:T(8,128)(2,1)S(1)} %get-tuple-element.39), channel_id=1, source_target_pairs={{64,0},{128,64},{192,128},{256,192},{320,256},{384,320},{448,384},... | collective-permute-start | bytes 1572872 | tf_op jit(solution)/shard_map/ppermute | solution.py:32
  52.9 1.9 %collective-permute-start.3 = (bf16[256,1024]{1,0:T(8,128)(2,1)S(1)}, bf16[256,1024]{1,0:T(8,128)(2,1)S(1)}, u32[]{:S(2)}, u32[]{:S(2)}) collective-permute-start(bf16[256,1024]{1,0:T(8,128)(2,1)S(1)} %get-tuple-element.40), channel_id=1, source_target_pairs={{704,0},{0,64},{64,128},{128,192},{192,256},{256,320},{320,384},{3... | collective-permute-start | bytes 1572872 | tf_op jit(solution)/shard_map/ppermute | solution.py:32
  55.8 7.4 %collective-permute-done.2 = bf16[256,1024]{1,0:T(8,128)(2,1)S(1)} collective-permute-done((bf16[256,1024]{1,0:T(8,128)(2,1)S(1)}, bf16[256,1024]{1,0:T(8,128)(2,1)S(1)}, u32[]{:S(2)}, u32[]{:S(2)}) %collective-permute-start.2) | collective-permute-done | bytes 524320 | tf_op jit(solution)/shard_map/ppermute | solution.py:32
  63.2 5.3 %collective-permute-done.3 = bf16[256,1024]{1,0:T(8,128)(2,1)S(1)} collective-permute-done((bf16[256,1024]{1,0:T(8,128)(2,1)S(1)}, bf16[256,1024]{1,0:T(8,128)(2,1)S(1)}, u32[]{:S(2)}, u32[]{:S(2)}) %collective-permute-start.3) | collective-permute-done | bytes 524320 | tf_op jit(solution)/shard_map/ppermute | solution.py:32
  69.5 1.4 fusion.16
  72.2 31.2 %all_to_all.15 = bf16[8,64,2176]{2,1,0:T(8,128)(2,1)} all-to-all(bf16[8,64,2176]{2,1,0:T(8,128)(2,1)S(1)} %bitcast.43), channel_id=1, replica_groups=mesh['node'=12,'y'=8,'x'=4,'core'=2] {'x','core'}, dimensions={0} | all-to-all | bytes 4456448 | tf_op jit(solution)/shard_map/all_to_all | solution.py:171
  103.4 2.7 %reduce_sum.60 = bf16[64,2176]{1,0:T(8,128)(2,1)} reduce(bf16[8,64,2176]{2,1,0:T(8,128)(2,1)} %all_to_all.15, bf16[]{:T(256)} %constant.90.clone.1), dimensions={0}, to_apply=%region_5.6 | reduce | flops 974848 | bytes 2506754 | tf_op jit(solution)/shard_map/reduce_sum | solution.py:175
  106.1 7.1 %all-to-all-start.1 = ((bf16[8,8,2176]{2,1,0:T(8,128)(2,1)}), bf16[8,8,2176]{2,1,0:T(8,128)(2,1)S(1)}, u32[]{:S(2)}, u32[]{:S(2)}) async-start(bf16[8,8,2176]{2,1,0:T(8,128)(2,1)} %bitcast.8), calls=%async_computation.1 | async-start | bytes 557056 | tf_op jit(solution)/shard_map/all_to_all | solution.py:171
  113.2 1.0 fusion.3
  114.2 11.0 %all-to-all-done.1 = bf16[8,8,2176]{2,1,0:T(8,128)(2,1)S(1)} async-done(((bf16[8,8,2176]{2,1,0:T(8,128)(2,1)}), bf16[8,8,2176]{2,1,0:T(8,128)(2,1)S(1)}, u32[]{:S(2)}, u32[]{:S(2)}) %all-to-all-start.1) | async-done | bytes 278560 | tf_op jit(solution)/shard_map/all_to_all | solution.py:171
  126.0 3.9 %all-to-all-start.2 = ((bf16[12,8,768]{2,1,0:T(8,128)(2,1)}), bf16[12,8,768]{2,1,0:T(8,128)(2,1)S(1)}, u32[]{:S(2)}, u32[]{:S(2)}) async-start(bf16[12,8,768]{2,1,0:T(8,128)(2,1)} %pad_maximum_fusion.4), calls=%async_computation.2 | async-start | bytes 294912 | tf_op jit(solution)/shard_map/all_to_all | solution.py:190
  130.0 2.0 %fusion.19 = bf16[1,256,512]{2,1,0:T(8,128)(2,1)} fusion(f32[256,512]{1,0:T(8,128)} %get-tuple-element.43, bf16[1,256,512]{2,1,0:T(8,128)(2,1)S(1)} %copy-done.2, bf16[1,256,512]{2,1,0:T(8,128)(2,1)S(1)} %copy-done.1, f32[256]{0:T(256)S(1)} %broadcast_multiply_fusion, f32[512]{0:T(512)S(1)} %copy-done.7, f32[256]{0:T(256)S(1)} %add_rsqrt_fusion), kind=kLoop, calls=%fused_computation.33 | loop fusion | flops 1179648 | bytes 1314816 | tf_op jit(solution)/shard_map/broadcast_in_dim | solution.py:158
  131.9 9.6 %all-to-all-done.2 = bf16[12,8,768]{2,1,0:T(8,128)(2,1)S(1)} async-done(((bf16[12,8,768]{2,1,0:T(8,128)(2,1)}), bf16[12,8,768]{2,1,0:T(8,128)(2,1)S(1)}, u32[]{:S(2)}, u32[]{:S(2)}) %all-to-all-start.2) | async-done | bytes 147488 | tf_op jit(solution)/shard_map/all_to_all | solution.py:190
  (54 shorter events, 9.4 us)
Async XLA Ops:
  0.6 1.5 %copy-start = (bf16[512,1536]{1,0:T(8,128)(2,1)S(1)}, bf16[512,1536]{1,0:T(8,128)(2,1)}, u32[]{:S(2)}) copy-start(bf16[512,1536]{1,0:T(8,128)(2,1)} %param.13) | copy-start | bytes 4718596
  2.1 19.0 %copy-start.8 = (s32[24,5]{0,1:T(8,128)S(1)}, s32[24,5]{0,1:T(8,128)}, u32[]{:S(2)}) copy-start(s32[24,5]{0,1:T(8,128)} %param.16) | copy-start | bytes 1444
  2.1 19.2 %copy-start.9 = (s32[24]{0:T(128)S(1)}, s32[24]{0:T(128)}, u32[]{:S(2)}) copy-start(s32[24]{0:T(128)} %param.17) | copy-start | bytes 292
  2.1 20.9 %copy-start.2 = (bf16[1,256,512]{2,1,0:T(8,128)(2,1)S(1)}, bf16[1,256,512]{2,1,0:T(8,128)(2,1)}, u32[]{:S(2)}) copy-start(bf16[1,256,512]{2,1,0:T(8,128)(2,1)} %param.12) | copy-start | bytes 786436
  2.1 20.9 %copy-start.3 = (bf16[512,512]{1,0:T(8,128)(2,1)S(1)}, bf16[512,512]{1,0:T(8,128)(2,1)}, u32[]{:S(2)}) copy-start(bf16[512,512]{1,0:T(8,128)(2,1)} %param.14) | copy-start | bytes 1572868
  4.6 26.8 %collective-permute-start = (bf16[256,1024]{1,0:T(8,128)(2,1)}, bf16[256,1024]{1,0:T(8,128)(2,1)}, u32[]{:S(2)}, u32[]{:S(2)}) collective-permute-start(bf16[256,1024]{1,0:T(8,128)(2,1)} %slice.82), channel_id=1, source_target_pairs={{0,64},{64,128},{128,192},{192,256},{256,320},{320,384},{384,448},... | collective-permute-start | bytes 1572872 | tf_op jit(solution)/shard_map/ppermute | solution.py:21
  8.9 23.7 %collective-permute-start.1 = (bf16[256,1024]{1,0:T(8,128)(2,1)}, bf16[256,1024]{1,0:T(8,128)(2,1)}, u32[]{:S(2)}, u32[]{:S(2)}) collective-permute-start(bf16[256,1024]{1,0:T(8,128)(2,1)} %slice.82), channel_id=1, source_target_pairs={{64,0},{128,64},{192,128},{256,192},{320,256},{384,320},{448,384},... | collective-permute-start | bytes 1572872 | tf_op jit(solution)/shard_map/ppermute | solution.py:24
  44.8 1.9 %copy-start.4 = (f32[768,512]{1,0:T(8,128)S(1)}, f32[768,512]{1,0:T(8,128)}, u32[]{:S(2)}) copy-start(f32[768,512]{1,0:T(8,128)} %get-tuple-element.36) | copy-start | bytes 4718596
  47.0 8.4 %copy-start.6 = (f32[256,512]{1,0:T(8,128)S(1)}, f32[256,512]{1,0:T(8,128)}, u32[]{:S(2)}) copy-start(f32[256,512]{1,0:T(8,128)} %get-tuple-element.34) | copy-start | bytes 1572868
  47.0 8.4 %copy-start.5 = (bf16[256,512]{1,0:T(8,128)(2,1)S(1)}, bf16[256,512]{1,0:T(8,128)(2,1)}, u32[]{:S(2)}) copy-start(bf16[256,512]{1,0:T(8,128)(2,1)} %get-tuple-element.33) | copy-start | bytes 786436
  47.1 16.0 %collective-permute-start.2 = (bf16[256,1024]{1,0:T(8,128)(2,1)S(1)}, bf16[256,1024]{1,0:T(8,128)(2,1)S(1)}, u32[]{:S(2)}, u32[]{:S(2)}) collective-permute-start(bf16[256,1024]{1,0:T(8,128)(2,1)S(1)} %get-tuple-element.39), channel_id=1, source_target_pairs={{64,0},{128,64},{192,128},{256,192},{320,256},{384,320},{448,384},... | collective-permute-start | bytes 1572872 | tf_op jit(solution)/shard_map/ppermute | solution.py:32
  52.9 15.7 %collective-permute-start.3 = (bf16[256,1024]{1,0:T(8,128)(2,1)S(1)}, bf16[256,1024]{1,0:T(8,128)(2,1)S(1)}, u32[]{:S(2)}, u32[]{:S(2)}) collective-permute-start(bf16[256,1024]{1,0:T(8,128)(2,1)S(1)} %get-tuple-element.40), channel_id=1, source_target_pairs={{704,0},{0,64},{64,128},{128,192},{192,256},{256,320},{320,384},{3... | collective-permute-start | bytes 1572872 | tf_op jit(solution)/shard_map/ppermute | solution.py:32
  55.8 13.0 %copy-start.1 = (bf16[1,256,512]{2,1,0:T(8,128)(2,1)S(1)}, bf16[1,256,512]{2,1,0:T(8,128)(2,1)}, u32[]{:S(2)}) copy-start(bf16[1,256,512]{2,1,0:T(8,128)(2,1)} %param.11) | copy-start | bytes 786436
  55.8 13.0 %copy-start.7 = (f32[512]{0:T(512)S(1)}, f32[512]{0:T(512)}, u32[]{:S(2)}) copy-start(f32[512]{0:T(512)} %param.15) | copy-start | bytes 6148
  106.1 19.1 %all-to-all-start.1 = ((bf16[8,8,2176]{2,1,0:T(8,128)(2,1)}), bf16[8,8,2176]{2,1,0:T(8,128)(2,1)S(1)}, u32[]{:S(2)}, u32[]{:S(2)}) async-start(bf16[8,8,2176]{2,1,0:T(8,128)(2,1)} %bitcast.8), calls=%async_computation.1 | async-start | bytes 557056 | tf_op jit(solution)/shard_map/all_to_all | solution.py:171
  126.0 15.6 %all-to-all-start.2 = ((bf16[12,8,768]{2,1,0:T(8,128)(2,1)}), bf16[12,8,768]{2,1,0:T(8,128)(2,1)S(1)}, u32[]{:S(2)}, u32[]{:S(2)}) async-start(bf16[12,8,768]{2,1,0:T(8,128)(2,1)} %pad_maximum_fusion.4), calls=%async_computation.2 | async-start | bytes 294912 | tf_op jit(solution)/shard_map/all_to_all | solution.py:190

commit v7 on v5

--- a/solution.py
+++ b/solution.py
@@ -100,7 +100,7 @@
     )(keep_rows, queries, window_keys, window_values, grad_attended)
 
 
-def on_device(tokens, cotangent, w_qkv, w_out, norm_gain, tile_lists, tile_counts):
+def device_step(tokens, cotangent, w_qkv, w_out, norm_gain, tile_lists, tile_counts):
     own_tokens = tokens[0]
     own_grads = cotangent[0]
     row_count, model_width = own_tokens.shape
@@ -138,13 +138,12 @@
     )
     grad_q = grad_queries.astype(jnp.bfloat16)
     term_q = lax.dot_general(normed, grad_q, contract_rows, preferred_element_type=jnp.float32)
-    early = section_sum(jnp.concatenate([term_q, term_out], axis=1))
+    early = chip_ring_sum(jnp.concatenate([term_q, term_out], axis=1))
     grad_keyvals = grad_window[row_count : 2 * row_count]
     for offset, side_index in ((-1, 0), (1, 2)):
         side_part = grad_window[side_index * row_count : (side_index + 1) * row_count]
-        grad_keyvals = grad_keyvals + passed_along(
-            side_part.astype(jnp.bfloat16), "node", offset
-        ).astype(side_part.dtype)
+        arrived = passed_along(side_part.astype(jnp.bfloat16), "node", offset)
+        grad_keyvals = grad_keyvals + arrived.astype(side_part.dtype)
     grad_kv = grad_keyvals.astype(jnp.bfloat16)
     term_kv = lax.dot_general(normed, grad_kv, contract_rows, preferred_element_type=jnp.float32)
     grad_normed = lax.dot_general(
@@ -159,7 +158,7 @@
         own_grads.astype(jnp.float32) + inverse_rms * (grad_unit - unit_rows * inner_mean)
     ).astype(jnp.bfloat16)
     gain_block = jnp.zeros((model_width, 128), jnp.float32).at[:, 0].set(term_gain)
-    late = section_sum(jnp.concatenate([term_kv, gain_block], axis=1))
+    late = chip_ring_sum(jnp.concatenate([term_kv, gain_block], axis=1))
     return (outputs[None], grad_tokens[None]) + node_sum(early, late, model_width)
 
 
@@ -180,14 +179,10 @@
     return jnp.sum(pieces.astype(jnp.float32), axis=0)
 
 
-def section_sum(term):
-    joined = section_order(term)
-    for axis in ("core", "x", "y"):
-        joined = exchange_sum(joined, axis)
-    return joined
-
-
 def node_sum(early, late, model_width):
+    joined = jnp.concatenate([early, late], axis=1)
+    joined = exchange_sum(joined, "y")
+    early, late = joined[:, : 2 * model_width], joined[:, 2 * model_width :]
     node_count = lax.axis_size("node")
     own_rows = early.shape[0]
     qkv = jnp.concatenate([early[:, :model_width], late[:, : 2 * model_width]], axis=1)
@@ -203,6 +198,13 @@
     return (part_qkv, part_out, part_gain)
 
 
+def chip_ring_sum(term):
+    joined = section_order(term)
+    for axis in ("core", "x"):
+        joined = exchange_sum(joined, axis)
+    return joined
+
+
 def solution(mesh):
     node_size, section_size = mesh.devices.shape
     core_size = 2
@@ -211,7 +213,7 @@
     fine = Mesh(mesh.devices.reshape(node_size, y_size, x_size, core_size), ("node", "y", "x", "core"))
     section = ("y", "x", "core")
     return jax.shard_map(
-        on_device,
+        device_step,
         mesh=fine,
         in_specs=(P(section, "node", None), P(section, "node", None), P(), P(), P(), P(), P()),
         out_specs=(

time: 152 us -> 142 us (0.934)
  waiting for transfers between devices: 53.6 us -> 47.5 us
  starting transfers between devices: 48.7 us -> 45.6 us
    all_to_all x4 -> x3, waiting for transfers between devices: 29.8 us -> 23.7 us  [exchange_sum(): lax.all_to_all(pieces.astype(jnp.bfloat16), axis, 0, 0, tiled=False)]
    all_to_all x4 -> x3, starting transfers between devices: 20.8 us -> 17.7 us  [exchange_sum(): lax.all_to_all(pieces.astype(jnp.bfloat16), axis, 0, 0, tiled=False)]
    reduce_sum x7 -> x6, other arithmetic: 3.85 us -> 2.53 us  [wide_sum(): return jnp.sum(pieces.astype(jnp.float32), axis=0)]
  transfers between devices with their start and end apart: 9 -> 8, of which waited for: 8 -> 7; matrix products, arithmetic and copies ran while one was open for 8% -> 8% of each run, Pallas kernels for 0% -> 0%
where the time goes in v7:
time: 142 us; the launch traced here: 140 us
  waiting for transfers between devices  47.5 us (33%)
  starting transfers between devices  45.6 us (32%)
  local copies, waits for them, and re-layouts  10.2 us (7%)
  other arithmetic  9.82 us (7%)
  Pallas kernels  9.4 us (7%)
  blocking collectives  9.39 us (7%)
  matrix products  7.48 us (5%)
    all_to_all x3, waiting for transfers between devices, exchange_sum(): lax.all_to_all(pieces.astype(jnp.bfloat16), axis, 0, 0, tiled=False)  23.7 us
    all_to_all x3, starting transfers between devices, exchange_sum(): lax.all_to_all(pieces.astype(jnp.bfloat16), axis, 0, 0, tiled=False)  17.7 us
    ppermute x1, starting transfers between devices, extended(): lax.ppermute(lax.slice_in_dim(block, 0, width, axis=dim), axis, backward)  12.2 us
    all_to_all x1, waiting for transfers between devices, node_sum(): lax.all_to_all(mixed.astype(jnp.bfloat16), 'node', 0, 0, tiled=False)  10.9 us
    pallas_call x1, Pallas kernels, fused_attention(): pl.pallas_call(attention_kernel, grid=(heads,), in_specs=[m_spec, q_spec,...  9.4 us
    all_to_all x2, blocking collectives, exchange_sum(): lax.all_to_all(pieces.astype(jnp.bfloat16), axis, 0, 0, tiled=False)  9.39 us
    ppermute x2, starting transfers between devices, passed_along(): return lax.ppermute(block, axis, route)  7.52 us
    ppermute x1, waiting for transfers between devices, extended(): lax.ppermute(lax.slice_in_dim(block, block.shape[dim] - width, None, axis...  6.43 us
  transfers between devices with their start and end apart: 8, of which 7 were waited for; matrix products, arithmetic and copies ran while one was open for 8% of the time, Pallas kernels for 0%

profile of v7, /device:TPU:6, one launch (start us, length us, event | category | flops | bytes accessed | tf_op | source)
XLA Modules:
  0.0 140.4 jit_solution(11939208818442326571)
XLA Ops:
  1.8 2.2 %convolution_convert_fusion = bf16[256,1536]{1,0:T(8,128)(2,1)S(1)} fusion(bf16[512,1536]{1,0:T(8,128)(2,1)} %param.13, bf16[1,256,512]{2,1,0:T(8,128)(2,1)} %param.11, f32[512]{0:T(512)} %param.15, f32[256]{0:T(256)S(1)} %add_rsqrt_fusion), kind=kOutput, calls=%fused_computation | convolution fusion | flops 403570688 | bytes 2624512 | tf_op jit(solution)/shard_map/dot_general | solution.py:117
  4.1 4.3 %collective-permute-start = (bf16[256,1024]{1,0:T(8,128)(2,1)S(1)}, bf16[256,1024]{1,0:T(8,128)(2,1)S(1)}, u32[]{:S(2)}, u32[]{:S(2)}) collective-permute-start(bf16[256,1024]{1,0:T(8,128)(2,1)S(1)} %slice.105), channel_id=1, source_target_pairs={{0,64},{64,128},{128,192},{192,256},{256,320},{320,384},{384,448},... | collective-permute-start | bytes 1572872 | tf_op jit(solution)/shard_map/ppermute | solution.py:21
  8.4 12.2 %collective-permute-start.1 = (bf16[256,1024]{1,0:T(8,128)(2,1)S(1)}, bf16[256,1024]{1,0:T(8,128)(2,1)S(1)}, u32[]{:S(2)}, u32[]{:S(2)}) collective-permute-start(bf16[256,1024]{1,0:T(8,128)(2,1)S(1)} %slice.105), channel_id=1, source_target_pairs={{64,0},{128,64},{192,128},{256,192},{320,256},{384,320},{448,384},... | collective-permute-start | bytes 1572872 | tf_op jit(solution)/shard_map/ppermute | solution.py:24
  24.1 6.4 %collective-permute-done = bf16[256,1024]{1,0:T(8,128)(2,1)S(1)} collective-permute-done((bf16[256,1024]{1,0:T(8,128)(2,1)S(1)}, bf16[256,1024]{1,0:T(8,128)(2,1)S(1)}, u32[]{:S(2)}, u32[]{:S(2)}) %collective-permute-start) | collective-permute-done | bytes 524320 | tf_op jit(solution)/shard_map/ppermute | solution.py:21
  30.6 1.2 collective-permute-done.1
  31.9 1.3 fusion.32
  33.1 9.4 %shard_map.110 = (bf16[256,512]{1,0:T(8,128)(2,1)}, f32[256,512]{1,0:T(8,128)}, f32[768,512]{1,0:T(8,128)}, f32[768,512]{1,0:T(8,128)}) custom-call(f32[8,768]{1,0:T(8,128)} %scatter.6.mask_ref, bf16[256,512]{1,0:T(8,128)(2,1)} %slice.104.q_ref, bf16[768,512]{1,0:T(8,128)(2,1)} %get-tuple-element.42.k_ref, bf16[768,512]{1,0:T(8,128)(2,1)} %get-tuple-element.41.v_ref, ...), custom_call_target="tpu_custom_call" | custom-call | flops 1207959552 | bytes 6029312 | tf_op jit(solution)/shard_map/pallas_call | solution.py:88
  42.5 1.6 %constant_dynamic-update-slice_fusion.1 = f32[768,1024]{1,0:T(8,128)S(1)} fusion(f32[768,512]{1,0:T(8,128)} %get-tuple-element.35), kind=kLoop, calls=%fused_computation.50 | loop fusion | bytes 3145728
  44.8 1.4 %copy-done.1 = f32[768,1024]{1,0:T(8,128)} copy-done((f32[768,1024]{1,0:T(8,128)}, f32[768,1024]{1,0:T(8,128)S(1)}, u32[]{:S(2)}) %copy-start.1) | copy-done | bytes 3145752
  47.3 5.6 %collective-permute-start.2 = (bf16[256,1024]{1,0:T(8,128)(2,1)}, bf16[256,1024]{1,0:T(8,128)(2,1)}, u32[]{:S(2)}, u32[]{:S(2)}) collective-permute-start(bf16[256,1024]{1,0:T(8,128)(2,1)} %get-tuple-element.39), channel_id=1, source_target_pairs={{64,0},{128,64},{192,128},{256,192},{320,256},{384,320},{448,384},... | collective-permute-start | bytes 1572872 | tf_op jit(solution)/shard_map/ppermute | solution.py:32
  52.9 1.9 %collective-permute-start.3 = (bf16[256,1024]{1,0:T(8,128)(2,1)}, bf16[256,1024]{1,0:T(8,128)(2,1)}, u32[]{:S(2)}, u32[]{:S(2)}) collective-permute-start(bf16[256,1024]{1,0:T(8,128)(2,1)} %get-tuple-element.40), channel_id=1, source_target_pairs={{704,0},{0,64},{64,128},{128,192},{192,256},{256,320},{320,384},{3... | collective-permute-start | bytes 1572872 | tf_op jit(solution)/shard_map/ppermute | solution.py:32
  56.4 4.7 %all_to_all.30 = bf16[2,256,1024]{2,1,0:T(8,128)(2,1)S(1)} all-to-all(bf16[2,256,1024]{2,1,0:T(8,128)(2,1)S(1)} %bitcast.52), channel_id=1, replica_groups=mesh['node'=12,'y'=8,'x'=4,'core'=2] {'core'}, dimensions={0} | all-to-all | bytes 2097152 | tf_op jit(solution)/shard_map/all_to_all | solution.py:175
  62.2 1.4 fusion.19
  63.6 5.3 %collective-permute-done.3 = bf16[256,1024]{1,0:T(8,128)(2,1)} collective-permute-done((bf16[256,1024]{1,0:T(8,128)(2,1)}, bf16[256,1024]{1,0:T(8,128)(2,1)}, u32[]{:S(2)}, u32[]{:S(2)}) %collective-permute-start.3) | collective-permute-done | bytes 524320 | tf_op jit(solution)/shard_map/ppermute | solution.py:32
  68.9 1.8 %fusion.5 = bf16[256,1024]{1,0:T(8,128)(2,1)S(1)} fusion(f32[768,1024]{1,0:T(8,128)} %copy-done.1, bf16[256,1024]{1,0:T(8,128)(2,1)} %collective-permute-done.3, bf16[256,1024]{1,0:T(8,128)(2,1)} %collective-permute-done.2), kind=kLoop, calls=%fused_computation.15 | loop fusion | flops 1310720 | bytes 2621440 | tf_op jit(solution)/shard_map/convert_element_type | solution.py:147
  72.8 4.7 %all_to_all.31 = bf16[2,256,1152]{2,1,0:T(8,128)(2,1)S(1)} all-to-all(bf16[2,256,1152]{2,1,0:T(8,128)(2,1)S(1)} %bitcast.50), channel_id=1, replica_groups=mesh['node'=12,'y'=8,'x'=4,'core'=2] {'core'}, dimensions={0} | all-to-all | bytes 2359296 | tf_op jit(solution)/shard_map/all_to_all | solution.py:175
  77.5 4.8 %all-to-all-start.1 = ((bf16[4,64,1024]{2,1,0:T(8,128)(2,1)}), bf16[4,64,1024]{2,1,0:T(8,128)(2,1)S(1)}, u32[]{:S(2)}, u32[]{:S(2)}) async-start(bf16[4,64,1024]{2,1,0:T(8,128)(2,1)} %bitcast.8), calls=%async_computation.1 | async-start | bytes 1048576 | tf_op jit(solution)/shard_map/all_to_all | solution.py:175
  83.4 6.6 %all-to-all-done.1 = bf16[4,64,1024]{2,1,0:T(8,128)(2,1)S(1)} async-done(((bf16[4,64,1024]{2,1,0:T(8,128)(2,1)}), bf16[4,64,1024]{2,1,0:T(8,128)(2,1)S(1)}, u32[]{:S(2)}, u32[]{:S(2)}) %all-to-all-start.1) | async-done | bytes 524320 | tf_op jit(solution)/shard_map/all_to_all | solution.py:175
  90.0 5.6 %all-to-all-start.3 = ((bf16[4,64,1152]{2,1,0:T(8,128)(2,1)}), bf16[4,64,1152]{2,1,0:T(8,128)(2,1)S(1)}, u32[]{:S(2)}, u32[]{:S(2)}) async-start(bf16[4,64,1152]{2,1,0:T(8,128)(2,1)} %bitcast.12), calls=%async_computation.3 | async-start | bytes 1179648 | tf_op jit(solution)/shard_map/all_to_all | solution.py:175
  95.7 7.5 %all-to-all-done.3 = bf16[4,64,1152]{2,1,0:T(8,128)(2,1)S(1)} async-done(((bf16[4,64,1152]{2,1,0:T(8,128)(2,1)}), bf16[4,64,1152]{2,1,0:T(8,128)(2,1)S(1)}, u32[]{:S(2)}, u32[]{:S(2)}) %all-to-all-start.3) | async-done | bytes 589856 | tf_op jit(solution)/shard_map/all_to_all | solution.py:175
  104.0 7.2 %all-to-all-start.4 = ((bf16[8,8,2176]{2,1,0:T(8,128)(2,1)}), bf16[8,8,2176]{2,1,0:T(8,128)(2,1)S(1)}, u32[]{:S(2)}, u32[]{:S(2)}) async-start(bf16[8,8,2176]{2,1,0:T(8,128)(2,1)} %maximum_bitcast_fusion), calls=%async_computation.4 | async-start | bytes 557056 | tf_op jit(solution)/shard_map/all_to_all | solution.py:175
  112.3 9.6 %all-to-all-done.4 = bf16[8,8,2176]{2,1,0:T(8,128)(2,1)S(1)} async-done(((bf16[8,8,2176]{2,1,0:T(8,128)(2,1)}), bf16[8,8,2176]{2,1,0:T(8,128)(2,1)S(1)}, u32[]{:S(2)}, u32[]{:S(2)}) %all-to-all-start.4) | async-done | bytes 278560 | tf_op jit(solution)/shard_map/all_to_all | solution.py:175
  122.7 3.9 %all-to-all-start.5 = ((bf16[12,8,768]{2,1,0:T(8,128)(2,1)}), bf16[12,8,768]{2,1,0:T(8,128)(2,1)S(1)}, u32[]{:S(2)}, u32[]{:S(2)}) async-start(bf16[12,8,768]{2,1,0:T(8,128)(2,1)} %pad_maximum_fusion.2), calls=%async_computation.5 | async-start | bytes 294912 | tf_op jit(solution)/shard_map/all_to_all | solution.py:193
  127.6 10.9 %all-to-all-done.5 = bf16[12,8,768]{2,1,0:T(8,128)(2,1)S(1)} async-done(((bf16[12,8,768]{2,1,0:T(8,128)(2,1)}), bf16[12,8,768]{2,1,0:T(8,128)(2,1)S(1)}, u32[]{:S(2)}, u32[]{:S(2)}) %all-to-all-start.5) | async-done | bytes 147488 | tf_op jit(solution)/shard_map/all_to_all | solution.py:193
  (76 shorter events, 17.9 us)
Async XLA Ops:
  0.6 22.5 %copy-start = (bf16[512,512]{1,0:T(8,128)(2,1)S(1)}, bf16[512,512]{1,0:T(8,128)(2,1)}, u32[]{:S(2)}) copy-start(bf16[512,512]{1,0:T(8,128)(2,1)} %param.14) | copy-start | bytes 1572868
  1.8 18.8 %copy-start.11 = (s32[24,5]{0,1:T(8,128)S(1)}, s32[24,5]{0,1:T(8,128)}, u32[]{:S(2)}) copy-start(s32[24,5]{0,1:T(8,128)} %param.16) | copy-start | bytes 1444
  1.8 19.0 %copy-start.12 = (s32[24]{0:T(128)S(1)}, s32[24]{0:T(128)}, u32[]{:S(2)}) copy-start(s32[24]{0:T(128)} %param.17) | copy-start | bytes 292
  1.8 21.3 %copy-start.4 = (bf16[1,256,512]{2,1,0:T(8,128)(2,1)S(1)}, bf16[1,256,512]{2,1,0:T(8,128)(2,1)}, u32[]{:S(2)}) copy-start(bf16[1,256,512]{2,1,0:T(8,128)(2,1)} %param.12) | copy-start | bytes 786436
  4.1 26.5 %collective-permute-start = (bf16[256,1024]{1,0:T(8,128)(2,1)S(1)}, bf16[256,1024]{1,0:T(8,128)(2,1)S(1)}, u32[]{:S(2)}, u32[]{:S(2)}) collective-permute-start(bf16[256,1024]{1,0:T(8,128)(2,1)S(1)} %slice.105), channel_id=1, source_target_pairs={{0,64},{64,128},{128,192},{192,256},{256,320},{320,384},{384,448},... | collective-permute-start | bytes 1572872 | tf_op jit(solution)/shard_map/ppermute | solution.py:21
  8.4 23.4 %collective-permute-start.1 = (bf16[256,1024]{1,0:T(8,128)(2,1)S(1)}, bf16[256,1024]{1,0:T(8,128)(2,1)S(1)}, u32[]{:S(2)}, u32[]{:S(2)}) collective-permute-start(bf16[256,1024]{1,0:T(8,128)(2,1)S(1)} %slice.105), channel_id=1, source_target_pairs={{64,0},{128,64},{192,128},{256,192},{320,256},{384,320},{448,384},... | collective-permute-start | bytes 1572872 | tf_op jit(solution)/shard_map/ppermute | solution.py:24
  42.5 1.9 %copy-start.7 = (f32[768,512]{1,0:T(8,128)S(1)}, f32[768,512]{1,0:T(8,128)}, u32[]{:S(2)}) copy-start(f32[768,512]{1,0:T(8,128)} %get-tuple-element.36) | copy-start | bytes 4718596
  44.5 1.7 %copy-start.1 = (f32[768,1024]{1,0:T(8,128)}, f32[768,1024]{1,0:T(8,128)S(1)}, u32[]{:S(2)}) copy-start(f32[768,1024]{1,0:T(8,128)S(1)} %constant_dynamic-update-slice_fusion) | copy-start | bytes 9437188
  46.2 8.6 %copy-start.2 = (bf16[1,256,512]{2,1,0:T(8,128)(2,1)S(1)}, bf16[1,256,512]{2,1,0:T(8,128)(2,1)}, u32[]{:S(2)}) copy-start(bf16[1,256,512]{2,1,0:T(8,128)(2,1)} %param.11) | copy-start | bytes 786436
  46.2 8.6 %copy-start.6 = (f32[256,512]{1,0:T(8,128)S(1)}, f32[256,512]{1,0:T(8,128)}, u32[]{:S(2)}) copy-start(f32[256,512]{1,0:T(8,128)} %get-tuple-element.34) | copy-start | bytes 1572868
  46.2 8.6 %copy-start.10 = (f32[512]{0:T(512)S(1)}, f32[512]{0:T(512)}, u32[]{:S(2)}) copy-start(f32[512]{0:T(512)} %param.15) | copy-start | bytes 6148
  46.2 9.1 %copy-start.8 = (bf16[256,512]{1,0:T(8,128)(2,1)S(1)}, bf16[256,512]{1,0:T(8,128)(2,1)}, u32[]{:S(2)}) copy-start(bf16[256,512]{1,0:T(8,128)(2,1)} %get-tuple-element.33) | copy-start | bytes 786436
  47.3 16.3 %collective-permute-start.2 = (bf16[256,1024]{1,0:T(8,128)(2,1)}, bf16[256,1024]{1,0:T(8,128)(2,1)}, u32[]{:S(2)}, u32[]{:S(2)}) collective-permute-start(bf16[256,1024]{1,0:T(8,128)(2,1)} %get-tuple-element.39), channel_id=1, source_target_pairs={{64,0},{128,64},{192,128},{256,192},{320,256},{384,320},{448,384},... | collective-permute-start | bytes 1572872 | tf_op jit(solution)/shard_map/ppermute | solution.py:32
  52.9 15.9 %collective-permute-start.3 = (bf16[256,1024]{1,0:T(8,128)(2,1)}, bf16[256,1024]{1,0:T(8,128)(2,1)}, u32[]{:S(2)}, u32[]{:S(2)}) collective-permute-start(bf16[256,1024]{1,0:T(8,128)(2,1)} %get-tuple-element.40), channel_id=1, source_target_pairs={{704,0},{0,64},{64,128},{128,192},{192,256},{256,320},{320,384},{3... | collective-permute-start | bytes 1572872 | tf_op jit(solution)/shard_map/ppermute | solution.py:32
  56.4 5.9 %copy-start.3 = (bf16[512,1536]{1,0:T(8,128)(2,1)S(1)}, bf16[512,1536]{1,0:T(8,128)(2,1)}, u32[]{:S(2)}) copy-start(bf16[512,1536]{1,0:T(8,128)(2,1)} %param.13) | copy-start | bytes 4718596
  77.5 12.5 %all-to-all-start.1 = ((bf16[4,64,1024]{2,1,0:T(8,128)(2,1)}), bf16[4,64,1024]{2,1,0:T(8,128)(2,1)S(1)}, u32[]{:S(2)}, u32[]{:S(2)}) async-start(bf16[4,64,1024]{2,1,0:T(8,128)(2,1)} %bitcast.8), calls=%async_computation.1 | async-start | bytes 1048576 | tf_op jit(solution)/shard_map/all_to_all | solution.py:175
  90.0 21.3 %copy-start.9 = (bf16[256,512]{1,0:T(8,128)(2,1)S(1)}, bf16[256,512]{1,0:T(8,128)(2,1)}, u32[]{:S(2)}) copy-start(bf16[256,512]{1,0:T(8,128)(2,1)} %get-tuple-element.33) | copy-start | bytes 786436
  90.0 13.2 %all-to-all-start.3 = ((bf16[4,64,1152]{2,1,0:T(8,128)(2,1)}), bf16[4,64,1152]{2,1,0:T(8,128)(2,1)S(1)}, u32[]{:S(2)}, u32[]{:S(2)}) async-start(bf16[4,64,1152]{2,1,0:T(8,128)(2,1)} %bitcast.12), calls=%async_computation.3 | async-start | bytes 1179648 | tf_op jit(solution)/shard_map/all_to_all | solution.py:175
  104.0 22.6 %copy-start.5 = (bf16[1,256,512]{2,1,0:T(8,128)(2,1)S(1)}, bf16[1,256,512]{2,1,0:T(8,128)(2,1)}, u32[]{:S(2)}) copy-start(bf16[1,256,512]{2,1,0:T(8,128)(2,1)} %param.12) | copy-start | bytes 786436
  104.0 17.9 %all-to-all-start.4 = ((bf16[8,8,2176]{2,1,0:T(8,128)(2,1)}), bf16[8,8,2176]{2,1,0:T(8,128)(2,1)S(1)}, u32[]{:S(2)}, u32[]{:S(2)}) async-start(bf16[8,8,2176]{2,1,0:T(8,128)(2,1)} %maximum_bitcast_fusion), calls=%async_computation.4 | async-start | bytes 557056 | tf_op jit(solution)/shard_map/all_to_all | solution.py:175
  122.7 15.8 %all-to-all-start.5 = ((bf16[12,8,768]{2,1,0:T(8,128)(2,1)}), bf16[12,8,768]{2,1,0:T(8,128)(2,1)S(1)}, u32[]{:S(2)}, u32[]{:S(2)}) async-start(bf16[12,8,768]{2,1,0:T(8,128)(2,1)} %pad_maximum_fusion.2), calls=%async_computation.5 | async-start | bytes 294912 | tf_op jit(solution)/shard_map/all_to_all | solution.py:193

commit v8 on v7

--- a/solution.py
+++ b/solution.py
@@ -138,7 +138,7 @@
     )
     grad_q = grad_queries.astype(jnp.bfloat16)
     term_q = lax.dot_general(normed, grad_q, contract_rows, preferred_element_type=jnp.float32)
-    early = chip_ring_sum(jnp.concatenate([term_q, term_out], axis=1))
+    early = chip_sum(jnp.concatenate([term_q, term_out], axis=1))
     grad_keyvals = grad_window[row_count : 2 * row_count]
     for offset, side_index in ((-1, 0), (1, 2)):
         side_part = grad_window[side_index * row_count : (side_index + 1) * row_count]
@@ -158,7 +158,7 @@
         own_grads.astype(jnp.float32) + inverse_rms * (grad_unit - unit_rows * inner_mean)
     ).astype(jnp.bfloat16)
     gain_block = jnp.zeros((model_width, 128), jnp.float32).at[:, 0].set(term_gain)
-    late = chip_ring_sum(jnp.concatenate([term_kv, gain_block], axis=1))
+    late = chip_sum(jnp.concatenate([term_kv, gain_block], axis=1))
     return (outputs[None], grad_tokens[None]) + node_sum(early, late, model_width)
 
 
@@ -181,7 +181,8 @@
 
 def node_sum(early, late, model_width):
     joined = jnp.concatenate([early, late], axis=1)
-    joined = exchange_sum(joined, "y")
+    for axis in ("x", "y"):
+        joined = exchange_sum(joined, axis)
     early, late = joined[:, : 2 * model_width], joined[:, 2 * model_width :]
     node_count = lax.axis_size("node")
     own_rows = early.shape[0]
@@ -198,11 +199,8 @@
     return (part_qkv, part_out, part_gain)
 
 
-def chip_ring_sum(term):
-    joined = section_order(term)
-    for axis in ("core", "x"):
-        joined = exchange_sum(joined, axis)
-    return joined
+def chip_sum(term):
+    return exchange_sum(section_order(term), "core")
 
 
 def solution(mesh):

time: 142 us -> 137 us (0.965)
  blocking collectives: 9.39 us -> 28.2 us
  waiting for transfers between devices: 47.5 us -> 33.9 us
  starting transfers between devices: 45.6 us -> 35.2 us
    all_to_all x2 -> x3, blocking collectives: 9.39 us -> 28.2 us  [exchange_sum(): lax.all_to_all(pieces.astype(jnp.bfloat16), axis, 0, 0, tiled=False)]
    all_to_all x3 -> x1, waiting for transfers between devices: 23.7 us -> 10.4 us  [exchange_sum(): lax.all_to_all(pieces.astype(jnp.bfloat16), axis, 0, 0, tiled=False)]
    all_to_all x3 -> x1, starting transfers between devices: 17.7 us -> 7.24 us  [exchange_sum(): lax.all_to_all(pieces.astype(jnp.bfloat16), axis, 0, 0, tiled=False)]
    unnamed x29 -> x33, local copies, waits for them, and re-layouts: 3.42 us -> 3.43 us
  transfers between devices with their start and end apart: 8 -> 6, of which waited for: 7 -> 5; matrix products, arithmetic and copies ran while one was open for 8% -> 7% of each run, Pallas kernels for 0% -> 0%
where the time goes in v8:
time: 137 us; the launch traced here: 135 us
  starting transfers between devices  35.2 us (26%)
  waiting for transfers between devices  33.9 us (25%)
  blocking collectives  28.2 us (21%)
  local copies, waits for them, and re-layouts  10.2 us (7%)
  Pallas kernels  9.4 us (7%)
  other arithmetic  9.02 us (7%)
  matrix products  8.19 us (6%)
    all_to_all x3, blocking collectives, exchange_sum(): lax.all_to_all(pieces.astype(jnp.bfloat16), axis, 0, 0, tiled=False)  28.2 us
    ppermute x1, starting transfers between devices, extended(): lax.ppermute(lax.slice_in_dim(block, 0, width, axis=dim), axis, backward)  12.2 us
    all_to_all x1, waiting for transfers between devices, node_sum(): lax.all_to_all(mixed.astype(jnp.bfloat16), 'node', 0, 0, tiled=False)  10.7 us
    all_to_all x1, waiting for transfers between devices, exchange_sum(): lax.all_to_all(pieces.astype(jnp.bfloat16), axis, 0, 0, tiled=False)  10.4 us
    pallas_call x1, Pallas kernels, fused_attention(): pl.pallas_call(attention_kernel, grid=(heads,), in_specs=[m_spec, q_spec,...  9.4 us
    ppermute x2, starting transfers between devices, passed_along(): return lax.ppermute(block, axis, route)  7.52 us
    all_to_all x1, starting transfers between devices, exchange_sum(): lax.all_to_all(pieces.astype(jnp.bfloat16), axis, 0, 0, tiled=False)  7.24 us
    ppermute x1, waiting for transfers between devices, extended(): lax.ppermute(lax.slice_in_dim(block, block.shape[dim] - width, None, axis...  6.43 us
  transfers between devices with their start and end apart: 6, of which 5 were waited for; matrix products, arithmetic and copies ran while one was open for 7% of the time, Pallas kernels for 0%

profile of v8, /device:TPU:6, one launch (start us, length us, event | category | flops | bytes accessed | tf_op | source)
XLA Modules:
  0.0 135.2 jit_solution(4928888599784867385)
XLA Ops:
  0.6 1.1 fusion.18
  1.8 2.2 %convolution_convert_fusion = bf16[256,1536]{1,0:T(8,128)(2,1)S(1)} fusion(bf16[512,1536]{1,0:T(8,128)(2,1)} %param.13, bf16[1,256,512]{2,1,0:T(8,128)(2,1)} %param.11, f32[512]{0:T(512)} %param.15, f32[256]{0:T(256)S(1)} %add_rsqrt_fusion), kind=kOutput, calls=%fused_computation | convolution fusion | flops 403570688 | bytes 2624512 | tf_op jit(solution)/shard_map/dot_general | solution.py:117
  4.1 4.3 %collective-permute-start = (bf16[256,1024]{1,0:T(8,128)(2,1)S(1)}, bf16[256,1024]{1,0:T(8,128)(2,1)S(1)}, u32[]{:S(2)}, u32[]{:S(2)}) collective-permute-start(bf16[256,1024]{1,0:T(8,128)(2,1)S(1)} %slice.105), channel_id=1, source_target_pairs={{0,64},{64,128},{128,192},{192,256},{256,320},{320,384},{384,448},... | collective-permute-start | bytes 1572872 | tf_op jit(solution)/shard_map/ppermute | solution.py:21
  8.4 12.2 %collective-permute-start.1 = (bf16[256,1024]{1,0:T(8,128)(2,1)S(1)}, bf16[256,1024]{1,0:T(8,128)(2,1)S(1)}, u32[]{:S(2)}, u32[]{:S(2)}) collective-permute-start(bf16[256,1024]{1,0:T(8,128)(2,1)S(1)} %slice.105), channel_id=1, source_target_pairs={{64,0},{128,64},{192,128},{256,192},{320,256},{384,320},{448,384},... | collective-permute-start | bytes 1572872 | tf_op jit(solution)/shard_map/ppermute | solution.py:24
  24.1 6.4 %collective-permute-done = bf16[256,1024]{1,0:T(8,128)(2,1)S(1)} collective-permute-done((bf16[256,1024]{1,0:T(8,128)(2,1)S(1)}, bf16[256,1024]{1,0:T(8,128)(2,1)S(1)}, u32[]{:S(2)}, u32[]{:S(2)}) %collective-permute-start) | collective-permute-done | bytes 524320 | tf_op jit(solution)/shard_map/ppermute | solution.py:21
  30.6 1.2 collective-permute-done.1
  31.9 1.3 fusion.32
  33.1 9.4 %shard_map.110 = (bf16[256,512]{1,0:T(8,128)(2,1)}, f32[256,512]{1,0:T(8,128)}, f32[768,512]{1,0:T(8,128)}, f32[768,512]{1,0:T(8,128)}) custom-call(f32[8,768]{1,0:T(8,128)} %scatter.6.mask_ref, bf16[256,512]{1,0:T(8,128)(2,1)} %slice.104.q_ref, bf16[768,512]{1,0:T(8,128)(2,1)} %get-tuple-element.42.k_ref, bf16[768,512]{1,0:T(8,128)(2,1)} %get-tuple-element.41.v_ref, ...), custom_call_target="tpu_custom_call" | custom-call | flops 1207959552 | bytes 6029312 | tf_op jit(solution)/shard_map/pallas_call | solution.py:88
  42.5 1.6 %constant_dynamic-update-slice_fusion.1 = f32[768,1024]{1,0:T(8,128)S(1)} fusion(f32[768,512]{1,0:T(8,128)} %get-tuple-element.35), kind=kLoop, calls=%fused_computation.50 | loop fusion | bytes 3145728
  44.8 1.4 %copy-done.1 = f32[768,1024]{1,0:T(8,128)} copy-done((f32[768,1024]{1,0:T(8,128)}, f32[768,1024]{1,0:T(8,128)S(1)}, u32[]{:S(2)}) %copy-start.1) | copy-done | bytes 3145752
  47.3 5.6 %collective-permute-start.2 = (bf16[256,1024]{1,0:T(8,128)(2,1)}, bf16[256,1024]{1,0:T(8,128)(2,1)}, u32[]{:S(2)}, u32[]{:S(2)}) collective-permute-start(bf16[256,1024]{1,0:T(8,128)(2,1)} %get-tuple-element.39), channel_id=1, source_target_pairs={{64,0},{128,64},{192,128},{256,192},{320,256},{384,320},{448,384},... | collective-permute-start | bytes 1572872 | tf_op jit(solution)/shard_map/ppermute | solution.py:32
  52.9 1.9 %collective-permute-start.3 = (bf16[256,1024]{1,0:T(8,128)(2,1)}, bf16[256,1024]{1,0:T(8,128)(2,1)}, u32[]{:S(2)}, u32[]{:S(2)}) collective-permute-start(bf16[256,1024]{1,0:T(8,128)(2,1)} %get-tuple-element.40), channel_id=1, source_target_pairs={{704,0},{0,64},{64,128},{128,192},{192,256},{256,320},{320,384},{3... | collective-permute-start | bytes 1572872 | tf_op jit(solution)/shard_map/ppermute | solution.py:32
  56.4 4.7 %all_to_all.25 = bf16[2,256,1024]{2,1,0:T(8,128)(2,1)S(1)} all-to-all(bf16[2,256,1024]{2,1,0:T(8,128)(2,1)S(1)} %bitcast.51), channel_id=1, replica_groups=mesh['node'=12,'y'=8,'x'=4,'core'=2] {'core'}, dimensions={0} | all-to-all | bytes 2097152 | tf_op jit(solution)/shard_map/all_to_all | solution.py:175
  61.1 1.1 reduce.10
  62.2 1.4 %fusion.19 = f32[256,512]{1,0:T(8,128)S(1)} fusion(bf16[512,1536]{1,0:T(8,128)(2,1)S(1)} %copy-done.3, f32[256,512]{1,0:T(8,128)} %get-tuple-element.34), kind=kOutput, calls=%fused_computation.34 | convolution fusion | flops 134348800 | bytes 1572864 | tf_op jit(solution)/shard_map/dot_general | solution.py:149
  63.6 5.3 %collective-permute-done.3 = bf16[256,1024]{1,0:T(8,128)(2,1)} collective-permute-done((bf16[256,1024]{1,0:T(8,128)(2,1)}, bf16[256,1024]{1,0:T(8,128)(2,1)}, u32[]{:S(2)}, u32[]{:S(2)}) %collective-permute-start.3) | collective-permute-done | bytes 524320 | tf_op jit(solution)/shard_map/ppermute | solution.py:32
  68.9 1.8 %fusion.5 = bf16[256,1024]{1,0:T(8,128)(2,1)S(1)} fusion(f32[768,1024]{1,0:T(8,128)} %copy-done.1, bf16[256,1024]{1,0:T(8,128)(2,1)} %collective-permute-done.3, bf16[256,1024]{1,0:T(8,128)(2,1)} %collective-permute-done.2), kind=kLoop, calls=%fused_computation.16 | loop fusion | flops 1310720 | bytes 2621440 | tf_op jit(solution)/shard_map/convert_element_type | solution.py:147
  71.2 1.3 fusion.17
  73.6 4.8 %all_to_all.26 = bf16[2,256,1152]{2,1,0:T(8,128)(2,1)S(1)} all-to-all(bf16[2,256,1152]{2,1,0:T(8,128)(2,1)S(1)} %bitcast.48), channel_id=1, replica_groups=mesh['node'=12,'y'=8,'x'=4,'core'=2] {'core'}, dimensions={0} | all-to-all | bytes 2359296 | tf_op jit(solution)/shard_map/all_to_all | solution.py:175
  78.7 18.7 %all_to_all.27 = bf16[4,64,2176]{2,1,0:T(8,128)(2,1)S(1)} all-to-all(bf16[4,64,2176]{2,1,0:T(8,128)(2,1)S(1)} %bitcast.49), channel_id=1, replica_groups=mesh['node'=12,'y'=8,'x'=4,'core'=2] {'x'}, dimensions={0} | all-to-all | bytes 2228224 | tf_op jit(solution)/shard_map/all_to_all | solution.py:175
  98.4 7.2 %all-to-all-start.3 = ((bf16[8,8,2176]{2,1,0:T(8,128)(2,1)}), bf16[8,8,2176]{2,1,0:T(8,128)(2,1)S(1)}, u32[]{:S(2)}, u32[]{:S(2)}) async-start(bf16[8,8,2176]{2,1,0:T(8,128)(2,1)} %bitcast.12), calls=%async_computation.3 | async-start | bytes 557056 | tf_op jit(solution)/shard_map/all_to_all | solution.py:175
  106.6 10.4 %all-to-all-done.3 = bf16[8,8,2176]{2,1,0:T(8,128)(2,1)S(1)} async-done(((bf16[8,8,2176]{2,1,0:T(8,128)(2,1)}), bf16[8,8,2176]{2,1,0:T(8,128)(2,1)S(1)}, u32[]{:S(2)}, u32[]{:S(2)}) %all-to-all-start.3) | async-done | bytes 278560 | tf_op jit(solution)/shard_map/all_to_all | solution.py:175
  117.8 3.9 %all-to-all-start.4 = ((bf16[12,8,768]{2,1,0:T(8,128)(2,1)}), bf16[12,8,768]{2,1,0:T(8,128)(2,1)S(1)}, u32[]{:S(2)}, u32[]{:S(2)}) async-start(bf16[12,8,768]{2,1,0:T(8,128)(2,1)} %pad_maximum_fusion.3), calls=%async_computation.4 | async-start | bytes 294912 | tf_op jit(solution)/shard_map/all_to_all | solution.py:194
  122.7 10.7 %all-to-all-done.4 = bf16[12,8,768]{2,1,0:T(8,128)(2,1)S(1)} async-done(((bf16[12,8,768]{2,1,0:T(8,128)(2,1)}), bf16[12,8,768]{2,1,0:T(8,128)(2,1)S(1)}, u32[]{:S(2)}, u32[]{:S(2)}) %all-to-all-start.4) | async-done | bytes 147488 | tf_op jit(solution)/shard_map/all_to_all | solution.py:194
  (76 shorter events, 14.2 us)
Async XLA Ops:
  0.6 22.5 %copy-start = (bf16[512,512]{1,0:T(8,128)(2,1)S(1)}, bf16[512,512]{1,0:T(8,128)(2,1)}, u32[]{:S(2)}) copy-start(bf16[512,512]{1,0:T(8,128)(2,1)} %param.14) | copy-start | bytes 1572868
  1.8 18.8 %copy-start.13 = (s32[24,5]{0,1:T(8,128)S(1)}, s32[24,5]{0,1:T(8,128)}, u32[]{:S(2)}) copy-start(s32[24,5]{0,1:T(8,128)} %param.16) | copy-start | bytes 1444
  1.8 19.0 %copy-start.14 = (s32[24]{0:T(128)S(1)}, s32[24]{0:T(128)}, u32[]{:S(2)}) copy-start(s32[24]{0:T(128)} %param.17) | copy-start | bytes 292
  1.8 21.3 %copy-start.4 = (bf16[1,256,512]{2,1,0:T(8,128)(2,1)S(1)}, bf16[1,256,512]{2,1,0:T(8,128)(2,1)}, u32[]{:S(2)}) copy-start(bf16[1,256,512]{2,1,0:T(8,128)(2,1)} %param.12) | copy-start | bytes 786436
  4.1 26.5 %collective-permute-start = (bf16[256,1024]{1,0:T(8,128)(2,1)S(1)}, bf16[256,1024]{1,0:T(8,128)(2,1)S(1)}, u32[]{:S(2)}, u32[]{:S(2)}) collective-permute-start(bf16[256,1024]{1,0:T(8,128)(2,1)S(1)} %slice.105), channel_id=1, source_target_pairs={{0,64},{64,128},{128,192},{192,256},{256,320},{320,384},{384,448},... | collective-permute-start | bytes 1572872 | tf_op jit(solution)/shard_map/ppermute | solution.py:21
  8.4 23.4 %collective-permute-start.1 = (bf16[256,1024]{1,0:T(8,128)(2,1)S(1)}, bf16[256,1024]{1,0:T(8,128)(2,1)S(1)}, u32[]{:S(2)}, u32[]{:S(2)}) collective-permute-start(bf16[256,1024]{1,0:T(8,128)(2,1)S(1)} %slice.105), channel_id=1, source_target_pairs={{64,0},{128,64},{192,128},{256,192},{320,256},{384,320},{448,384},... | collective-permute-start | bytes 1572872 | tf_op jit(solution)/shard_map/ppermute | solution.py:24
  42.5 1.9 %copy-start.8 = (f32[768,512]{1,0:T(8,128)S(1)}, f32[768,512]{1,0:T(8,128)}, u32[]{:S(2)}) copy-start(f32[768,512]{1,0:T(8,128)} %get-tuple-element.36) | copy-start | bytes 4718596
  44.5 1.7 %copy-start.1 = (f32[768,1024]{1,0:T(8,128)}, f32[768,1024]{1,0:T(8,128)S(1)}, u32[]{:S(2)}) copy-start(f32[768,1024]{1,0:T(8,128)S(1)} %constant_dynamic-update-slice_fusion) | copy-start | bytes 9437188
  46.2 8.6 %copy-start.2 = (bf16[1,256,512]{2,1,0:T(8,128)(2,1)S(1)}, bf16[1,256,512]{2,1,0:T(8,128)(2,1)}, u32[]{:S(2)}) copy-start(bf16[1,256,512]{2,1,0:T(8,128)(2,1)} %param.11) | copy-start | bytes 786436
  46.2 8.6 %copy-start.6 = (f32[256,512]{1,0:T(8,128)S(1)}, f32[256,512]{1,0:T(8,128)}, u32[]{:S(2)}) copy-start(f32[256,512]{1,0:T(8,128)} %get-tuple-element.34) | copy-start | bytes 1572868
  46.2 8.6 %copy-start.12 = (f32[512]{0:T(512)S(1)}, f32[512]{0:T(512)}, u32[]{:S(2)}) copy-start(f32[512]{0:T(512)} %param.15) | copy-start | bytes 6148
  46.2 9.1 %copy-start.9 = (bf16[256,512]{1,0:T(8,128)(2,1)S(1)}, bf16[256,512]{1,0:T(8,128)(2,1)}, u32[]{:S(2)}) copy-start(bf16[256,512]{1,0:T(8,128)(2,1)} %get-tuple-element.33) | copy-start | bytes 786436
  47.3 16.3 %collective-permute-start.2 = (bf16[256,1024]{1,0:T(8,128)(2,1)}, bf16[256,1024]{1,0:T(8,128)(2,1)}, u32[]{:S(2)}, u32[]{:S(2)}) collective-permute-start(bf16[256,1024]{1,0:T(8,128)(2,1)} %get-tuple-element.39), channel_id=1, source_target_pairs={{64,0},{128,64},{192,128},{256,192},{320,256},{384,320},{448,384},... | collective-permute-start | bytes 1572872 | tf_op jit(solution)/shard_map/ppermute | solution.py:32
  52.9 15.9 %collective-permute-start.3 = (bf16[256,1024]{1,0:T(8,128)(2,1)}, bf16[256,1024]{1,0:T(8,128)(2,1)}, u32[]{:S(2)}, u32[]{:S(2)}) collective-permute-start(bf16[256,1024]{1,0:T(8,128)(2,1)} %get-tuple-element.40), channel_id=1, source_target_pairs={{704,0},{0,64},{64,128},{128,192},{192,256},{256,320},{320,384},{3... | collective-permute-start | bytes 1572872 | tf_op jit(solution)/shard_map/ppermute | solution.py:32
  56.4 5.9 %copy-start.3 = (bf16[512,1536]{1,0:T(8,128)(2,1)S(1)}, bf16[512,1536]{1,0:T(8,128)(2,1)}, u32[]{:S(2)}) copy-start(bf16[512,1536]{1,0:T(8,128)(2,1)} %param.13) | copy-start | bytes 4718596
  73.5 5.1 %copy-start.7 = (bf16[256,1024]{1,0:T(8,128)(2,1)S(1)}, bf16[256,1024]{1,0:T(8,128)(2,1)}, u32[]{:S(2)}) copy-start(bf16[256,1024]{1,0:T(8,128)(2,1)} %reduce.10) | copy-start | bytes 1572868
  78.7 26.9 %copy-start.10 = (bf16[256,512]{1,0:T(8,128)(2,1)S(1)}, bf16[256,512]{1,0:T(8,128)(2,1)}, u32[]{:S(2)}) copy-start(bf16[256,512]{1,0:T(8,128)(2,1)} %get-tuple-element.33) | copy-start | bytes 786436
  98.4 23.4 %copy-start.5 = (bf16[1,256,512]{2,1,0:T(8,128)(2,1)S(1)}, bf16[1,256,512]{2,1,0:T(8,128)(2,1)}, u32[]{:S(2)}) copy-start(bf16[1,256,512]{2,1,0:T(8,128)(2,1)} %param.12) | copy-start | bytes 786436
  98.4 23.4 %copy-start.11 = (f32[256,512]{1,0:T(8,128)S(1)}, f32[256,512]{1,0:T(8,128)}, u32[]{:S(2)}) copy-start(f32[256,512]{1,0:T(8,128)} %get-tuple-element.45) | copy-start | bytes 1572868
  98.4 18.6 %all-to-all-start.3 = ((bf16[8,8,2176]{2,1,0:T(8,128)(2,1)}), bf16[8,8,2176]{2,1,0:T(8,128)(2,1)S(1)}, u32[]{:S(2)}, u32[]{:S(2)}) async-start(bf16[8,8,2176]{2,1,0:T(8,128)(2,1)} %bitcast.12), calls=%async_computation.3 | async-start | bytes 557056 | tf_op jit(solution)/shard_map/all_to_all | solution.py:175
  117.8 15.6 %all-to-all-start.4 = ((bf16[12,8,768]{2,1,0:T(8,128)(2,1)}), bf16[12,8,768]{2,1,0:T(8,128)(2,1)S(1)}, u32[]{:S(2)}, u32[]{:S(2)}) async-start(bf16[12,8,768]{2,1,0:T(8,128)(2,1)} %pad_maximum_fusion.3), calls=%async_computation.4 | async-start | bytes 294912 | tf_op jit(solution)/shard_map/all_to_all | solution.py:194

commit v9 on v8

--- a/solution.py
+++ b/solution.py
@@ -10,20 +10,6 @@
 
 EPS = 1e-06
 MASKED = -1000000000.0
-
-
-def extended(block, sides, width):
-    for axis, dim in sides:
-        count = lax.axis_size(axis)
-        forward = [(i, i + 1) for i in range(count - 1)]
-        forward.append((count - 1, 0))
-        backward = [(target, source) for source, target in forward]
-        low = lax.ppermute(
-            lax.slice_in_dim(block, block.shape[dim] - width, None, axis=dim), axis, forward
-        )
-        high = lax.ppermute(lax.slice_in_dim(block, 0, width, axis=dim), axis, backward)
-        block = jnp.concatenate([low, block, high], axis=dim)
-    return block
 
 
 def passed_along(block, axis, distance):
@@ -44,15 +30,17 @@
     return jnp.any(matches, axis=1)
 
 
-def attention_kernel(mask_ref, q_ref, k_ref, v_ref, ga_ref, att_ref, gq_ref, gk_ref, gv_ref):
+def attention_kernel(mask_ref, q_ref, k_ref, v_ref, kp_ref, vp_ref, kn_ref, vn_ref, ga_ref,
+                     att_ref, gq_ref, gk_ref, gv_ref, gkp_ref, gvp_ref, gkn_ref, gvn_ref):
     head_dim = q_ref.shape[1]
+    block_rows = k_ref.shape[0]
     score_scale = head_dim ** (-0.5)
-    keys = k_ref[...]
-    values = v_ref[...]
+    keys = jnp.concatenate([kp_ref[...], k_ref[...], kn_ref[...]], axis=0)
+    values = jnp.concatenate([vp_ref[...], v_ref[...], vn_ref[...]], axis=0)
     nt = (((1,), (1,)), ((), ()))
     tn = (((0,), (0,)), ((), ()))
-    grad_keys = jnp.zeros(gk_ref.shape, jnp.float32)
-    grad_values = jnp.zeros(gv_ref.shape, jnp.float32)
+    grad_keys = jnp.zeros(keys.shape, jnp.float32)
+    grad_values = jnp.zeros(values.shape, jnp.float32)
     for tile in range(q_ref.shape[0] // TILE):
         rows = slice(tile * TILE, (tile + 1) * TILE)
         queries = q_ref[rows, :]
@@ -68,36 +56,39 @@
         grad_probs = lax.dot_general(grads, values, nt, preferred_element_type=jnp.float32)
         centre = jnp.sum(grad_probs * probabilities, axis=1, keepdims=True)
         grad_scores = (probabilities * (grad_probs - centre) * score_scale).astype(jnp.bfloat16)
-        gq_ref[rows, :] = jnp.dot(grad_scores, keys, preferred_element_type=jnp.float32)
+        gq_ref[rows, :] = jnp.dot(grad_scores, keys, preferred_element_type=jnp.float32).astype(gq_ref.dtype)
         grad_keys = grad_keys + lax.dot_general(grad_scores, queries, tn, preferred_element_type=jnp.float32)
         grad_values = grad_values + lax.dot_general(rounded, grads, tn, preferred_element_type=jnp.float32)
-    gk_ref[...] = grad_keys
-    gv_ref[...] = grad_values
-
-
-def fused_attention(keep_rows, queries, window_keys, window_values, grad_attended, heads):
-    rows, width = queries.shape
-    span = window_keys.shape[0]
+    gkp_ref[...] = grad_keys[:block_rows].astype(gkp_ref.dtype)
+    gvp_ref[...] = grad_values[:block_rows].astype(gvp_ref.dtype)
+    gk_ref[...] = grad_keys[block_rows : 2 * block_rows]
+    gv_ref[...] = grad_values[block_rows : 2 * block_rows]
+    gkn_ref[...] = grad_keys[2 * block_rows :].astype(gkn_ref.dtype)
+    gvn_ref[...] = grad_values[2 * block_rows :].astype(gvn_ref.dtype)
+
+
+def fused_attention(keep_rows, projected, low, high, grad_attended, heads):
+    rows, width = grad_attended.shape
     head_dim = width // heads
-    q_spec = pl.BlockSpec((rows, head_dim), lambda h: (0, h))
-    w_spec = pl.BlockSpec((span, head_dim), lambda h: (0, h))
+    span = 3 * rows
+
+    def column(offset):
+        return pl.BlockSpec((rows, head_dim), lambda h: (0, h + offset))
+
     m_spec = pl.BlockSpec(keep_rows.shape, lambda h: (0, 0))
-    flops = 12 * rows * span * width
-    cost = pl.CostEstimate(flops=flops, transcendentals=rows * span * heads,
-                           bytes_accessed=2 * (2 * rows * width + 2 * span * width) + 4 * (rows * width + 2 * span * width) + 2 * rows * width)
+    cost = pl.CostEstimate(flops=12 * rows * span * width, transcendentals=rows * span * heads,
+                           bytes_accessed=2 * (3 * rows * width + 2 * span * width) + 4 * (2 * rows * width) + 2 * (5 * rows * width))
+    bf16_out = jax.ShapeDtypeStruct((rows, width), jnp.bfloat16)
+    f32_out = jax.ShapeDtypeStruct((rows, width), jnp.float32)
     return pl.pallas_call(
         attention_kernel,
         grid=(heads,),
-        in_specs=[m_spec, q_spec, w_spec, w_spec, q_spec],
-        out_specs=[q_spec, q_spec, w_spec, w_spec],
-        out_shape=[
-            jax.ShapeDtypeStruct((rows, width), jnp.bfloat16),
-            jax.ShapeDtypeStruct((rows, width), jnp.float32),
-            jax.ShapeDtypeStruct((span, width), jnp.float32),
-            jax.ShapeDtypeStruct((span, width), jnp.float32),
-        ],
+        in_specs=[m_spec, column(0), column(heads), column(2 * heads), column(0), column(heads),
+                  column(0), column(heads), column(0)],
+        out_specs=[column(0)] * 8,
+        out_shape=[bf16_out, bf16_out, f32_out, f32_out, bf16_out, bf16_out, bf16_out, bf16_out],
         cost_estimate=cost,
-    )(keep_rows, queries, window_keys, window_values, grad_attended)
+    )(keep_rows, projected, projected, projected, low, low, high, high, grad_attended)
 
 
 def device_step(tokens, cotangent, w_qkv, w_out, norm_gain, tile_lists, tile_counts):
@@ -115,35 +106,32 @@
     unit_rows = widened * inverse_rms
     normed = (unit_rows * norm_gain).astype(jnp.bfloat16)
     projected = jnp.dot(normed, w_qkv, preferred_element_type=jnp.float32).astype(jnp.bfloat16)
-    queries = projected[:, :model_width]
-    window = extended(projected[:, model_width:], (("node", 0),), row_count)
-    window_keys = window[:, :model_width]
-    window_values = window[:, model_width:]
+    keyvals = projected[:, model_width:]
+    low = passed_along(keyvals, "node", 1)
+    high = passed_along(keyvals, "node", -1)
     contract_rows = (((0,), (0,)), ((), ()))
     contract_cols = (((1,), (1,)), ((), ()))
     grad_attended = lax.dot_general(
         own_grads, w_out, contract_cols, preferred_element_type=jnp.float32
     ).astype(jnp.bfloat16)
-    keep_rows = jnp.zeros((8, window_keys.shape[0]), jnp.float32)
+    keep_rows = jnp.zeros((8, 3 * row_count), jnp.float32)
     keep_rows = keep_rows.at[:tile_count].set(jnp.repeat(allowed, TILE, axis=1).astype(jnp.float32))
-    attended, grad_queries, grad_keys, grad_values = fused_attention(
-        keep_rows, queries, window_keys, window_values, grad_attended, HEADS
-    )
-    grad_window = jnp.concatenate([grad_keys, grad_values], axis=1)
+    (attended, grad_q, grad_keys, grad_values, low_keys, low_values, high_keys, high_values) = (
+        fused_attention(keep_rows, projected, low, high, grad_attended, HEADS)
+    )
     outputs = (widened + jnp.dot(attended, w_out, preferred_element_type=jnp.float32)).astype(
         jnp.bfloat16
     )
     term_out = lax.dot_general(
         attended, own_grads, contract_rows, preferred_element_type=jnp.float32
     )
-    grad_q = grad_queries.astype(jnp.bfloat16)
     term_q = lax.dot_general(normed, grad_q, contract_rows, preferred_element_type=jnp.float32)
     early = chip_sum(jnp.concatenate([term_q, term_out], axis=1))
-    grad_keyvals = grad_window[row_count : 2 * row_count]
-    for offset, side_index in ((-1, 0), (1, 2)):
-        side_part = grad_window[side_index * row_count : (side_index + 1) * row_count]
-        arrived = passed_along(side_part.astype(jnp.bfloat16), "node", offset)
-        grad_keyvals = grad_keyvals + arrived.astype(side_part.dtype)
+    grad_keyvals = jnp.concatenate([grad_keys, grad_values], axis=1)
+    for offset, side_keys, side_values in ((-1, low_keys, low_values), (1, high_keys, high_values)):
+        side_part = jnp.concatenate([side_keys, side_values], axis=1)
+        arrived = passed_along(side_part, "node", offset)
+        grad_keyvals = grad_keyvals + arrived.astype(jnp.float32)
     grad_kv = grad_keyvals.astype(jnp.bfloat16)
     term_kv = lax.dot_general(normed, grad_kv, contract_rows, preferred_element_type=jnp.float32)
     grad_normed = lax.dot_general(

time: 137 us -> 135 us (0.985)
  local copies, waits for them, and re-layouts: 10.2 us -> 4.55 us
  waiting for transfers between devices: 33.9 us -> 36.9 us
  other arithmetic: 9.02 us -> 11.5 us
    ppermute x2 -> x0, starting transfers between devices: 16.5 us -> none  [the longest x1 12.2 us: extended(): lax.ppermute(lax.slice_in_dim(block, 0, width, axis=dim), axis, backward)]
    ppermute x2 -> x4, starting transfers between devices: 7.52 us -> 24 us  [passed_along(): return lax.ppermute(block, axis, route)]
    ppermute x2 -> x4, waiting for transfers between devices: 5.26 us -> 15.9 us  [passed_along(): return lax.ppermute(block, axis, route)]
    ppermute x2 -> x0, waiting for transfers between devices: 7.61 us -> none  [the longest x1 6.43 us: extended(): lax.ppermute(lax.slice_in_dim(block, block.shape[dim] - width, None, axis...]
    concatenate x1 -> x2, other arithmetic: 0.12 us -> 3.86 us  [device_step(): side_part = jnp.concatenate([side_keys, side_values], axis=1)]
    slice x4 -> x1, local copies, waits for them, and re-layouts: 3.13 us -> 0.06 us  [device_step(): keyvals = projected[:, model_width:]]
    unnamed x33 -> x34, local copies, waits for them, and re-layouts: 3.43 us -> 0.97 us
  transfers between devices with their start and end apart: 6 -> 6, of which waited for: 5 -> 6; matrix products, arithmetic and copies ran while one was open for 7% -> 6% of each run, Pallas kernels for 0% -> 0%
where the time goes in v9:
time: 135 us; the launch traced here: 134 us
  waiting for transfers between devices  36.9 us (27%)
  starting transfers between devices  35.2 us (26%)
  blocking collectives  28.1 us (21%)
  other arithmetic  11.5 us (9%)
  Pallas kernels  9.3 us (7%)
  matrix products  7.17 us (5%)
  local copies, waits for them, and re-layouts  4.55 us (3%)
    all_to_all x3, blocking collectives, exchange_sum(): lax.all_to_all(pieces.astype(jnp.bfloat16), axis, 0, 0, tiled=False)  28.1 us
    ppermute x4, starting transfers between devices, passed_along(): return lax.ppermute(block, axis, route)  24 us
    ppermute x4, waiting for transfers between devices, passed_along(): return lax.ppermute(block, axis, route)  15.9 us
    all_to_all x1, waiting for transfers between devices, node_sum(): lax.all_to_all(mixed.astype(jnp.bfloat16), 'node', 0, 0, tiled=False)  10.7 us
    all_to_all x1, waiting for transfers between devices, exchange_sum(): lax.all_to_all(pieces.astype(jnp.bfloat16), axis, 0, 0, tiled=False)  10.4 us
    pallas_call x1, Pallas kernels, fused_attention(): pl.pallas_call(attention_kernel, grid=(heads,), in_specs=[m_spec, column(...  9.3 us
    all_to_all x1, starting transfers between devices, exchange_sum(): lax.all_to_all(pieces.astype(jnp.bfloat16), axis, 0, 0, tiled=False)  7.24 us
    all_to_all x1, starting transfers between devices, node_sum(): lax.all_to_all(mixed.astype(jnp.bfloat16), 'node', 0, 0, tiled=False)  3.94 us
  transfers between devices with their start and end apart: 6, of which 6 were waited for; matrix products, arithmetic and copies ran while one was open for 6% of the time, Pallas kernels for 0%

profile of v9, /device:TPU:6, one launch (start us, length us, event | category | flops | bytes accessed | tf_op | source)
XLA Modules:
  0.0 133.8 jit_solution(2226281249685739330)
XLA Ops:
  0.6 1.1 fusion.19
  1.8 2.2 %convolution_convert_fusion.q_ref.k_ref.v_ref = bf16[256,1536]{1,0:T(8,128)(2,1)S(1)} fusion(bf16[512,1536]{1,0:T(8,128)(2,1)} %param.13, bf16[1,256,512]{2,1,0:T(8,128)(2,1)} %param.11, f32[512]{0:T(512)} %param.15, f32[256]{0:T(256)S(1)} %add_rsqrt_fusion), kind=kOutput, calls=%fused_computation | convolution fusion | flops 403570688 | bytes 2624512 | tf_op jit(solution)/shard_map/dot_general | solution.py:108
  4.1 4.3 %collective-permute-start = (bf16[256,1024]{1,0:T(8,128)(2,1)S(1)}, bf16[256,1024]{1,0:T(8,128)(2,1)S(1)}, u32[]{:S(2)}, u32[]{:S(2)}) collective-permute-start(bf16[256,1024]{1,0:T(8,128)(2,1)S(1)} %slice.78), channel_id=1, source_target_pairs={{704,0},{0,64},{64,128},{128,192},{192,256},{256,320},{320,384},{3... | collective-permute-start | bytes 1572872 | tf_op jit(solution)/shard_map/ppermute | solution.py:18
  8.4 12.2 %collective-permute-start.1 = (bf16[256,1024]{1,0:T(8,128)(2,1)S(1)}, bf16[256,1024]{1,0:T(8,128)(2,1)S(1)}, u32[]{:S(2)}, u32[]{:S(2)}) collective-permute-start(bf16[256,1024]{1,0:T(8,128)(2,1)S(1)} %slice.78), channel_id=1, source_target_pairs={{64,0},{128,64},{192,128},{256,192},{320,256},{384,320},{448,384},... | collective-permute-start | bytes 1572872 | tf_op jit(solution)/shard_map/ppermute | solution.py:18
  22.4 1.0 convolution_convert_fusion.4.ga_ref
  23.4 7.2 %collective-permute-done.kp_ref.vp_ref = bf16[256,1024]{1,0:T(8,128)(2,1)S(1)} collective-permute-done((bf16[256,1024]{1,0:T(8,128)(2,1)S(1)}, bf16[256,1024]{1,0:T(8,128)(2,1)S(1)}, u32[]{:S(2)}, u32[]{:S(2)}) %collective-permute-start) | collective-permute-done | bytes 524320 | tf_op jit(solution)/shard_map/ppermute | solution.py:18
  30.6 1.2 collective-permute-done.1.kn_ref.vn_ref
  32.6 9.3 %shard_map.110 = (bf16[256,512]{1,0:T(8,128)(2,1)}, bf16[256,512]{1,0:T(8,128)(2,1)}, f32[256,512]{1,0:T(8,128)}, f32[256,512]{1,0:T(8,128)}, bf16[256,512]{1,0:...) custom-call(f32[8,768]{1,0:T(8,128)} %scatter.6.mask_ref, ...), custom_call_target="tpu_custom_call" | custom-call | flops 1207959552 | bytes 4718592 | tf_op jit(solution)/shard_map/pallas_call | solution.py:83
  41.9 2.0 %pad_maximum_fusion.2 = bf16[256,1024]{1,0:T(8,128)(2,1)} fusion(bf16[256,512]{1,0:T(8,128)(2,1)} %get-tuple-element.42, bf16[256,512]{1,0:T(8,128)(2,1)} %get-tuple-element.41), kind=kLoop, calls=%fused_computation.34 | loop fusion | flops 1048576 | bytes 1048576 | tf_op jit(solution)/shard_map/concatenate | solution.py:132
  43.9 5.6 %collective-permute-start.2 = (bf16[256,1024]{1,0:T(8,128)(2,1)}, bf16[256,1024]{1,0:T(8,128)(2,1)}, u32[]{:S(2)}, u32[]{:S(2)}) collective-permute-start(bf16[256,1024]{1,0:T(8,128)(2,1)} %pad_maximum_fusion.2), channel_id=1, source_target_pairs={{64,0},{128,64},{192,128},{256,192},{320,256},{384,320},{448,384},... | collective-permute-start | bytes 1572872 | tf_op jit(solution)/shard_map/ppermute | solution.py:18
  49.5 1.9 %pad_maximum_fusion.3 = bf16[256,1024]{1,0:T(8,128)(2,1)} fusion(bf16[256,512]{1,0:T(8,128)(2,1)} %get-tuple-element.44, bf16[256,512]{1,0:T(8,128)(2,1)} %get-tuple-element.43), kind=kLoop, calls=%fused_computation.35 | loop fusion | flops 1048576 | bytes 1048576 | tf_op jit(solution)/shard_map/concatenate | solution.py:132
  51.4 1.9 %collective-permute-start.3 = (bf16[256,1024]{1,0:T(8,128)(2,1)}, bf16[256,1024]{1,0:T(8,128)(2,1)}, u32[]{:S(2)}, u32[]{:S(2)}) collective-permute-start(bf16[256,1024]{1,0:T(8,128)(2,1)} %pad_maximum_fusion.3), channel_id=1, source_target_pairs={{704,0},{0,64},{64,128},{128,192},{192,256},{256,320},{320,384},{3... | collective-permute-start | bytes 1572872 | tf_op jit(solution)/shard_map/ppermute | solution.py:18
  54.8 4.7 %all_to_all.25 = bf16[2,256,1024]{2,1,0:T(8,128)(2,1)S(1)} all-to-all(bf16[2,256,1024]{2,1,0:T(8,128)(2,1)S(1)} %bitcast.53), channel_id=1, replica_groups=mesh['node'=12,'y'=8,'x'=4,'core'=2] {'core'}, dimensions={0} | all-to-all | bytes 2097152 | tf_op jit(solution)/shard_map/all_to_all | solution.py:163
  60.1 7.2 %collective-permute-done.3 = bf16[256,1024]{1,0:T(8,128)(2,1)} collective-permute-done((bf16[256,1024]{1,0:T(8,128)(2,1)}, bf16[256,1024]{1,0:T(8,128)(2,1)}, u32[]{:S(2)}, u32[]{:S(2)}) %collective-permute-start.3) | collective-permute-done | bytes 524320 | tf_op jit(solution)/shard_map/ppermute | solution.py:18
  67.3 1.6 %fusion.5 = bf16[256,1024]{1,0:T(8,128)(2,1)S(1)} fusion(f32[256,512]{1,0:T(8,128)} %get-tuple-element.40, f32[256,512]{1,0:T(8,128)S(1)} %copy-done.12, bf16[256,1024]{1,0:T(8,128)(2,1)} %collective-permute-done.3, bf16[256,1024]{1,0:T(8,128)(2,1)} %collective-permute-done.2), kind=kLoop, calls=%fused_computation.15 | loop fusion | flops 1572864 | bytes 2621440 | tf_op jit(solution)/shard_map/convert_element_type | solution.py:135
  70.0 1.2 fusion.18
  72.2 4.7 %all_to_all.26 = bf16[2,256,1152]{2,1,0:T(8,128)(2,1)S(1)} all-to-all(bf16[2,256,1152]{2,1,0:T(8,128)(2,1)S(1)} %bitcast.50), channel_id=1, replica_groups=mesh['node'=12,'y'=8,'x'=4,'core'=2] {'core'}, dimensions={0} | all-to-all | bytes 2359296 | tf_op jit(solution)/shard_map/all_to_all | solution.py:163
  77.3 18.7 %all_to_all.27 = bf16[4,64,2176]{2,1,0:T(8,128)(2,1)S(1)} all-to-all(bf16[4,64,2176]{2,1,0:T(8,128)(2,1)S(1)} %bitcast.51), channel_id=1, replica_groups=mesh['node'=12,'y'=8,'x'=4,'core'=2] {'x'}, dimensions={0} | all-to-all | bytes 2228224 | tf_op jit(solution)/shard_map/all_to_all | solution.py:163
  96.0 0.9 reduce_sum.80
  96.9 7.2 %all-to-all-start.3 = ((bf16[8,8,2176]{2,1,0:T(8,128)(2,1)}), bf16[8,8,2176]{2,1,0:T(8,128)(2,1)S(1)}, u32[]{:S(2)}, u32[]{:S(2)}) async-start(bf16[8,8,2176]{2,1,0:T(8,128)(2,1)} %bitcast.12), calls=%async_computation.3 | async-start | bytes 557056 | tf_op jit(solution)/shard_map/all_to_all | solution.py:163
  104.2 1.0 fusion.3
  105.2 10.4 %all-to-all-done.3 = bf16[8,8,2176]{2,1,0:T(8,128)(2,1)S(1)} async-done(((bf16[8,8,2176]{2,1,0:T(8,128)(2,1)}), bf16[8,8,2176]{2,1,0:T(8,128)(2,1)S(1)}, u32[]{:S(2)}, u32[]{:S(2)}) %all-to-all-start.3) | async-done | bytes 278560 | tf_op jit(solution)/shard_map/all_to_all | solution.py:163
  116.3 3.9 %all-to-all-start.4 = ((bf16[12,8,768]{2,1,0:T(8,128)(2,1)}), bf16[12,8,768]{2,1,0:T(8,128)(2,1)S(1)}, u32[]{:S(2)}, u32[]{:S(2)}) async-start(bf16[12,8,768]{2,1,0:T(8,128)(2,1)} %pad_maximum_fusion.4), calls=%async_computation.4 | async-start | bytes 294912 | tf_op jit(solution)/shard_map/all_to_all | solution.py:182
  121.2 10.7 %all-to-all-done.4 = bf16[12,8,768]{2,1,0:T(8,128)(2,1)S(1)} async-done(((bf16[12,8,768]{2,1,0:T(8,128)(2,1)}), bf16[12,8,768]{2,1,0:T(8,128)(2,1)S(1)}, u32[]{:S(2)}, u32[]{:S(2)}) %all-to-all-start.4) | async-done | bytes 147488 | tf_op jit(solution)/shard_map/all_to_all | solution.py:182
  (73 shorter events, 10.6 us)
Async XLA Ops:
  0.6 21.8 %copy-start = (bf16[512,512]{1,0:T(8,128)(2,1)S(1)}, bf16[512,512]{1,0:T(8,128)(2,1)}, u32[]{:S(2)}) copy-start(bf16[512,512]{1,0:T(8,128)(2,1)} %param.14) | copy-start | bytes 1572868
  1.8 18.8 %copy-start.14 = (s32[24,5]{0,1:T(8,128)S(1)}, s32[24,5]{0,1:T(8,128)}, u32[]{:S(2)}) copy-start(s32[24,5]{0,1:T(8,128)} %param.16) | copy-start | bytes 1444
  1.8 19.0 %copy-start.15 = (s32[24]{0:T(128)S(1)}, s32[24]{0:T(128)}, u32[]{:S(2)}) copy-start(s32[24]{0:T(128)} %param.17) | copy-start | bytes 292
  1.8 20.6 %copy-start.4 = (bf16[1,256,512]{2,1,0:T(8,128)(2,1)S(1)}, bf16[1,256,512]{2,1,0:T(8,128)(2,1)}, u32[]{:S(2)}) copy-start(bf16[1,256,512]{2,1,0:T(8,128)(2,1)} %param.12) | copy-start | bytes 786436
  4.0 27.8 %copy-start.1 = (bf16[256,1536]{1,0:T(8,128)(2,1)}, bf16[256,1536]{1,0:T(8,128)(2,1)S(1)}, u32[]{:S(2)}) copy-start(bf16[256,1536]{1,0:T(8,128)(2,1)S(1)} %convolution_convert_fusion.q_ref.k_ref.v_ref) | copy-start | bytes 2359300
  4.1 26.5 %collective-permute-start = (bf16[256,1024]{1,0:T(8,128)(2,1)S(1)}, bf16[256,1024]{1,0:T(8,128)(2,1)S(1)}, u32[]{:S(2)}, u32[]{:S(2)}) collective-permute-start(bf16[256,1024]{1,0:T(8,128)(2,1)S(1)} %slice.78), channel_id=1, source_target_pairs={{704,0},{0,64},{64,128},{128,192},{192,256},{256,320},{320,384},{3... | collective-permute-start | bytes 1572872 | tf_op jit(solution)/shard_map/ppermute | solution.py:18
  8.4 23.4 %collective-permute-start.1 = (bf16[256,1024]{1,0:T(8,128)(2,1)S(1)}, bf16[256,1024]{1,0:T(8,128)(2,1)S(1)}, u32[]{:S(2)}, u32[]{:S(2)}) collective-permute-start(bf16[256,1024]{1,0:T(8,128)(2,1)S(1)} %slice.78), channel_id=1, source_target_pairs={{64,0},{128,64},{192,128},{256,192},{320,256},{384,320},{448,384},... | collective-permute-start | bytes 1572872 | tf_op jit(solution)/shard_map/ppermute | solution.py:18
  30.6 1.2 copy-start.5
  31.8 0.8 copy-start.6
  41.9 11.4 %copy-start.8 = (bf16[256,512]{1,0:T(8,128)(2,1)S(1)}, bf16[256,512]{1,0:T(8,128)(2,1)}, u32[]{:S(2)}) copy-start(bf16[256,512]{1,0:T(8,128)(2,1)} %get-tuple-element.37) | copy-start | bytes 786436
  41.9 11.8 %copy-start.2 = (bf16[1,256,512]{2,1,0:T(8,128)(2,1)S(1)}, bf16[1,256,512]{2,1,0:T(8,128)(2,1)}, u32[]{:S(2)}) copy-start(bf16[1,256,512]{2,1,0:T(8,128)(2,1)} %param.11) | copy-start | bytes 786436
  41.9 11.8 %copy-start.10 = (bf16[256,512]{1,0:T(8,128)(2,1)S(1)}, bf16[256,512]{1,0:T(8,128)(2,1)}, u32[]{:S(2)}) copy-start(bf16[256,512]{1,0:T(8,128)(2,1)} %get-tuple-element.38) | copy-start | bytes 786436
  41.9 11.8 %copy-start.13 = (f32[512]{0:T(512)S(1)}, f32[512]{0:T(512)}, u32[]{:S(2)}) copy-start(f32[512]{0:T(512)} %param.15) | copy-start | bytes 6148
  43.9 16.2 %collective-permute-start.2 = (bf16[256,1024]{1,0:T(8,128)(2,1)}, bf16[256,1024]{1,0:T(8,128)(2,1)}, u32[]{:S(2)}, u32[]{:S(2)}) collective-permute-start(bf16[256,1024]{1,0:T(8,128)(2,1)} %pad_maximum_fusion.2), channel_id=1, source_target_pairs={{64,0},{128,64},{192,128},{256,192},{320,256},{384,320},{448,384},... | collective-permute-start | bytes 1572872 | tf_op jit(solution)/shard_map/ppermute | solution.py:18
  51.4 15.9 %collective-permute-start.3 = (bf16[256,1024]{1,0:T(8,128)(2,1)}, bf16[256,1024]{1,0:T(8,128)(2,1)}, u32[]{:S(2)}, u32[]{:S(2)}) collective-permute-start(bf16[256,1024]{1,0:T(8,128)(2,1)} %pad_maximum_fusion.3), channel_id=1, source_target_pairs={{704,0},{0,64},{64,128},{128,192},{192,256},{256,320},{320,384},{3... | collective-permute-start | bytes 1572872 | tf_op jit(solution)/shard_map/ppermute | solution.py:18
  54.8 12.5 %copy-start.12 = (f32[256,512]{1,0:T(8,128)S(1)}, f32[256,512]{1,0:T(8,128)}, u32[]{:S(2)}) copy-start(f32[256,512]{1,0:T(8,128)} %get-tuple-element.39) | copy-start | bytes 1572868
  59.8 9.1 %copy-start.3 = (bf16[512,1536]{1,0:T(8,128)(2,1)S(1)}, bf16[512,1536]{1,0:T(8,128)(2,1)}, u32[]{:S(2)}) copy-start(bf16[512,1536]{1,0:T(8,128)(2,1)} %param.13) | copy-start | bytes 4718596
  68.9 1.1 copy-start.11
  77.2 26.9 %copy-start.9 = (bf16[256,512]{1,0:T(8,128)(2,1)S(1)}, bf16[256,512]{1,0:T(8,128)(2,1)}, u32[]{:S(2)}) copy-start(bf16[256,512]{1,0:T(8,128)(2,1)} %get-tuple-element.37) | copy-start | bytes 786436
  96.9 23.4 %copy-start.7 = (f32[256,512]{1,0:T(8,128)S(1)}, f32[256,512]{1,0:T(8,128)}, u32[]{:S(2)}) copy-start(f32[256,512]{1,0:T(8,128)} %get-tuple-element.49) | copy-start | bytes 1572868
  96.9 18.6 %all-to-all-start.3 = ((bf16[8,8,2176]{2,1,0:T(8,128)(2,1)}), bf16[8,8,2176]{2,1,0:T(8,128)(2,1)S(1)}, u32[]{:S(2)}, u32[]{:S(2)}) async-start(bf16[8,8,2176]{2,1,0:T(8,128)(2,1)} %bitcast.12), calls=%async_computation.3 | async-start | bytes 557056 | tf_op jit(solution)/shard_map/all_to_all | solution.py:163
  116.3 15.6 %all-to-all-start.4 = ((bf16[12,8,768]{2,1,0:T(8,128)(2,1)}), bf16[12,8,768]{2,1,0:T(8,128)(2,1)S(1)}, u32[]{:S(2)}, u32[]{:S(2)}) async-start(bf16[12,8,768]{2,1,0:T(8,128)(2,1)} %pad_maximum_fusion.4), calls=%async_computation.4 | async-start | bytes 294912 | tf_op jit(solution)/shard_map/all_to_all | solution.py:182

commit v10 on v9

--- a/solution.py
+++ b/solution.py
@@ -31,7 +31,7 @@
 
 
 def attention_kernel(mask_ref, q_ref, k_ref, v_ref, kp_ref, vp_ref, kn_ref, vn_ref, ga_ref,
-                     att_ref, gq_ref, gk_ref, gv_ref, gkp_ref, gvp_ref, gkn_ref, gvn_ref):
+                     att_ref, gq_ref, own_ref, low_ref, high_ref):
     head_dim = q_ref.shape[1]
     block_rows = k_ref.shape[0]
     score_scale = head_dim ** (-0.5)
@@ -59,12 +59,10 @@
         gq_ref[rows, :] = jnp.dot(grad_scores, keys, preferred_element_type=jnp.float32).astype(gq_ref.dtype)
         grad_keys = grad_keys + lax.dot_general(grad_scores, queries, tn, preferred_element_type=jnp.float32)
         grad_values = grad_values + lax.dot_general(rounded, grads, tn, preferred_element_type=jnp.float32)
-    gkp_ref[...] = grad_keys[:block_rows].astype(gkp_ref.dtype)
-    gvp_ref[...] = grad_values[:block_rows].astype(gvp_ref.dtype)
-    gk_ref[...] = grad_keys[block_rows : 2 * block_rows]
-    gv_ref[...] = grad_values[block_rows : 2 * block_rows]
-    gkn_ref[...] = grad_keys[2 * block_rows :].astype(gkn_ref.dtype)
-    gvn_ref[...] = grad_values[2 * block_rows :].astype(gvn_ref.dtype)
+    for side, side_ref in enumerate((low_ref, own_ref, high_ref)):
+        part = slice(side * block_rows, (side + 1) * block_rows)
+        side_ref[0] = grad_keys[part].astype(side_ref.dtype)
+        side_ref[1] = grad_values[part].astype(side_ref.dtype)
 
 
 def fused_attention(keep_rows, projected, low, high, grad_attended, heads):
@@ -79,14 +77,20 @@
     cost = pl.CostEstimate(flops=12 * rows * span * width, transcendentals=rows * span * heads,
                            bytes_accessed=2 * (3 * rows * width + 2 * span * width) + 4 * (2 * rows * width) + 2 * (5 * rows * width))
     bf16_out = jax.ShapeDtypeStruct((rows, width), jnp.bfloat16)
-    f32_out = jax.ShapeDtypeStruct((rows, width), jnp.float32)
+    pair_spec = pl.BlockSpec((2, rows, head_dim), lambda h: (0, 0, h))
     return pl.pallas_call(
         attention_kernel,
         grid=(heads,),
         in_specs=[m_spec, column(0), column(heads), column(2 * heads), column(0), column(heads),
                   column(0), column(heads), column(0)],
-        out_specs=[column(0)] * 8,
-        out_shape=[bf16_out, bf16_out, f32_out, f32_out, bf16_out, bf16_out, bf16_out, bf16_out],
+        out_specs=[column(0), column(0), pair_spec, pair_spec, pair_spec],
+        out_shape=[
+            bf16_out,
+            bf16_out,
+            jax.ShapeDtypeStruct((2, rows, width), jnp.float32),
+            jax.ShapeDtypeStruct((2, rows, width), jnp.bfloat16),
+            jax.ShapeDtypeStruct((2, rows, width), jnp.bfloat16),
+        ],
         cost_estimate=cost,
     )(keep_rows, projected, projected, projected, low, low, high, high, grad_attended)
 
@@ -116,8 +120,8 @@
     ).astype(jnp.bfloat16)
     keep_rows = jnp.zeros((8, 3 * row_count), jnp.float32)
     keep_rows = keep_rows.at[:tile_count].set(jnp.repeat(allowed, TILE, axis=1).astype(jnp.float32))
-    (attended, grad_q, grad_keys, grad_values, low_keys, low_values, high_keys, high_values) = (
-        fused_attention(keep_rows, projected, low, high, grad_attended, HEADS)
+    attended, grad_q, grad_own, grad_low, grad_high = fused_attention(
+        keep_rows, projected, low, high, grad_attended, HEADS
     )
     outputs = (widened + jnp.dot(attended, w_out, preferred_element_type=jnp.float32)).astype(
         jnp.bfloat16
@@ -127,11 +131,11 @@
     )
     term_q = lax.dot_general(normed, grad_q, contract_rows, preferred_element_type=jnp.float32)
     early = chip_sum(jnp.concatenate([term_q, term_out], axis=1))
-    grad_keyvals = jnp.concatenate([grad_keys, grad_values], axis=1)
-    for offset, side_keys, side_values in ((-1, low_keys, low_values), (1, high_keys, high_values)):
-        side_part = jnp.concatenate([side_keys, side_values], axis=1)
+    grad_pair = grad_own
+    for offset, side_part in ((-1, grad_low), (1, grad_high)):
         arrived = passed_along(side_part, "node", offset)
-        grad_keyvals = grad_keyvals + arrived.astype(jnp.float32)
+        grad_pair = grad_pair + arrived.astype(jnp.float32)
+    grad_keyvals = jnp.concatenate([grad_pair[0], grad_pair[1]], axis=1)
     grad_kv = grad_keyvals.astype(jnp.bfloat16)
     term_kv = lax.dot_general(normed, grad_kv, contract_rows, preferred_element_type=jnp.float32)
     grad_normed = lax.dot_general(

time: 135 us -> 133 us (0.985)
  other arithmetic: 11.5 us -> 7.76 us
  matrix products: 7.17 us -> 9.03 us
  waiting for transfers between devices: 36.9 us -> 35.2 us
    concatenate x2 -> x0, other arithmetic: 3.86 us -> none  [device_step(): side_part = jnp.concatenate([side_keys, side_values], axis=1)]
    another operation x3 -> x4, other arithmetic: 1.29 us -> 3.02 us
    ppermute x4, waiting for transfers between devices: 15.9 us -> 14.1 us  [passed_along(): return lax.ppermute(block, axis, route)]
    convert_element_type x1 -> x0, other arithmetic: 1.6 us -> none  [device_step(): grad_kv = grad_keyvals.astype(jnp.bfloat16)]
where the time goes in v10:
time: 133 us; the launch traced here: 131 us
  starting transfers between devices  35.2 us (26%)
  waiting for transfers between devices  35.2 us (26%)
  blocking collectives  28 us (21%)
  Pallas kernels  9.33 us (7%)
  matrix products  9.03 us (7%)
  other arithmetic  7.76 us (6%)
  local copies, waits for them, and re-layouts  5.81 us (4%)
    all_to_all x3, blocking collectives, exchange_sum(): lax.all_to_all(pieces.astype(jnp.bfloat16), axis, 0, 0, tiled=False)  28 us
    ppermute x4, starting transfers between devices, passed_along(): return lax.ppermute(block, axis, route)  24 us
    ppermute x4, waiting for transfers between devices, passed_along(): return lax.ppermute(block, axis, route)  14.1 us
    all_to_all x1, waiting for transfers between devices, node_sum(): lax.all_to_all(mixed.astype(jnp.bfloat16), 'node', 0, 0, tiled=False)  10.7 us
    all_to_all x1, waiting for transfers between devices, exchange_sum(): lax.all_to_all(pieces.astype(jnp.bfloat16), axis, 0, 0, tiled=False)  10.4 us
    pallas_call x1, Pallas kernels, fused_attention(): pl.pallas_call(attention_kernel, grid=(heads,), in_specs=[m_spec, column(...  9.33 us
    all_to_all x1, starting transfers between devices, exchange_sum(): lax.all_to_all(pieces.astype(jnp.bfloat16), axis, 0, 0, tiled=False)  7.23 us
    all_to_all x1, starting transfers between devices, node_sum(): lax.all_to_all(mixed.astype(jnp.bfloat16), 'node', 0, 0, tiled=False)  3.95 us
  transfers between devices with their start and end apart: 6, of which 6 were waited for; matrix products, arithmetic and copies ran while one was open for 6% of the time, Pallas kernels for 0%

profile of v10, /device:TPU:6, one launch (start us, length us, event | category | flops | bytes accessed | tf_op | source)
XLA Modules:
  0.0 131.3 jit_solution(3862903936977908877)
XLA Ops:
  0.6 1.1 fusion.17
  1.8 2.2 %convolution_convert_fusion.q_ref.k_ref.v_ref = bf16[256,1536]{1,0:T(8,128)(2,1)S(1)} fusion(bf16[512,1536]{1,0:T(8,128)(2,1)} %param.13, bf16[1,256,512]{2,1,0:T(8,128)(2,1)} %param.11, f32[512]{0:T(512)} %param.15, f32[256]{0:T(256)S(1)} %add_rsqrt_fusion), kind=kOutput, calls=%fused_computation | convolution fusion | flops 403570688 | bytes 2624512 | tf_op jit(solution)/shard_map/dot_general | solution.py:112
  4.1 4.3 %collective-permute-start = (bf16[256,1024]{1,0:T(8,128)(2,1)S(1)}, bf16[256,1024]{1,0:T(8,128)(2,1)S(1)}, u32[]{:S(2)}, u32[]{:S(2)}) collective-permute-start(bf16[256,1024]{1,0:T(8,128)(2,1)S(1)} %slice.88), channel_id=1, source_target_pairs={{704,0},{0,64},{64,128},{128,192},{192,256},{256,320},{320,384},{3... | collective-permute-start | bytes 1572872 | tf_op jit(solution)/shard_map/ppermute | solution.py:18
  8.4 12.2 %collective-permute-start.1 = (bf16[256,1024]{1,0:T(8,128)(2,1)S(1)}, bf16[256,1024]{1,0:T(8,128)(2,1)S(1)}, u32[]{:S(2)}, u32[]{:S(2)}) collective-permute-start(bf16[256,1024]{1,0:T(8,128)(2,1)S(1)} %slice.88), channel_id=1, source_target_pairs={{64,0},{128,64},{192,128},{256,192},{320,256},{384,320},{448,384},... | collective-permute-start | bytes 1572872 | tf_op jit(solution)/shard_map/ppermute | solution.py:18
  22.4 1.0 convolution_convert_fusion.4.ga_ref
  23.4 7.2 %collective-permute-done.kp_ref.vp_ref = bf16[256,1024]{1,0:T(8,128)(2,1)S(1)} collective-permute-done((bf16[256,1024]{1,0:T(8,128)(2,1)S(1)}, bf16[256,1024]{1,0:T(8,128)(2,1)S(1)}, u32[]{:S(2)}, u32[]{:S(2)}) %collective-permute-start) | collective-permute-done | bytes 524320 | tf_op jit(solution)/shard_map/ppermute | solution.py:18
  30.6 1.2 collective-permute-done.1.kn_ref.vn_ref
  32.6 9.3 %shard_map.110 = (bf16[256,512]{1,0:T(8,128)(2,1)}, bf16[256,512]{1,0:T(8,128)(2,1)}, f32[2,256,512]{2,1,0:T(8,128)}, bf16[2,256,512]{2,1,0:T(8,128)(2,1)}, bf16[2,256,512]{2,1,0:T(8,128)(2,1)}) custom-call(f32[8,768]{1,0:T(8,128)} %scatter.6.mask_ref, bf16[256,1536]{1,0:T(8,128)(2,1)} %copy-done.1, bf16[256,1536]{1,0:T(8,128)(2,1)} %copy-done.1, ...), custom_call_target="tpu_custom_call" | custom-call | flops 1207959552 | bytes 4718592 | tf_op jit(solution)/shard_map/pallas_call | solution.py:81
  41.9 5.6 %collective-permute-start.2 = (bf16[2,256,512]{2,1,0:T(8,128)(2,1)}, bf16[2,256,512]{2,1,0:T(8,128)(2,1)}, u32[]{:S(2)}, u32[]{:S(2)}) collective-permute-start(bf16[2,256,512]{2,1,0:T(8,128)(2,1)} %get-tuple-element.37), channel_id=1, source_target_pairs={{64,0},{128,64},{192,128},{256,192},{320,256},{384,320},{448,384},... | collective-permute-start | bytes 1572872 | tf_op jit(solution)/shard_map/ppermute | solution.py:18
  47.5 1.9 %collective-permute-start.3 = (bf16[2,256,512]{2,1,0:T(8,128)(2,1)}, bf16[2,256,512]{2,1,0:T(8,128)(2,1)}, u32[]{:S(2)}, u32[]{:S(2)}) collective-permute-start(bf16[2,256,512]{2,1,0:T(8,128)(2,1)} %get-tuple-element.38), channel_id=1, source_target_pairs={{704,0},{0,64},{64,128},{128,192},{192,256},{256,320},{320,384},{3... | collective-permute-start | bytes 1572872 | tf_op jit(solution)/shard_map/ppermute | solution.py:18
  49.4 1.3 convolution_convert_fusion.2
  50.8 1.3 %convolution_convert_fusion.3 = bf16[512,512]{0,1:T(8,128)(2,1)S(1)} fusion(bf16[256,512]{1,0:T(8,128)(2,1)} %get-tuple-element.35, bf16[1,256,512]{2,1,0:T(8,128)(2,1)S(1)} %copy-done.2, f32[512]{0:T(512)S(1)} %copy-done.10, f32[256]{0:T(256)S(1)} %add_rsqrt_fusion), kind=kOutput, calls=%fused_computation.5 | convolution fusion | flops 135004160 | bytes 1051648 | tf_op jit(solution)/shard_map/dot_general | solution.py:132
  52.8 4.6 %all_to_all.25 = bf16[2,256,1024]{2,1,0:T(8,128)(2,1)S(1)} all-to-all(bf16[2,256,1024]{2,1,0:T(8,128)(2,1)S(1)} %bitcast.55), channel_id=1, replica_groups=mesh['node'=12,'y'=8,'x'=4,'core'=2] {'core'}, dimensions={0} | all-to-all | bytes 2097152 | tf_op jit(solution)/shard_map/all_to_all | solution.py:167
  58.1 5.3 %collective-permute-done.3 = bf16[2,256,512]{2,1,0:T(8,128)(2,1)} collective-permute-done((bf16[2,256,512]{2,1,0:T(8,128)(2,1)}, bf16[2,256,512]{2,1,0:T(8,128)(2,1)}, u32[]{:S(2)}, u32[]{:S(2)}) %collective-permute-start.3) | collective-permute-done | bytes 524320 | tf_op jit(solution)/shard_map/ppermute | solution.py:18
  63.5 1.7 %add_convert_fusion = bf16[2,256,512]{2,1,0:T(8,128)(2,1)S(1)} fusion(bf16[2,256,512]{2,1,0:T(8,128)(2,1)} %collective-permute-done.3, f32[2,256,512]{2,1,0:T(8,128)} %get-tuple-element.36, bf16[2,256,512]{2,1,0:T(8,128)(2,1)} %collective-permute-done.2), kind=kLoop, calls=%fused_computation.16 | loop fusion | flops 1310720 | bytes 2621440 | tf_op jit(solution)/shard_map/convert.24
  67.6 1.2 fusion.16
  69.8 4.7 %all_to_all.26 = bf16[2,256,1152]{2,1,0:T(8,128)(2,1)S(1)} all-to-all(bf16[2,256,1152]{2,1,0:T(8,128)(2,1)S(1)} %bitcast.52), channel_id=1, replica_groups=mesh['node'=12,'y'=8,'x'=4,'core'=2] {'core'}, dimensions={0} | all-to-all | bytes 2359296 | tf_op jit(solution)/shard_map/all_to_all | solution.py:167
  74.8 18.7 %all_to_all.27 = bf16[4,64,2176]{2,1,0:T(8,128)(2,1)S(1)} all-to-all(bf16[4,64,2176]{2,1,0:T(8,128)(2,1)S(1)} %bitcast.53), channel_id=1, replica_groups=mesh['node'=12,'y'=8,'x'=4,'core'=2] {'x'}, dimensions={0} | all-to-all | bytes 2228224 | tf_op jit(solution)/shard_map/all_to_all | solution.py:167
  93.5 0.9 reduce_sum.80
  94.5 7.2 %all-to-all-start.3 = ((bf16[8,8,2176]{2,1,0:T(8,128)(2,1)}), bf16[8,8,2176]{2,1,0:T(8,128)(2,1)S(1)}, u32[]{:S(2)}, u32[]{:S(2)}) async-start(bf16[8,8,2176]{2,1,0:T(8,128)(2,1)} %bitcast.14), calls=%async_computation.3 | async-start | bytes 557056 | tf_op jit(solution)/shard_map/all_to_all | solution.py:167
  101.7 1.0 fusion.3
  102.7 10.4 %all-to-all-done.3 = bf16[8,8,2176]{2,1,0:T(8,128)(2,1)S(1)} async-done(((bf16[8,8,2176]{2,1,0:T(8,128)(2,1)}), bf16[8,8,2176]{2,1,0:T(8,128)(2,1)S(1)}, u32[]{:S(2)}, u32[]{:S(2)}) %all-to-all-start.3) | async-done | bytes 278560 | tf_op jit(solution)/shard_map/all_to_all | solution.py:167
  113.9 3.9 %all-to-all-start.4 = ((bf16[12,8,768]{2,1,0:T(8,128)(2,1)}), bf16[12,8,768]{2,1,0:T(8,128)(2,1)S(1)}, u32[]{:S(2)}, u32[]{:S(2)}) async-start(bf16[12,8,768]{2,1,0:T(8,128)(2,1)} %pad_maximum_fusion.5), calls=%async_computation.4 | async-start | bytes 294912 | tf_op jit(solution)/shard_map/all_to_all | solution.py:186
  118.8 10.7 %all-to-all-done.4 = bf16[12,8,768]{2,1,0:T(8,128)(2,1)S(1)} async-done(((bf16[12,8,768]{2,1,0:T(8,128)(2,1)}), bf16[12,8,768]{2,1,0:T(8,128)(2,1)S(1)}, u32[]{:S(2)}, u32[]{:S(2)}) %all-to-all-start.4) | async-done | bytes 147488 | tf_op jit(solution)/shard_map/all_to_all | solution.py:186
  (66 shorter events, 11.3 us)
Async XLA Ops:
  0.6 21.8 %copy-start = (bf16[512,512]{1,0:T(8,128)(2,1)S(1)}, bf16[512,512]{1,0:T(8,128)(2,1)}, u32[]{:S(2)}) copy-start(bf16[512,512]{1,0:T(8,128)(2,1)} %param.14) | copy-start | bytes 1572868
  1.8 18.8 %copy-start.11 = (s32[24,5]{0,1:T(8,128)S(1)}, s32[24,5]{0,1:T(8,128)}, u32[]{:S(2)}) copy-start(s32[24,5]{0,1:T(8,128)} %param.16) | copy-start | bytes 1444
  1.8 19.0 %copy-start.12 = (s32[24]{0:T(128)S(1)}, s32[24]{0:T(128)}, u32[]{:S(2)}) copy-start(s32[24]{0:T(128)} %param.17) | copy-start | bytes 292
  1.8 20.6 %copy-start.4 = (bf16[1,256,512]{2,1,0:T(8,128)(2,1)S(1)}, bf16[1,256,512]{2,1,0:T(8,128)(2,1)}, u32[]{:S(2)}) copy-start(bf16[1,256,512]{2,1,0:T(8,128)(2,1)} %param.12) | copy-start | bytes 786436
  4.0 27.8 %copy-start.1 = (bf16[256,1536]{1,0:T(8,128)(2,1)}, bf16[256,1536]{1,0:T(8,128)(2,1)S(1)}, u32[]{:S(2)}) copy-start(bf16[256,1536]{1,0:T(8,128)(2,1)S(1)} %convolution_convert_fusion.q_ref.k_ref.v_ref) | copy-start | bytes 2359300
  4.1 26.5 %collective-permute-start = (bf16[256,1024]{1,0:T(8,128)(2,1)S(1)}, bf16[256,1024]{1,0:T(8,128)(2,1)S(1)}, u32[]{:S(2)}, u32[]{:S(2)}) collective-permute-start(bf16[256,1024]{1,0:T(8,128)(2,1)S(1)} %slice.88), channel_id=1, source_target_pairs={{704,0},{0,64},{64,128},{128,192},{192,256},{256,320},{320,384},{3... | collective-permute-start | bytes 1572872 | tf_op jit(solution)/shard_map/ppermute | solution.py:18
  8.4 23.4 %collective-permute-start.1 = (bf16[256,1024]{1,0:T(8,128)(2,1)S(1)}, bf16[256,1024]{1,0:T(8,128)(2,1)S(1)}, u32[]{:S(2)}, u32[]{:S(2)}) collective-permute-start(bf16[256,1024]{1,0:T(8,128)(2,1)S(1)} %slice.88), channel_id=1, source_target_pairs={{64,0},{128,64},{192,128},{256,192},{320,256},{384,320},{448,384},... | collective-permute-start | bytes 1572872 | tf_op jit(solution)/shard_map/ppermute | solution.py:18
  23.4 27.3 %copy-start.2 = (bf16[1,256,512]{2,1,0:T(8,128)(2,1)S(1)}, bf16[1,256,512]{2,1,0:T(8,128)(2,1)}, u32[]{:S(2)}) copy-start(bf16[1,256,512]{2,1,0:T(8,128)(2,1)} %param.11) | copy-start | bytes 786436
  23.4 27.3 %copy-start.10 = (f32[512]{0:T(512)S(1)}, f32[512]{0:T(512)}, u32[]{:S(2)}) copy-start(f32[512]{0:T(512)} %param.15) | copy-start | bytes 6148
  30.6 1.2 copy-start.5
  31.8 0.8 copy-start.6
  41.9 16.2 %collective-permute-start.2 = (bf16[2,256,512]{2,1,0:T(8,128)(2,1)}, bf16[2,256,512]{2,1,0:T(8,128)(2,1)}, u32[]{:S(2)}, u32[]{:S(2)}) collective-permute-start(bf16[2,256,512]{2,1,0:T(8,128)(2,1)} %get-tuple-element.37), channel_id=1, source_target_pairs={{64,0},{128,64},{192,128},{256,192},{320,256},{384,320},{448,384},... | collective-permute-start | bytes 1572872 | tf_op jit(solution)/shard_map/ppermute | solution.py:18
  47.5 15.9 %collective-permute-start.3 = (bf16[2,256,512]{2,1,0:T(8,128)(2,1)}, bf16[2,256,512]{2,1,0:T(8,128)(2,1)}, u32[]{:S(2)}, u32[]{:S(2)}) collective-permute-start(bf16[2,256,512]{2,1,0:T(8,128)(2,1)} %get-tuple-element.38), channel_id=1, source_target_pairs={{704,0},{0,64},{64,128},{128,192},{192,256},{256,320},{320,384},{3... | collective-permute-start | bytes 1572872 | tf_op jit(solution)/shard_map/ppermute | solution.py:18
  65.2 1.4 %copy-start.3 = (bf16[512,1536]{1,0:T(8,128)(2,1)S(1)}, bf16[512,1536]{1,0:T(8,128)(2,1)}, u32[]{:S(2)}) copy-start(bf16[512,1536]{1,0:T(8,128)(2,1)} %param.13) | copy-start | bytes 4718596
  66.6 0.9 copy-start.9
  74.8 26.9 %copy-start.8 = (bf16[256,512]{1,0:T(8,128)(2,1)S(1)}, bf16[256,512]{1,0:T(8,128)(2,1)}, u32[]{:S(2)}) copy-start(bf16[256,512]{1,0:T(8,128)(2,1)} %get-tuple-element.34) | copy-start | bytes 786436
  94.5 23.4 %copy-start.7 = (f32[256,512]{1,0:T(8,128)S(1)}, f32[256,512]{1,0:T(8,128)}, u32[]{:S(2)}) copy-start(f32[256,512]{1,0:T(8,128)} %get-tuple-element.45) | copy-start | bytes 1572868
  94.5 18.6 %all-to-all-start.3 = ((bf16[8,8,2176]{2,1,0:T(8,128)(2,1)}), bf16[8,8,2176]{2,1,0:T(8,128)(2,1)S(1)}, u32[]{:S(2)}, u32[]{:S(2)}) async-start(bf16[8,8,2176]{2,1,0:T(8,128)(2,1)} %bitcast.14), calls=%async_computation.3 | async-start | bytes 557056 | tf_op jit(solution)/shard_map/all_to_all | solution.py:167
  113.9 15.6 %all-to-all-start.4 = ((bf16[12,8,768]{2,1,0:T(8,128)(2,1)}), bf16[12,8,768]{2,1,0:T(8,128)(2,1)S(1)}, u32[]{:S(2)}, u32[]{:S(2)}) async-start(bf16[12,8,768]{2,1,0:T(8,128)(2,1)} %pad_maximum_fusion.5), calls=%async_computation.4 | async-start | bytes 294912 | tf_op jit(solution)/shard_map/all_to_all | solution.py:186
